TPU v7x, 32 devices: a whole 2x2x4 slice. The times are simulated.
32 devices in a mesh: clips: 2 (over y), patch: 4 (over z), span: 2 (over x), chan: 2 (over core).
Axes of the slice: x: 2, y: 2, z: 4, core: 2. Of those that a mesh axis runs over, the one named last changes fastest.
Arguments:
- latent_tiles: bfloat16 [4, 256, 4, 384], P(('clips', 'span'), 'patch'), parts along dimension 0, may hold values from -12 to 12
- route: int32 [4, 256], P(('clips', 'span')), parts along dimension 0, may hold values from 0 to 255, as said below
- w_query: bfloat16 [384, 384], replicated, may hold values from -0.5 to 4.6
- w_keyval: bfloat16 [384, 768], replicated, may hold values from -0.5 to 4.6
- conv_weight: bfloat16 [3, 3, 3, 384, 384], P(None, None, None, None, 'chan'), may hold values from -0.0625 to 0.0625
Outputs:
- decoded: bfloat16 [8, 8, 64, 384], P(('clips', 'span'), 'patch', None, 'chan'), parts along dimension 0
There are 2 independent parts, one for each index of `clips`. A program takes and returns all parts, laid end to end along the dimension named above; an argument that names none is the same for every part. Nothing has to cross between parts.
Inputs may be any that keep to these rules, and one draw needn't show every extreme that they name: `route`: each span's row is a permutation of 0 .. 255. The 64 tiles of positions j * 64 to (j + 1) * 64 - 1 go to at most 32 per owner, and in every span some such group sends exactly 32 to one owner.
All inputs are finite; a program needn't handle non-finite values.
Results may differ from a plain program's by a relative error of at most 0.0065.
Values may be sent and summed in bfloat16 or wider, within the bound.
No kernel may reach another device: no remote copies, remote signals or barrier semaphores. Data moves between devices by JAX's collectives and lax.ppermute only.
A program may use at most 64 MiB of HBM per device.

v0:
```python
import math

import jax
import jax.numpy as jnp
from jax import lax
from jax.sharding import PartitionSpec as P

C = 384
W = 64
RD = 2
FD = 2


epsilon = 1e-06


def shifted(x, axis, by):
    length = lax.axis_size(axis)
    pairs = [(i, i + by) for i in range(length) if 0 <= i + by < length]
    return lax.ppermute(x, axis, pairs)


def with_halo(cells, sides, width):
    for axis, dim in sides:
        count = lax.axis_size(axis)
        ends = count - 1
        head = lax.slice_in_dim(cells, 0, width, axis=dim)
        tail = lax.slice_in_dim(cells, cells.shape[dim] - width, cells.shape[dim], axis=dim)
        cells = jnp.concatenate(
            [
                lax.ppermute(tail, axis, [(i, (i + 1) % count) for i in range(ends)]),
                cells,
                lax.ppermute(head, axis, [((i + 1) % count, i) for i in range(ends)]),
            ],
            axis=dim,
        )
    return cells


def scaled_rms(values):
    wide = values.astype(jnp.float32)
    return wide / jnp.sqrt(jnp.mean(wide * wide, axis=-1, keepdims=True) + epsilon)


def fold_scores(carry, queries, key_rows, value_rows):
    run_max, run_total, run_acc = carry
    scale = 1.0 / math.sqrt(queries.shape[-1])
    scores = (
        jnp.einsum("fqc,fkc->fqk", queries, key_rows, preferred_element_type=jnp.float32) * scale
    )
    new_max = jnp.max(scores, axis=-1)
    factor = jnp.exp(run_max - new_max)
    powers = jnp.exp(scores - new_max[..., None])
    run_total = run_total * factor + jnp.sum(powers, axis=-1)
    weights = powers.astype(jnp.bfloat16)
    run_acc = run_acc * factor[..., None] + jnp.einsum(
        "fqk,fkc->fqc", weights, value_rows, preferred_element_type=jnp.float32
    )
    return (new_max, run_total, run_acc)


def local(latent_tiles, route, w_query, w_keyval, conv_weight):
    patch_count = lax.axis_size("patch")
    patch_index = lax.axis_index("patch")
    chan_count = lax.axis_size("chan")
    chan_index = lax.axis_index("chan")
    table = route[0]
    frames_core = FD // chan_count
    cell_count = RD * W
    start_carry = (
        jnp.full((frames_core, cell_count), -jnp.inf, jnp.float32),
        jnp.zeros((frames_core, cell_count), jnp.float32),
        jnp.zeros((frames_core, cell_count, C), jnp.float32),
    )
    every_tile = lax.all_gather(latent_tiles, "patch", axis=1, tiled=True)[0]
    tile_total = every_tile.shape[0]
    inverse = (
        jnp.zeros((tile_total,), jnp.int32).at[table].set(jnp.arange(tile_total, dtype=jnp.int32))
    )
    placed = jnp.take(every_tile, inverse, axis=0).reshape(patch_count, FD, RD, W, C)
    whole = placed.transpose(1, 0, 2, 3, 4).reshape(FD, patch_count * RD, W, C)
    features = lax.dynamic_slice_in_dim(whole, patch_index * RD, RD, 1)
    own_frames = lax.dynamic_slice_in_dim(features, chan_index * frames_core, frames_core, 0)
    frame_all = lax.dynamic_slice_in_dim(whole, chan_index * frames_core, frames_core, 0)
    normed_all = scaled_rms(frame_all).astype(jnp.bfloat16)
    normed = lax.dynamic_slice_in_dim(normed_all, patch_index * RD, RD, 1).reshape(
        frames_core, cell_count, C
    )
    queries = jnp.einsum("fnc,cd->fnd", normed, w_query, preferred_element_type=jnp.float32).astype(
        jnp.bfloat16
    )
    keyvals = jnp.einsum(
        "fnc,cd->fnd",
        normed_all.reshape(frames_core, patch_count * cell_count, C),
        w_keyval,
        preferred_element_type=jnp.float32,
    ).astype(jnp.bfloat16)
    run_max, run_total, run_acc = fold_scores(
        start_carry, queries, keyvals[..., :C], keyvals[..., C:]
    )
    attended = run_acc / run_total[..., None]
    mixed_own = (own_frames.astype(jnp.float32) + attended.reshape(frames_core, RD, W, C)).astype(
        jnp.bfloat16
    )
    mixed = lax.all_gather(mixed_own, "chan", axis=0, tiled=True)
    activated = jax.nn.silu(scaled_rms(mixed)).astype(jnp.bfloat16)
    cached = shifted(activated, "span", 1)
    stacked = jnp.concatenate([cached, activated], axis=0)
    padded = with_halo(stacked, (("patch", 1),), 1)
    padded = jnp.pad(padded, ((0, 0), (0, 0), (1, 1), (0, 0)))
    conv_sum = lax.conv_general_dilated(
        padded[None],
        conv_weight,
        (1, 1, 1),
        "VALID",
        dimension_numbers=("NDHWC", "DHWIO", "NDHWC"),
        preferred_element_type=jnp.float32,
    )[0]
    out_width = conv_weight.shape[-1]
    own_channels = lax.dynamic_slice_in_dim(mixed, chan_index * out_width, out_width, 3)
    return (own_channels.astype(jnp.float32) + conv_sum).astype(jnp.bfloat16)


def solution(mesh):
    placed = (
        P(("clips", "span"), "patch", None, None),
        P(("clips", "span"), None),
        P(),
        P(),
        P(None, None, None, None, "chan"),
    )
    return jax.shard_map(
        local,
        mesh=mesh,
        in_specs=placed,
        out_specs=P(("clips", "span"), "patch", None, "chan"),
        check_vma=False,
    )
```

profile of v0, /device:TPU:0, one launch (start us, length us, event | category | flops | bytes accessed | tf_op | source)
XLA Modules:
  0.0 52.7 jit_solution(9467739739827908105)
XLA Ops:
  0.0 0.7 %compare_select_fusion = s32[256,1]{0,1:T(1,128)S(1)} fusion(s32[1,256]{1,0:T(1,128)} %param.6), kind=kLoop, calls=%fused_computation.49 | loop fusion | flops 768 | bytes 2048 | tf_op jit(solution)/shard_map/select_n | solution.py:78
  0.8 1.4 %scatter_custom_fusion = s32[256]{0:T(256)S(1)} fusion(s32[256]{0:T(256)S(1)} %bitcast.54, s32[256]{0:T(256)S(1)} %iota.3, s32[]{:T(128)} %constant.59.clone.1), kind=kCustom, calls=%fused_computation.58 | custom fusion | bytes 1028 | tf_op jit(solution)/shard_map/scatter | solution.py:78
  2.5 21.5 %all_gather.6 = bf16[1,256,4,384]{3,2,0,1:T(4,128)(2,1)S(1)} all-gather(bf16[1,64,4,384]{3,2,0,1:T(4,128)(2,1)} %bitcast.53), channel_id=1, replica_groups=mesh['clips'=2,'patch'=4,'span'=2,'chan'=2] {'patch'}, dimensions={1}, use_global_device_ids=true | all-gather | bytes 983040 | tf_op jit(solution)/shard_map/all_gather | solution.py:75
  24.1 1.5 %gather_fusion = bf16[256,4,384]{2,1,0:T(4,128)(2,1)S(1)} fusion(bf16[256,4,384]{2,1,0:T(4,128)(2,1)S(1)} %bitcast.48, s32[1024]{0:T(1024)S(1)} %pad_clamp_fusion), kind=kCustom, calls=%fused_computation | custom fusion | bytes 1573888 | tf_op jit(solution)/shard_map/jit(_take)/gather | solution.py:80
  25.7 0.2 copy_select_fusion
  26.3 0.6 %fusion.2 = bf16[1,512,768]{2,1,0:T(8,128)(2,1)S(1)} fusion(bf16[512,384]{1,0:T(8,128)(2,1)S(1)} %bitcast.49, bf16[384,768]{1,0:T(8,128)(2,1)S(1)} %copy-done), kind=kOutput, calls=%fused_computation.8 | convolution fusion | flops 302383104 | bytes 1769472 | tf_op jit(solution)/shard_map/fnc,cd->fnd/dot_general | solution.py:92
  26.9 0.5 fusion.31
  27.4 0.2 fusion.20
  27.6 0.3 fusion.3
  27.9 1.9 %all_gather.7 = bf16[2,2,64,384]{3,2,1,0:T(8,128)(2,1)S(1)} all-gather(bf16[1,2,64,384]{3,2,1,0:T(8,128)(2,1)S(1)} %add_convert_fusion), channel_id=1, replica_groups=mesh['clips'=2,'patch'=4,'span'=2,'chan'=2] {'chan'}, dimensions={0}, use_global_device_ids=true | all-gather | bytes 294912 | tf_op jit(solution)/shard_map/all_gather | solution.py:105
  30.0 0.2 multiply_convert_fusion
  30.2 3.4 %collective-permute-start = (bf16[2,2,64,384]{3,2,1,0:T(8,128)(2,1)S(1)}, bf16[2,2,64,384]{3,2,1,0:T(8,128)(2,1)S(1)}, u32[]{:S(2)}, u32[]{:S(2)}) collective-permute-start(bf16[2,2,64,384]{3,2,1,0:T(8,128)(2,1)S(1)} %multiply_convert_fusion), channel_id=1, source_target_pairs={{0,2},{1,3},{4,6},{5,7},{8,10},{9,11},{12,14},{13,15},{16,18},{17,... | collective-permute-start | bytes 589832 | tf_op jit(solution)/shard_map/ppermute | solution.py:20
  33.6 4.4 %collective-permute-done = bf16[2,2,64,384]{3,2,1,0:T(8,128)(2,1)S(1)} collective-permute-done((bf16[2,2,64,384]{3,2,1,0:T(8,128)(2,1)S(1)}, bf16[2,2,64,384]{3,2,1,0:T(8,128)(2,1)S(1)}, u32[]{:S(2)}, u32[]{:S(2)}) %collective-permute-start) | collective-permute-done | bytes 196640 | tf_op jit(solution)/shard_map/ppermute | solution.py:20
  38.1 1.6 %collective-permute-start.1 = (bf16[4,1,64,384]{3,2,1,0:T(8,128)(2,1)S(1)}, bf16[4,1,64,384]{3,2,1,0:T(8,128)(2,1)S(1)}, u32[]{:S(2)}, u32[]{:S(2)}) collective-permute-start(bf16[4,1,64,384]{3,2,1,0:T(8,128)(2,1)S(1)} %get-tuple-element.5), channel_id=1, source_target_pairs={{0,4},{4,8},{8,12},{1,5},{5,9},{9,13},{2,6},{6,10},{10,14},{3,7},{... | collective-permute-start | bytes 589832 | tf_op jit(solution)/shard_map/ppermute | solution.py:31
  39.7 1.3 %collective-permute-start.2 = (bf16[4,1,64,384]{3,2,1,0:T(8,128)(2,1)S(1)}, bf16[4,1,64,384]{3,2,1,0:T(8,128)(2,1)S(1)}, u32[]{:S(2)}, u32[]{:S(2)}) collective-permute-start(bf16[4,1,64,384]{3,2,1,0:T(8,128)(2,1)S(1)} %get-tuple-element.6), channel_id=1, source_target_pairs={{4,0},{8,4},{12,8},{5,1},{9,5},{13,9},{6,2},{10,6},{14,10},{7,3},{... | collective-permute-start | bytes 589832 | tf_op jit(solution)/shard_map/ppermute | solution.py:33
  41.1 2.2 %collective-permute-done.1 = bf16[4,1,64,384]{3,2,1,0:T(8,128)(2,1)S(1)} collective-permute-done((bf16[4,1,64,384]{3,2,1,0:T(8,128)(2,1)S(1)}, bf16[4,1,64,384]{3,2,1,0:T(8,128)(2,1)S(1)}, u32[]{:S(2)}, u32[]{:S(2)}) %collective-permute-start.1) | collective-permute-done | bytes 196640 | tf_op jit(solution)/shard_map/ppermute | solution.py:31
  43.4 4.1 %collective-permute-done.2 = bf16[4,1,64,384]{3,2,1,0:T(8,128)(2,1)S(1)} collective-permute-done((bf16[4,1,64,384]{3,2,1,0:T(8,128)(2,1)S(1)}, bf16[4,1,64,384]{3,2,1,0:T(8,128)(2,1)S(1)}, u32[]{:S(2)}, u32[]{:S(2)}) %collective-permute-start.2) | collective-permute-done | bytes 196640 | tf_op jit(solution)/shard_map/ppermute | solution.py:33
  47.5 0.3 fusion.10
  47.8 0.3 copy.34
  48.2 0.3 pad.5.clone
  48.7 1.3 %copy-done.2 = bf16[3,3,3,384,192]{3,4,2,1,0:T(8,128)(2,1)S(1)} copy-done((bf16[3,3,3,384,192]{3,4,2,1,0:T(8,128)(2,1)S(1)}, bf16[3,3,3,384,192]{3,4,2,1,0:T(8,128)(2,1)}, u32[]{:S(2)}) %copy-start.2) | copy-done | bytes 3981336
  49.9 1.8 %convolution_select_fusion = f32[2,2,8,9,192]{4,2,3,1,0:T(8,128)S(1)} fusion(bf16[3,3,3,384,192]{3,4,2,1,0:T(8,128)(2,1)S(1)} %copy-done.2, bf16[4,4,1,7,2,384]{5,3,4,1,0,2:T(8,128)(2,1)S(1)} %slice.24, bf16[4,4,1,8,9,384]{5,3,4,1,0,2:T(8,128)(2,1)S(1)} %copy.30, pred[8,9]{0,1:T(8,128)(4,1)S(1)} %copy-done.3), kind=kOutput, calls=%fused_computation.10 | convolution fusion | flops 1149917184 | bytes 5259336 | tf_op jit(solution)/shard_map/conv_general_dilated | solution.py:111
  51.9 0.2 fusion.19
  52.0 0.7 %copy.32 = bf16[2,2,64,192]{3,2,1,0:T(8,128)(2,1)} copy(bf16[2,2,64,192]{3,1,2,0:T(2,128)(2,1)S(1)} %fusion.19) | data formatting | bytes 196608 | tf_op jit(solution)/shard_map/convert_element_type | solution.py:121
  (30 shorter events, 1.5 us)
Async XLA Ops:
  0.0 26.3 %copy-start = (bf16[384,768]{1,0:T(8,128)(2,1)S(1)}, bf16[384,768]{1,0:T(8,128)(2,1)}, u32[]{:S(2)}) copy-start(bf16[384,768]{1,0:T(8,128)(2,1)} %param.8) | copy-start | bytes 1769476
  25.9 1.0 %copy-start.1 = (bf16[384,384]{1,0:T(8,128)(2,1)S(1)}, bf16[384,384]{1,0:T(8,128)(2,1)}, u32[]{:S(2)}) copy-start(bf16[384,384]{1,0:T(8,128)(2,1)} %param.7) | copy-start | bytes 884740
  30.2 7.9 %collective-permute-start = (bf16[2,2,64,384]{3,2,1,0:T(8,128)(2,1)S(1)}, bf16[2,2,64,384]{3,2,1,0:T(8,128)(2,1)S(1)}, u32[]{:S(2)}, u32[]{:S(2)}) collective-permute-start(bf16[2,2,64,384]{3,2,1,0:T(8,128)(2,1)S(1)} %multiply_convert_fusion), channel_id=1, source_target_pairs={{0,2},{1,3},{4,6},{5,7},{8,10},{9,11},{12,14},{13,15},{16,18},{17,... | collective-permute-start | bytes 589832 | tf_op jit(solution)/shard_map/ppermute | solution.py:20
  38.1 5.2 %collective-permute-start.1 = (bf16[4,1,64,384]{3,2,1,0:T(8,128)(2,1)S(1)}, bf16[4,1,64,384]{3,2,1,0:T(8,128)(2,1)S(1)}, u32[]{:S(2)}, u32[]{:S(2)}) collective-permute-start(bf16[4,1,64,384]{3,2,1,0:T(8,128)(2,1)S(1)} %get-tuple-element.5), channel_id=1, source_target_pairs={{0,4},{4,8},{8,12},{1,5},{5,9},{9,13},{2,6},{6,10},{10,14},{3,7},{... | collective-permute-start | bytes 589832 | tf_op jit(solution)/shard_map/ppermute | solution.py:31
  39.7 7.8 %collective-permute-start.2 = (bf16[4,1,64,384]{3,2,1,0:T(8,128)(2,1)S(1)}, bf16[4,1,64,384]{3,2,1,0:T(8,128)(2,1)S(1)}, u32[]{:S(2)}, u32[]{:S(2)}) collective-permute-start(bf16[4,1,64,384]{3,2,1,0:T(8,128)(2,1)S(1)} %get-tuple-element.6), channel_id=1, source_target_pairs={{4,0},{8,4},{12,8},{5,1},{9,5},{13,9},{6,2},{10,6},{14,10},{7,3},{... | collective-permute-start | bytes 589832 | tf_op jit(solution)/shard_map/ppermute | solution.py:33
  47.8 2.1 %copy-start.2 = (bf16[3,3,3,384,192]{3,4,2,1,0:T(8,128)(2,1)S(1)}, bf16[3,3,3,384,192]{3,4,2,1,0:T(8,128)(2,1)}, u32[]{:S(2)}) copy-start(bf16[3,3,3,384,192]{3,4,2,1,0:T(8,128)(2,1)} %param.9) | copy-start | bytes 11943940
  48.1 1.8 %copy-start.3 = (pred[8,9]{0,1:T(8,128)(4,1)S(1)}, pred[8,9]{0,1:T(8,128)(4,1)}, u32[]{:S(2)}) copy-start(pred[8,9]{0,1:T(8,128)(4,1)} %constant.87) | copy-start | bytes 220
where the time goes:
time: 53 us; the launch traced here: 52.7 us
  blocking collectives  23.5 us (44%)
  waiting for transfers between devices  10.8 us (20%)
  local copies, waits for them, and re-layouts  6.42 us (12%)
  starting transfers between devices  6.26 us (12%)
  matrix products  3.09 us (6%)
  other arithmetic  2.41 us (5%)
    all_gather x1, blocking collectives, local(): every_tile = lax.all_gather(latent_tiles, 'patch', axis=1, tiled=True)[0]  21.5 us
    ppermute x1, waiting for transfers between devices, shifted(): return lax.ppermute(x, axis, pairs)  4.45 us
    ppermute x1, waiting for transfers between devices, with_halo(): lax.ppermute(head, axis, [((i + 1) % count, i) for i in range(ends)])  4.12 us
    ppermute x1, starting transfers between devices, shifted(): return lax.ppermute(x, axis, pairs)  3.41 us
    ppermute x1, waiting for transfers between devices, with_halo(): lax.ppermute(tail, axis, [(i, (i + 1) % count) for i in range(ends)])  2.23 us
    all_gather x1, blocking collectives, local(): mixed = lax.all_gather(mixed_own, 'chan', axis=0, tiled=True)  1.95 us
    conv_general_dilated x1, matrix products, local(): lax.conv_general_dilated(padded[None], conv_weight, (1, 1, 1), 'VALID', d...  1.75 us
    gather x2, local copies, waits for them, and re-layouts, local(): jnp.take(every_tile, inverse, axis=0).reshape(patch_count, FD, RD, W, C)  1.65 us
  transfers between devices with their start and end apart: 3, of which 3 were waited for; matrix products, arithmetic and copies ran while one was open for 0% of the time, Pallas kernels for 0%

commit v1 on v0

v1 whole, which is shorter than its diff:
```python
import math

import jax
import jax.numpy as jnp
from jax import lax
from jax.sharding import PartitionSpec as P

C = 384
W = 64
RD = 2
FD = 2


epsilon = 1e-06


def scaled_rms(values):
    wide = values.astype(jnp.float32)
    return wide / jnp.sqrt(jnp.mean(wide * wide, axis=-1, keepdims=True) + epsilon)


def attend(queries, key_rows, value_rows):
    scale = 1.0 / math.sqrt(queries.shape[-1])
    scores = (
        jnp.einsum("fqc,fkc->fqk", queries, key_rows, preferred_element_type=jnp.float32) * scale
    )
    largest = jnp.max(scores, axis=-1, keepdims=True)
    powers = jnp.exp(scores - largest)
    totals = jnp.sum(powers, axis=-1, keepdims=True)
    weights = powers.astype(jnp.bfloat16)
    summed = jnp.einsum("fqk,fkc->fqc", weights, value_rows, preferred_element_type=jnp.float32)
    return summed / totals


def spatial_conv(frames, kernel):
    return lax.conv_general_dilated(
        frames,
        kernel,
        (1, 1),
        ((0, 0), (1, 1)),
        dimension_numbers=("NHWC", "HWIO", "NHWC"),
        preferred_element_type=jnp.float32,
    )


def local(latent_tiles, route, w_query, w_keyval, conv_weight):
    patch_count = lax.axis_size("patch")
    patch_index = lax.axis_index("patch")
    chan_count = lax.axis_size("chan")
    chan_index = lax.axis_index("chan")
    span_count = lax.axis_size("span")
    table = route[0]
    block = latent_tiles.shape[1]
    share = block // chan_count
    own_share = lax.dynamic_slice_in_dim(latent_tiles, chan_index * share, share, 1)
    every_tile = lax.all_gather(own_share, ("patch", "chan"), axis=1, tiled=True)[0]
    tile_total = every_tile.shape[0]
    rows = patch_count * RD
    inverse = (
        jnp.zeros((tile_total,), jnp.int32).at[table].set(jnp.arange(tile_total, dtype=jnp.int32))
    )
    placed = jnp.take(every_tile, inverse, axis=0).reshape(patch_count, FD, RD, W, C)
    whole = placed.transpose(1, 0, 2, 3, 4).reshape(FD, rows, W, C)
    normed_all = scaled_rms(whole).astype(jnp.bfloat16)
    padded = jnp.pad(whole, ((0, 0), (1, 1), (0, 0), (0, 0)))
    features = lax.dynamic_slice_in_dim(padded, patch_index * RD, RD + 2, 1)
    normed = scaled_rms(features).astype(jnp.bfloat16)
    ext_cells = (RD + 2) * W
    queries = jnp.einsum(
        "fnc,cd->fnd", normed.reshape(FD, ext_cells, C), w_query, preferred_element_type=jnp.float32
    ).astype(jnp.bfloat16)
    keyvals = jnp.einsum(
        "fnc,cd->fnd",
        normed_all.reshape(FD, rows * W, C),
        w_keyval,
        preferred_element_type=jnp.float32,
    ).astype(jnp.bfloat16)
    attended = attend(queries, keyvals[..., :C], keyvals[..., C:])
    mixed = (features.astype(jnp.float32) + attended.reshape(FD, RD + 2, W, C)).astype(
        jnp.bfloat16
    )
    row_ids = patch_index * RD - 1 + jnp.arange(RD + 2)
    inside = ((row_ids >= 0) & (row_ids < rows))[None, :, None, None]
    activated = jnp.where(inside, jax.nn.silu(scaled_rms(mixed)), 0.0).astype(jnp.bfloat16)
    tap_sums = [spatial_conv(activated, conv_weight[a]) for a in range(3)]
    to_next = jnp.stack([tap_sums[0][0] + tap_sums[1][1], tap_sums[0][1]])
    pairs = [(i, i + 1) for i in range(span_count - 1)]
    from_prev = lax.ppermute(to_next, "span", pairs)
    own_sum = jnp.stack([tap_sums[2][0], tap_sums[1][0] + tap_sums[2][1]])
    out_width = conv_weight.shape[-1]
    own_rows = mixed[:, 1 : RD + 1]
    own_channels = lax.dynamic_slice_in_dim(own_rows, chan_index * out_width, out_width, 3)
    return (own_channels.astype(jnp.float32) + own_sum + from_prev).astype(jnp.bfloat16)


def solution(mesh):
    placed = (
        P(("clips", "span"), "patch", None, None),
        P(("clips", "span"), None),
        P(),
        P(),
        P(None, None, None, None, "chan"),
    )
    return jax.shard_map(
        local,
        mesh=mesh,
        in_specs=placed,
        out_specs=P(("clips", "span"), "patch", None, "chan"),
        check_vma=False,
    )
```

time: 53 us -> 45.6 us (0.86)
  blocking collectives: 23.5 us -> 17.2 us
  waiting for transfers between devices: 10.8 us -> 5.99 us
  matrix products: 3.09 us -> 7.88 us
  starting transfers between devices: 6.26 us -> 3.44 us
  other arithmetic: 2.41 us -> 4.2 us
    all_gather x2 -> x1, blocking collectives: 23.5 us -> 17.2 us  [local(): lax.all_gather(own_share, ('patch', 'chan'), axis=1, tiled=True)[0]]
    ppermute x3 -> x1, waiting for transfers between devices: 10.8 us -> 5.99 us  [local(): from_prev = lax.ppermute(to_next, 'span', pairs)]
    dot_general x3, matrix products: 1.34 us -> 5.73 us  [the longest x1 2.13 us: local(): jnp.einsum('fnc,cd->fnd', normed_all.reshape(FD, rows * W, C), w_keyval,...]
    ppermute x3 -> x1, starting transfers between devices: 6.26 us -> 3.44 us  [local(): from_prev = lax.ppermute(to_next, 'span', pairs)]
    convert_element_type x4 -> x5, other arithmetic: 0.58 us -> 1.63 us  [the longest x1 0.76 us: local(): (own_channels.astype(jnp.float32) + own_sum + from_prev).astype(jnp.bfloa...]
    unnamed x9 -> x10, local copies, waits for them, and re-layouts: 1.61 us -> 0.67 us
    dynamic_slice x2 -> x1, local copies, waits for them, and re-layouts: 0.13 us -> 0.93 us  [local(): lax.dynamic_slice_in_dim(latent_tiles, chan_index * share, share, 1)]
    reduce_sum x2 -> x3, other arithmetic: 0.27 us -> 0.89 us  [scaled_rms(): jnp.mean(wide * wide, axis=-1, keepdims=True) + epsilon]
  transfers between devices with their start and end apart: 3 -> 1, of which waited for: 3 -> 1; matrix products, arithmetic and copies ran while one was open for 0% -> 0% of each run, Pallas kernels for 0% -> 0%
where the time goes in v1:
time: 45.6 us; the launch traced here: 45.3 us
  blocking collectives  17.2 us (38%)
  matrix products  7.88 us (17%)
  local copies, waits for them, and re-layouts  6.26 us (14%)
  waiting for transfers between devices  5.99 us (13%)
  other arithmetic  4.2 us (9%)
  starting transfers between devices  3.44 us (8%)
    all_gather x1, blocking collectives, local(): lax.all_gather(own_share, ('patch', 'chan'), axis=1, tiled=True)[0]  17.2 us
    ppermute x1, waiting for transfers between devices, local(): from_prev = lax.ppermute(to_next, 'span', pairs)  5.99 us
    ppermute x1, starting transfers between devices, local(): from_prev = lax.ppermute(to_next, 'span', pairs)  3.44 us
    conv_general_dilated x3, matrix products, spatial_conv(): lax.conv_general_dilated(frames, kernel, (1, 1), ((0, 0), (1, 1)), dimens...  2.15 us
    dot_general x1, matrix products, local(): jnp.einsum('fnc,cd->fnd', normed_all.reshape(FD, rows * W, C), w_keyval,...  2.13 us
    dot_general x1, matrix products, attend(): jnp.einsum('fqc,fkc->fqk', queries, key_rows, preferred_element_type=jnp....  1.93 us
    dot_general x1, matrix products, attend(): jnp.einsum('fqk,fkc->fqc', weights, value_rows, preferred_element_type=jn...  1.66 us
    gather x2, local copies, waits for them, and re-layouts, local(): jnp.take(every_tile, inverse, axis=0).reshape(patch_count, FD, RD, W, C)  1.65 us
  transfers between devices with their start and end apart: 1, of which 1 were waited for; matrix products, arithmetic and copies ran while one was open for 0% of the time, Pallas kernels for 0%

profile of v1, /device:TPU:0, one launch (start us, length us, event | category | flops | bytes accessed | tf_op | source)
XLA Modules:
  0.0 45.3 jit_solution(2556529948983996494)
XLA Ops:
  0.0 0.7 %compare_select_fusion.1 = s32[256,1]{0,1:T(1,128)S(1)} fusion(s32[1,256]{1,0:T(1,128)} %param.6), kind=kLoop, calls=%fused_computation.61 | loop fusion | flops 768 | bytes 2048 | tf_op jit(solution)/shard_map/select_n | solution.py:60
  0.8 1.4 %scatter_custom_fusion = s32[256]{0:T(256)S(1)} fusion(s32[256]{0:T(256)S(1)} %bitcast.81, s32[256]{0:T(256)S(1)} %iota.8, s32[]{:T(128)} %constant.22.clone.1), kind=kCustom, calls=%fused_computation.69 | custom fusion | bytes 1028 | tf_op jit(solution)/shard_map/scatter | solution.py:60
  2.6 0.9 %constant_dynamic-slice_fusion = bf16[1,32,4,384]{3,2,0,1:T(4,128)(2,1)S(1)} fusion(bf16[1,64,4,384]{3,2,0,1:T(4,128)(2,1)} %bitcast.80, s32[]{:T(128)S(6)} %select_n.35), kind=kLoop, calls=%fused_computation.68 | loop fusion | bytes 196612 | tf_op jit(solution)/shard_map/dynamic_slice | solution.py:55
  3.5 17.2 %all_gather.3 = bf16[1,256,4,384]{3,2,0,1:T(4,128)(2,1)S(1)} all-gather(bf16[1,32,4,384]{3,2,0,1:T(4,128)(2,1)S(1)} %constant_dynamic-slice_fusion), channel_id=1, replica_groups=mesh['clips'=2,'patch'=4,'span'=2,'chan'=2] {'patch','chan'}, dimensions={1}, use_global_device_ids=true | all-gather | bytes 884736 | tf_op jit(solution)/shard_map/all_gather | solution.py:56
  20.7 1.5 %gather_fusion = bf16[256,4,384]{2,1,0:T(4,128)(2,1)S(1)} fusion(bf16[256,4,384]{2,1,0:T(4,128)(2,1)S(1)} %bitcast.71, s32[1024]{0:T(1024)S(1)} %pad_clamp_fusion), kind=kCustom, calls=%fused_computation | custom fusion | bytes 1573888 | tf_op jit(solution)/shard_map/jit(_take)/gather | solution.py:62
  22.4 0.5 %multiply_reduce_fusion = (f32[2,4,2,64]{3,2,1,0:T(2,128)S(1)}, bf16[4,2,2,64,384]{4,3,2,0,1:T(8,128)(2,1)S(1)}) fusion(bf16[4,2,2,64,384]{4,3,2,1,0:T(8,128)(2,1)S(1)} %gather.7, pred[4,2,2,64]{3,2,0,1:T(4,128)(4,1)S(1)} %copy.32), kind=kLoop, calls=%fused_computation.6 | loop fusion | flops 1571840 | bytes 1577984 | tf_op jit(solution)/shard_map/reduce_sum | solution.py:19
  23.7 2.1 %convolution_convert_fusion = bf16[2,512,768]{2,1,0:T(8,128)(2,1)} fusion(bf16[2,512,384]{2,1,0:T(8,128)(2,1)S(1)} %fusion, bf16[384,768]{1,0:T(8,128)(2,1)S(1)} %copy-done), kind=kOutput, calls=%fused_computation.3 | convolution fusion | flops 604766208 | bytes 2949120 | tf_op jit(solution)/shard_map/fnc,cd->fnd/dot_general | solution.py:72
  25.9 1.9 %fusion.46 = (f32[2,256]{1,0:T(2,128)S(1)}, f32[2,256,512]{2,1,0:T(8,128)S(1)}) fusion(bf16[2,512,768]{2,1,0:T(8,128)(2,1)} %convolution_convert_fusion, bf16[2,256,384]{2,1,0:T(8,128)(2,1)S(1)} %bitcast.79, bf16[384,384]{1,0:T(8,128)(2,1)S(1)} %copy-done.2), kind=kOutput, calls=%fused_computation.72 | convolution fusion | flops 353041920 | bytes 2525184 | tf_op jit(solution)/shard_map/fqc,fkc->fqk/dot_general | solution.py:25
  27.8 0.3 fusion.19
  28.1 1.7 %convolution_divide_fusion = f32[2,256,384]{2,1,0:T(8,128)S(1)} fusion(bf16[2,512,768]{2,1,0:T(8,128)(2,1)} %convolution_convert_fusion, f32[2,256,512]{2,1,0:T(8,128)S(1)} %get-tuple-element.14, f32[2,256]{1,0:T(2,128)S(1)} %get-tuple-element.13, f32[2,256]{1,0:T(2,128)S(1)} %fusion.19), kind=kOutput, calls=%fused_computation.17 | convolution fusion | flops 202047488 | bytes 2625536 | tf_op jit(solution)/shard_map/fqk,fkc->fqc/dot_general | solution.py:31
  29.8 0.2 fusion.21
  30.1 0.3 fusion.37
  30.4 0.4 copy.46
  30.8 0.3 pad.5.clone
  31.2 0.5 %fusion.28 = bf16[4,2,8,11,384]{4,1,3,2,0:T(2,128)(2,1)S(1)} fusion(bf16[4,2,7,2,384]{4,1,3,2,0:T(2,128)(2,1)S(1)} %slice.59, bf16[4,2,8,9,384]{4,1,3,2,0:T(2,128)(2,1)S(1)} %bitcast.73), kind=kLoop, calls=%fused_computation.41 | loop fusion | flops 1622016 | bytes 1069056 | tf_op jit(solution)/shard_map/conv_general_dilated | solution.py:36
  31.9 0.7 %fusion.16 = f32[2,16,9,192]{3,1,2,0:T(8,128)S(1)} fusion(bf16[3,3,3,384,192]{3,4,2,1,0:T(8,128)(2,1)S(1)} %copy-done.1, bf16[4,2,8,11,384]{4,1,3,2,0:T(2,128)(2,1)S(1)} %fusion.28, pred[16,9]{0,1:T(8,128)(4,1)S(1)} %copy-done.3), kind=kOutput, calls=%fused_computation.24 | convolution fusion | flops 382261248 | bytes 2091008 | tf_op jit(solution)/shard_map/conv_general_dilated | solution.py:36
  32.7 0.7 %fusion.13 = f32[2,16,9,192]{3,1,2,0:T(8,128)S(1)} fusion(bf16[3,3,3,384,192]{3,4,2,1,0:T(8,128)(2,1)S(1)} %copy-done.1, bf16[4,2,8,11,384]{4,1,3,2,0:T(2,128)(2,1)S(1)} %fusion.28, pred[16,9]{0,1:T(8,128)(4,1)S(1)} %copy-done.3), kind=kOutput, calls=%fused_computation.23 | convolution fusion | flops 382261248 | bytes 2091008 | tf_op jit(solution)/shard_map/conv_general_dilated | solution.py:36
  33.4 0.7 %fusion.10 = f32[2,16,9,192]{3,1,2,0:T(8,128)S(1)} fusion(bf16[3,3,3,384,192]{3,4,2,1,0:T(8,128)(2,1)S(1)} %copy-done.1, bf16[4,2,8,11,384]{4,1,3,2,0:T(2,128)(2,1)S(1)} %fusion.28, pred[16,9]{0,1:T(8,128)(4,1)S(1)} %copy-done.3), kind=kOutput, calls=%fused_computation.22 | convolution fusion | flops 382261248 | bytes 2091008 | tf_op jit(solution)/shard_map/conv_general_dilated | solution.py:36
  34.1 0.2 copy.41
  34.4 0.2 copy.37
  34.7 0.2 copy.39
  35.1 3.4 %collective-permute-start = (f32[2,2,64,192]{3,2,1,0:T(8,128)S(1)}, f32[2,2,64,192]{3,2,1,0:T(8,128)S(1)}, u32[]{:S(2)}, u32[]{:S(2)}) collective-permute-start(f32[2,2,64,192]{3,2,1,0:T(8,128)S(1)} %pad_maximum_fusion), channel_id=1, source_target_pairs={{0,2},{1,3},{4,6},{5,7},{8,10},{9,11},{12,14},{13,15},{16,18},{17,... | collective-permute-start | bytes 589832 | tf_op jit(solution)/shard_map/ppermute | solution.py:88
  38.6 6.0 %collective-permute-done = f32[2,2,64,192]{3,2,1,0:T(8,128)S(1)} collective-permute-done((f32[2,2,64,192]{3,2,1,0:T(8,128)S(1)}, f32[2,2,64,192]{3,2,1,0:T(8,128)S(1)}, u32[]{:S(2)}, u32[]{:S(2)}) %collective-permute-start) | collective-permute-done | bytes 196640 | tf_op jit(solution)/shard_map/ppermute | solution.py:88
  44.5 0.8 %fusion.41 = bf16[2,2,64,192]{3,2,1,0:T(8,128)(2,1)} fusion(f32[2,2,64,192]{3,2,1,0:T(8,128)S(1)} %collective-permute-done, f32[1,2,64,192]{3,2,1,0:T(8,128)S(1)} %get-tuple-element.10, f32[1,2,64,192]{3,2,1,0:T(8,128)S(1)} %get-tuple-element.9, bf16[2,2,64,384]{3,2,1,0:T(8,128)(2,1)S(1)} %slice.58, s32[]{:T(128)S(6)} %select_n.38), kind=kLoop, calls=%fused_computation.53 | loop fusion | flops 245760 | bytes 589828 | tf_op jit(solution)/shard_map/convert_element_type | solution.py:93
  (36 shorter events, 1.9 us)
Async XLA Ops:
  0.0 23.7 %copy-start = (bf16[384,768]{1,0:T(8,128)(2,1)S(1)}, bf16[384,768]{1,0:T(8,128)(2,1)}, u32[]{:S(2)}) copy-start(bf16[384,768]{1,0:T(8,128)(2,1)} %param.8) | copy-start | bytes 1769476
  23.7 2.1 %copy-start.2 = (bf16[384,384]{1,0:T(8,128)(2,1)S(1)}, bf16[384,384]{1,0:T(8,128)(2,1)}, u32[]{:S(2)}) copy-start(bf16[384,384]{1,0:T(8,128)(2,1)} %param.7) | copy-start | bytes 884740
  29.8 2.1 %copy-start.1 = (bf16[3,3,3,384,192]{3,4,2,1,0:T(8,128)(2,1)S(1)}, bf16[3,3,3,384,192]{3,4,2,1,0:T(8,128)(2,1)}, u32[]{:S(2)}) copy-start(bf16[3,3,3,384,192]{3,4,2,1,0:T(8,128)(2,1)} %param.9) | copy-start | bytes 11943940
  30.4 1.5 %copy-start.3 = (pred[16,9]{0,1:T(8,128)(4,1)S(1)}, pred[16,9]{0,1:T(8,128)(4,1)}, u32[]{:S(2)}) copy-start(pred[16,9]{0,1:T(8,128)(4,1)} %constant.82) | copy-start | bytes 436
  35.1 9.5 %collective-permute-start = (f32[2,2,64,192]{3,2,1,0:T(8,128)S(1)}, f32[2,2,64,192]{3,2,1,0:T(8,128)S(1)}, u32[]{:S(2)}, u32[]{:S(2)}) collective-permute-start(f32[2,2,64,192]{3,2,1,0:T(8,128)S(1)} %pad_maximum_fusion), channel_id=1, source_target_pairs={{0,2},{1,3},{4,6},{5,7},{8,10},{9,11},{12,14},{13,15},{16,18},{17,... | collective-permute-start | bytes 589832 | tf_op jit(solution)/shard_map/ppermute | solution.py:88

commit v2 on v1

--- a/solution.py
+++ b/solution.py
@@ -56,10 +56,12 @@
     every_tile = lax.all_gather(own_share, ("patch", "chan"), axis=1, tiled=True)[0]
     tile_total = every_tile.shape[0]
     rows = patch_count * RD
-    inverse = (
-        jnp.zeros((tile_total,), jnp.int32).at[table].set(jnp.arange(tile_total, dtype=jnp.int32))
-    )
-    placed = jnp.take(every_tile, inverse, axis=0).reshape(patch_count, FD, RD, W, C)
+    slots = jnp.arange(tile_total, dtype=jnp.int32)
+    one_hot = (slots[:, None] == table[None, :]).astype(jnp.bfloat16)
+    placed = jnp.dot(
+        one_hot, every_tile.reshape(tile_total, -1), preferred_element_type=jnp.float32
+    ).astype(jnp.bfloat16)
+    placed = placed.reshape(patch_count, FD, RD, W, C)
     whole = placed.transpose(1, 0, 2, 3, 4).reshape(FD, rows, W, C)
     normed_all = scaled_rms(whole).astype(jnp.bfloat16)
     padded = jnp.pad(whole, ((0, 0), (1, 1), (0, 0), (0, 0)))
@@ -83,14 +85,14 @@
     inside = ((row_ids >= 0) & (row_ids < rows))[None, :, None, None]
     activated = jnp.where(inside, jax.nn.silu(scaled_rms(mixed)), 0.0).astype(jnp.bfloat16)
     tap_sums = [spatial_conv(activated, conv_weight[a]) for a in range(3)]
-    to_next = jnp.stack([tap_sums[0][0] + tap_sums[1][1], tap_sums[0][1]])
+    to_next = jnp.stack([tap_sums[0][0] + tap_sums[1][1], tap_sums[0][1]]).astype(jnp.bfloat16)
     pairs = [(i, i + 1) for i in range(span_count - 1)]
     from_prev = lax.ppermute(to_next, "span", pairs)
     own_sum = jnp.stack([tap_sums[2][0], tap_sums[1][0] + tap_sums[2][1]])
     out_width = conv_weight.shape[-1]
     own_rows = mixed[:, 1 : RD + 1]
     own_channels = lax.dynamic_slice_in_dim(own_rows, chan_index * out_width, out_width, 3)
-    return (own_channels.astype(jnp.float32) + own_sum + from_prev).astype(jnp.bfloat16)
+    return (own_channels.astype(jnp.float32) + own_sum + from_prev.astype(jnp.float32)).astype(jnp.bfloat16)
 
 
 def solution(mesh):

time: 45.6 us -> 41.8 us (0.917)
  waiting for transfers between devices: 5.99 us -> 3.2 us
  local copies, waits for them, and re-layouts: 6.26 us -> 4.71 us
    ppermute x1, waiting for transfers between devices: 5.99 us -> 3.2 us  [local(): from_prev = lax.ppermute(to_next, 'span', pairs)]
    gather x2 -> x0, local copies, waits for them, and re-layouts: 1.65 us -> none  [local(): jnp.take(every_tile, inverse, axis=0).reshape(patch_count, FD, RD, W, C)]
    scatter x1 -> x0, local copies, waits for them, and re-layouts: 1.39 us -> none  [local(): jnp.zeros((tile_total,), jnp.int32).at[table]]
    reshape x0 -> x1, other arithmetic: none -> 1.39 us  [local(): placed = placed.reshape(patch_count, FD, RD, W, C)]
    unnamed x10 -> x16, local copies, waits for them, and re-layouts: 0.67 us -> 1.74 us
    select_n x2 -> x0, other arithmetic: 0.75 us -> none  [the longest x1 0.74 us: local(): jnp.zeros((tile_total,), jnp.int32).at[table]]
    reshape x0 -> x1, local copies, waits for them, and re-layouts: none -> 0.47 us  [local(): placed = placed.reshape(patch_count, FD, RD, W, C)]
    convert_element_type x2 -> x1, other arithmetic: 0.92 us -> 0.77 us  [local(): (own_channels.astype(jnp.float32) + own_sum + from_prev.astype(jnp.float3...]
where the time goes in v2:
time: 41.8 us; the launch traced here: 41.5 us
  blocking collectives  17.2 us (41%)
  matrix products  8.24 us (20%)
  local copies, waits for them, and re-layouts  4.71 us (11%)
  other arithmetic  4.38 us (10%)
  starting transfers between devices  3.42 us (8%)
  waiting for transfers between devices  3.2 us (8%)
    all_gather x1, blocking collectives, local(): lax.all_gather(own_share, ('patch', 'chan'), axis=1, tiled=True)[0]  17.2 us
    ppermute x1, starting transfers between devices, local(): from_prev = lax.ppermute(to_next, 'span', pairs)  3.42 us
    ppermute x1, waiting for transfers between devices, local(): from_prev = lax.ppermute(to_next, 'span', pairs)  3.2 us
    conv_general_dilated x3, matrix products, spatial_conv(): lax.conv_general_dilated(frames, kernel, (1, 1), ((0, 0), (1, 1)), dimens...  2.15 us
    dot_general x1, matrix products, local(): jnp.einsum('fnc,cd->fnd', normed_all.reshape(FD, rows * W, C), w_keyval,...  2.13 us
    dot_general x1, matrix products, attend(): jnp.einsum('fqc,fkc->fqk', queries, key_rows, preferred_element_type=jnp....  1.93 us
    unnamed x16, local copies, waits for them, and re-layouts  1.74 us
    dot_general x1, matrix products, attend(): jnp.einsum('fqk,fkc->fqc', weights, value_rows, preferred_element_type=jn...  1.65 us
  transfers between devices with their start and end apart: 1, of which 1 were waited for; matrix products, arithmetic and copies ran while one was open for 0% of the time, Pallas kernels for 0%

profile of v2, /device:TPU:0, one launch (start us, length us, event | category | flops | bytes accessed | tf_op | source)
XLA Modules:
  0.0 41.5 jit_solution(15235671486107116068)
XLA Ops:
  0.0 1.0 %constant_dynamic-slice_fusion = bf16[1,32,4,384]{3,2,0,1:T(4,128)(2,1)S(1)} fusion(bf16[1,64,4,384]{3,2,0,1:T(4,128)(2,1)} %bitcast.88, s32[]{:T(128)S(6)} %select_n.13), kind=kLoop, calls=%fused_computation.68 | loop fusion | bytes 196612 | tf_op jit(solution)/shard_map/dynamic_slice | solution.py:55
  1.0 17.2 %all_gather.3 = bf16[1,256,4,384]{3,2,0,1:T(4,128)(2,1)S(1)} all-gather(bf16[1,32,4,384]{3,2,0,1:T(4,128)(2,1)S(1)} %constant_dynamic-slice_fusion), channel_id=1, replica_groups=mesh['clips'=2,'patch'=4,'span'=2,'chan'=2] {'patch','chan'}, dimensions={1}, use_global_device_ids=true | all-gather | bytes 884736 | tf_op jit(solution)/shard_map/all_gather | solution.py:56
  18.4 0.4 convolution_convert_fusion
  18.7 0.5 %reshape.60 = bf16[4,2,2,64,384]{4,3,2,1,0:T(8,128)(2,1)S(1)} reshape(bf16[256,1536]{1,0:T(8,128)(2,1)S(1)} %convolution_convert_fusion) | data formatting | bytes 1572864 | tf_op jit(solution)/shard_map/reshape | solution.py:64
  19.2 0.2 multiply_reduce_fusion
  19.4 1.4 %fusion.47 = (bf16[4,2,2,64,384]{4,3,2,0,1:T(8,128)(2,1)S(1)}, f32[2,4,2,64,384]{4,3,2,1,0:T(8,128)}) fusion(bf16[4,2,2,64,384]{4,3,2,1,0:T(8,128)(2,1)S(1)} %reshape.60), kind=kLoop, calls=%fused_computation.69 | loop fusion | flops 393216 | bytes 3145728 | tf_op jit(solution)/shard_map/reshape | solution.py:64
  21.3 0.9 %copy-done.1 = f32[2,4,2,64,384]{4,3,2,1,0:T(8,128)S(1)} copy-done((f32[2,4,2,64,384]{4,3,2,1,0:T(8,128)S(1)}, f32[2,4,2,64,384]{4,3,2,1,0:T(8,128)}, u32[]{:S(2)}) %copy-start.1) | copy-done | bytes 1572888
  22.5 2.1 %convolution_convert_fusion.1 = bf16[2,512,768]{2,1,0:T(8,128)(2,1)} fusion(bf16[2,512,384]{2,1,0:T(8,128)(2,1)S(1)} %fusion, bf16[384,768]{1,0:T(8,128)(2,1)S(1)} %copy-done), kind=kOutput, calls=%fused_computation.2 | convolution fusion | flops 604766208 | bytes 2949120 | tf_op jit(solution)/shard_map/fnc,cd->fnd/dot_general | solution.py:74
  24.6 1.9 %fusion.48 = (f32[2,256]{1,0:T(2,128)S(1)}, f32[2,256,512]{2,1,0:T(8,128)S(1)}) fusion(bf16[2,512,768]{2,1,0:T(8,128)(2,1)} %convolution_convert_fusion.1, bf16[2,256,384]{2,1,0:T(8,128)(2,1)S(1)} %bitcast.86, bf16[384,384]{1,0:T(8,128)(2,1)S(1)} %copy-done.4), kind=kOutput, calls=%fused_computation.70 | convolution fusion | flops 353041920 | bytes 2525184 | tf_op jit(solution)/shard_map/fqc,fkc->fqk/dot_general | solution.py:25
  26.5 0.3 fusion.19
  26.9 1.6 %convolution_divide_fusion = f32[2,256,384]{2,1,0:T(8,128)S(1)} fusion(bf16[2,512,768]{2,1,0:T(8,128)(2,1)} %convolution_convert_fusion.1, f32[2,256,512]{2,1,0:T(8,128)S(1)} %get-tuple-element.13, f32[2,256]{1,0:T(2,128)S(1)} %get-tuple-element.12, f32[2,256]{1,0:T(2,128)S(1)} %fusion.19), kind=kOutput, calls=%fused_computation.16 | convolution fusion | flops 202047488 | bytes 2625536 | tf_op jit(solution)/shard_map/fqk,fkc->fqc/dot_general | solution.py:31
  28.8 0.3 fusion.37
  29.1 0.4 copy.78
  29.5 0.3 pad.5.clone
  29.9 0.5 %fusion.28 = bf16[4,2,8,11,384]{4,1,3,2,0:T(2,128)(2,1)S(1)} fusion(bf16[4,2,7,2,384]{4,1,3,2,0:T(2,128)(2,1)S(1)} %slice.59, bf16[4,2,8,9,384]{4,1,3,2,0:T(2,128)(2,1)S(1)} %bitcast.79), kind=kLoop, calls=%fused_computation.39 | loop fusion | flops 1622016 | bytes 1069056 | tf_op jit(solution)/shard_map/conv_general_dilated | solution.py:36
  30.7 0.7 %fusion.13 = f32[2,16,9,192]{3,1,2,0:T(8,128)S(1)} fusion(bf16[3,3,3,384,192]{3,4,2,1,0:T(8,128)(2,1)S(1)} %copy-done.3, bf16[4,2,8,11,384]{4,1,3,2,0:T(2,128)(2,1)S(1)} %fusion.28, pred[16,9]{0,1:T(8,128)(4,1)S(1)} %copy-done.5), kind=kOutput, calls=%fused_computation.22 | convolution fusion | flops 382261248 | bytes 2091008 | tf_op jit(solution)/shard_map/conv_general_dilated | solution.py:36
  31.4 0.7 %fusion.10 = f32[2,16,9,192]{3,1,2,0:T(8,128)S(1)} fusion(bf16[3,3,3,384,192]{3,4,2,1,0:T(8,128)(2,1)S(1)} %copy-done.3, bf16[4,2,8,11,384]{4,1,3,2,0:T(2,128)(2,1)S(1)} %fusion.28, pred[16,9]{0,1:T(8,128)(4,1)S(1)} %copy-done.5), kind=kOutput, calls=%fused_computation.21 | convolution fusion | flops 382261248 | bytes 2091008 | tf_op jit(solution)/shard_map/conv_general_dilated | solution.py:36
  32.1 0.7 %fusion.51 = (bf16[2,16,9,192]{3,1,2,0:T(8,128)(2,1)S(1)}, f32[2,16,9,192]{3,1,2,0:T(8,128)S(1)}) fusion(bf16[3,3,3,384,192]{3,4,2,1,0:T(8,128)(2,1)S(1)} %copy-done.3, bf16[4,2,8,11,384]{4,1,3,2,0:T(2,128)(2,1)S(1)} %fusion.28, pred[16,9]{0,1:T(8,128)(4,1)S(1)} %copy-done.5), kind=kOutput, calls=%fused_computation.71 | convolution fusion | flops 382316544 | bytes 2201600 | tf_op jit(solution)/shard_map/conv_general_dilated | solution.py:36
  32.8 0.2 copy.67
  33.4 0.2 copy.65
  33.6 0.2 copy.69
  34.0 3.4 %collective-permute-start = (bf16[2,2,64,192]{3,2,1,0:T(8,128)(2,1)S(1)}, bf16[2,2,64,192]{3,2,1,0:T(8,128)(2,1)S(1)}, u32[]{:S(2)}, u32[]{:S(2)}) collective-permute-start(bf16[2,2,64,192]{3,2,1,0:T(8,128)(2,1)S(1)} %pad_maximum_fusion), channel_id=1, source_target_pairs={{0,2},{1,3},{4,6},{5,7},{8,10},{9,11},{12,14},{13,15},{16,18},{17,... | collective-permute-start | bytes 294920 | tf_op jit(solution)/shard_map/ppermute | solution.py:90
  37.5 3.2 %collective-permute-done = bf16[2,2,64,192]{3,2,1,0:T(8,128)(2,1)S(1)} collective-permute-done((bf16[2,2,64,192]{3,2,1,0:T(8,128)(2,1)S(1)}, bf16[2,2,64,192]{3,2,1,0:T(8,128)(2,1)S(1)}, u32[]{:S(2)}, u32[]{:S(2)}) %collective-permute-start) | collective-permute-done | bytes 98336 | tf_op jit(solution)/shard_map/ppermute | solution.py:90
  40.7 0.8 %fusion.41 = bf16[2,2,64,192]{3,2,1,0:T(8,128)(2,1)} fusion(f32[1,2,64,192]{3,2,1,0:T(8,128)S(1)} %get-tuple-element.10, f32[1,2,64,192]{3,2,1,0:T(8,128)S(1)} %get-tuple-element.11, bf16[2,2,64,192]{3,2,1,0:T(8,128)(2,1)S(1)} %collective-permute-done, bf16[2,2,64,384]{3,2,1,0:T(8,128)(2,1)S(1)} %slice.58, s32[]{:T(128)S(6)} %select_n.15), kind=kLoop, calls=%fused_computation.51 | loop fusion | flops 294912 | bytes 491524 | tf_op jit(solution)/shard_map/convert_element_type | solution.py:95
  (35 shorter events, 1.7 us)
Async XLA Ops:
  0.0 22.5 %copy-start = (bf16[384,768]{1,0:T(8,128)(2,1)S(1)}, bf16[384,768]{1,0:T(8,128)(2,1)}, u32[]{:S(2)}) copy-start(bf16[384,768]{1,0:T(8,128)(2,1)} %param.8) | copy-start | bytes 1769476
  0.0 18.4 %copy-start.2 = (s32[1,256]{1,0:T(1,128)S(1)}, s32[1,256]{1,0:T(1,128)}, u32[]{:S(2)}) copy-start(s32[1,256]{1,0:T(1,128)} %param.6) | copy-start | bytes 3076
  20.8 1.4 %copy-start.1 = (f32[2,4,2,64,384]{4,3,2,1,0:T(8,128)S(1)}, f32[2,4,2,64,384]{4,3,2,1,0:T(8,128)}, u32[]{:S(2)}) copy-start(f32[2,4,2,64,384]{4,3,2,1,0:T(8,128)} %get-tuple-element.8) | copy-start | bytes 4718596
  22.5 2.1 %copy-start.4 = (bf16[384,384]{1,0:T(8,128)(2,1)S(1)}, bf16[384,384]{1,0:T(8,128)(2,1)}, u32[]{:S(2)}) copy-start(bf16[384,384]{1,0:T(8,128)(2,1)} %param.7) | copy-start | bytes 884740
  28.5 2.1 %copy-start.3 = (bf16[3,3,3,384,192]{3,4,2,1,0:T(8,128)(2,1)S(1)}, bf16[3,3,3,384,192]{3,4,2,1,0:T(8,128)(2,1)}, u32[]{:S(2)}) copy-start(bf16[3,3,3,384,192]{3,4,2,1,0:T(8,128)(2,1)} %param.9) | copy-start | bytes 11943940
  29.1 1.5 %copy-start.5 = (pred[16,9]{0,1:T(8,128)(4,1)S(1)}, pred[16,9]{0,1:T(8,128)(4,1)}, u32[]{:S(2)}) copy-start(pred[16,9]{0,1:T(8,128)(4,1)} %constant.65) | copy-start | bytes 436
  34.0 6.7 %collective-permute-start = (bf16[2,2,64,192]{3,2,1,0:T(8,128)(2,1)S(1)}, bf16[2,2,64,192]{3,2,1,0:T(8,128)(2,1)S(1)}, u32[]{:S(2)}, u32[]{:S(2)}) collective-permute-start(bf16[2,2,64,192]{3,2,1,0:T(8,128)(2,1)S(1)} %pad_maximum_fusion), channel_id=1, source_target_pairs={{0,2},{1,3},{4,6},{5,7},{8,10},{9,11},{12,14},{13,15},{16,18},{17,... | collective-permute-start | bytes 294920 | tf_op jit(solution)/shard_map/ppermute | solution.py:90

commit v3 on v2

v3 whole, which is shorter than its diff:
```python
import functools
import math

import jax
import jax.numpy as jnp
from jax import lax
from jax.experimental import pallas as pl
from jax.sharding import PartitionSpec as P

C = 384
W = 64
RD = 2
FD = 2
KEY_BLOCK = 512


epsilon = 1e-06


def scaled_rms(values):
    wide = values.astype(jnp.float32)
    return wide / jnp.sqrt(jnp.mean(wide * wide, axis=-1, keepdims=True) + epsilon)


def attention_kernel(cells_ref, query_ref, mask_ref, wq_ref, wkv_ref, mixed_ref, act_ref):
    width = wq_ref.shape[0]
    scale = 1.0 / math.sqrt(width)
    feats = query_ref[0].astype(jnp.float32)
    queries = jnp.dot(
        scaled_rms(feats).astype(jnp.bfloat16), wq_ref[...], preferred_element_type=jnp.float32
    ).astype(jnp.bfloat16)
    count = cells_ref.shape[1]
    block = min(count, KEY_BLOCK)

    def fold(step, carry):
        run_max, run_total, run_acc = carry
        cells = cells_ref[0, pl.ds(step * block, block), :]
        keyvals = jnp.dot(
            scaled_rms(cells).astype(jnp.bfloat16), wkv_ref[...], preferred_element_type=jnp.float32
        ).astype(jnp.bfloat16)
        scores = (
            lax.dot_general(
                queries,
                keyvals[:, :width],
                (((1,), (1,)), ((), ())),
                preferred_element_type=jnp.float32,
            )
            * scale
        )
        new_max = jnp.maximum(run_max, jnp.max(scores, axis=-1, keepdims=True))
        factor = jnp.exp(run_max - new_max)
        powers = jnp.exp(scores - new_max)
        run_total = run_total * factor + jnp.sum(powers, axis=-1, keepdims=True)
        run_acc = run_acc * factor + jnp.dot(
            powers.astype(jnp.bfloat16), keyvals[:, width:], preferred_element_type=jnp.float32
        )
        return new_max, run_total, run_acc

    rows = feats.shape[0]
    carry = (
        jnp.full((rows, 1), -jnp.inf, jnp.float32),
        jnp.zeros((rows, 1), jnp.float32),
        jnp.zeros((rows, width), jnp.float32),
    )
    steps = count // block
    if steps == 1:
        carry = fold(0, carry)
    else:
        carry = lax.fori_loop(0, steps, fold, carry)
    _, run_total, run_acc = carry
    mixed = (feats + run_acc / run_total).astype(jnp.bfloat16)
    mixed_ref[0] = mixed
    normed = scaled_rms(mixed)
    act_ref[0] = (normed / (1.0 + jnp.exp(-normed)) * mask_ref[...]).astype(jnp.bfloat16)


def attend_frames(cells, query_feats, mask, w_query, w_keyval):
    frames, count, width = cells.shape
    rows = query_feats.shape[1]
    out = jax.ShapeDtypeStruct((frames, rows, width), jnp.bfloat16)
    return pl.pallas_call(
        attention_kernel,
        grid=(frames,),
        in_specs=[
            pl.BlockSpec((1, count, width), lambda f: (f, 0, 0)),
            pl.BlockSpec((1, rows, width), lambda f: (f, 0, 0)),
            pl.BlockSpec((rows, 1), lambda f: (0, 0)),
            pl.BlockSpec(w_query.shape, lambda f: (0, 0)),
            pl.BlockSpec(w_keyval.shape, lambda f: (0, 0)),
        ],
        out_specs=[
            pl.BlockSpec((1, rows, width), lambda f: (f, 0, 0)),
            pl.BlockSpec((1, rows, width), lambda f: (f, 0, 0)),
        ],
        out_shape=[out, out],
    )(cells, query_feats, mask, w_query, w_keyval)


def spatial_conv(frames, kernel):
    return lax.conv_general_dilated(
        frames,
        kernel,
        (1, 1),
        ((0, 0), (1, 1)),
        dimension_numbers=("NHWC", "HWIO", "NHWC"),
        preferred_element_type=jnp.float32,
    )


def local(latent_tiles, route, w_query, w_keyval, conv_weight):
    patch_count = lax.axis_size("patch")
    patch_index = lax.axis_index("patch")
    chan_count = lax.axis_size("chan")
    chan_index = lax.axis_index("chan")
    span_count = lax.axis_size("span")
    table = route[0]
    block = latent_tiles.shape[1]
    share = block // chan_count
    own_share = lax.dynamic_slice_in_dim(latent_tiles, chan_index * share, share, 1)
    every_tile = lax.all_gather(own_share, ("patch", "chan"), axis=1, tiled=True)[0]
    tile_total = every_tile.shape[0]
    rows = patch_count * RD
    per_owner = tile_total // patch_count
    per_frame = per_owner // FD
    owner = table // per_owner
    spot = table % per_owner
    dest = (spot // per_frame) * (tile_total // FD) + owner * per_frame + spot % per_frame
    slots = jnp.arange(tile_total, dtype=jnp.int32)
    one_hot = (slots[:, None] == dest[None, :]).astype(jnp.bfloat16)
    placed = jnp.dot(
        one_hot, every_tile.reshape(tile_total, -1), preferred_element_type=jnp.float32
    ).astype(jnp.bfloat16)
    whole = placed.reshape(FD, rows, W, C)
    padded = jnp.pad(whole, ((0, 0), (1, 1), (0, 0), (0, 0)))
    features = lax.dynamic_slice_in_dim(padded, patch_index * RD, RD + 2, 1)
    ext_cells = (RD + 2) * W
    row_ids = patch_index * RD - 1 + jnp.arange(RD + 2)
    inside = ((row_ids >= 0) & (row_ids < rows)).astype(jnp.float32)
    mask = jnp.repeat(inside, W)[:, None]
    mixed, activated = attend_frames(
        whole.reshape(FD, rows * W, C),
        features.reshape(FD, ext_cells, C),
        mask,
        w_query,
        w_keyval,
    )
    mixed = mixed.reshape(FD, RD + 2, W, C)
    activated = activated.reshape(FD, RD + 2, W, C)
    tap_sums = [spatial_conv(activated, conv_weight[a]) for a in range(3)]
    to_next = jnp.stack([tap_sums[0][0] + tap_sums[1][1], tap_sums[0][1]]).astype(jnp.bfloat16)
    pairs = [(i, i + 1) for i in range(span_count - 1)]
    from_prev = lax.ppermute(to_next, "span", pairs)
    own_sum = jnp.stack([tap_sums[2][0], tap_sums[1][0] + tap_sums[2][1]])
    out_width = conv_weight.shape[-1]
    own_rows = mixed[:, 1 : RD + 1]
    own_channels = lax.dynamic_slice_in_dim(own_rows, chan_index * out_width, out_width, 3)
    total = own_channels.astype(jnp.float32) + own_sum + from_prev.astype(jnp.float32)
    return total.astype(jnp.bfloat16)


def solution(mesh):
    placed = (
        P(("clips", "span"), "patch", None, None),
        P(("clips", "span"), None),
        P(),
        P(),
        P(None, None, None, None, "chan"),
    )
    return jax.shard_map(
        local,
        mesh=mesh,
        in_specs=placed,
        out_specs=P(("clips", "span"), "patch", None, "chan"),
        check_vma=False,
    )
```

time: 41.8 us -> 42.5 us (1.017)
  Pallas kernels: 0 us -> 5.13 us
  matrix products: 8.24 us -> 4 us
  local copies, waits for them, and re-layouts: 4.71 us -> 7.04 us
  other arithmetic: 4.38 us -> 2.06 us
    dot_general x3 -> x0, matrix products: 5.71 us -> none  [the longest x1 2.13 us: local(): jnp.einsum('fnc,cd->fnd', normed_all.reshape(FD, rows * W, C), w_keyval,...]
    pallas_call x0 -> x1, Pallas kernels: none -> 5.13 us  [attend_frames(): pl.pallas_call(attention_kernel, grid=(frames,), in_specs=[pl.BlockSpec((...]
    another operation x2 -> x4, local copies, waits for them, and re-layouts: 0.21 us -> 2.36 us  [the longest x1 1.35 us: local(): whole.reshape(FD, rows * W, C)]
    reshape x1 -> x3, local copies, waits for them, and re-layouts: 0.47 us -> 2.21 us  [the longest x2 1.74 us: local(): activated = activated.reshape(FD, RD + 2, W, C)]
    conv_general_dilated x3, matrix products: 2.15 us -> 3.63 us  [spatial_conv(): lax.conv_general_dilated(frames, kernel, (1, 1), ((0, 0), (1, 1)), dimens...]
    reshape x1 -> x0, other arithmetic: 1.39 us -> none  [local(): placed = placed.reshape(patch_count, FD, RD, W, C)]
    unnamed x16 -> x11, local copies, waits for them, and re-layouts: 1.74 us -> 0.67 us
    dynamic_slice x1, local copies, waits for them, and re-layouts: 1 us -> 0.04 us  [local(): lax.dynamic_slice_in_dim(latent_tiles, chan_index * share, share, 1)]
where the time goes in v3:
time: 42.5 us; the launch traced here: 42.3 us
  blocking collectives  17.2 us (40%)
  local copies, waits for them, and re-layouts  7.04 us (17%)
  Pallas kernels  5.13 us (12%)
  matrix products  4 us (9%)
  starting transfers between devices  3.41 us (8%)
  waiting for transfers between devices  3.19 us (8%)
  other arithmetic  2.06 us (5%)
    all_gather x1, blocking collectives, local(): lax.all_gather(own_share, ('patch', 'chan'), axis=1, tiled=True)[0]  17.2 us
    pallas_call x1, Pallas kernels, attend_frames(): pl.pallas_call(attention_kernel, grid=(frames,), in_specs=[pl.BlockSpec((...  5.13 us
    conv_general_dilated x3, matrix products, spatial_conv(): lax.conv_general_dilated(frames, kernel, (1, 1), ((0, 0), (1, 1)), dimens...  3.63 us
    ppermute x1, starting transfers between devices, local(): from_prev = lax.ppermute(to_next, 'span', pairs)  3.41 us
    ppermute x1, waiting for transfers between devices, local(): from_prev = lax.ppermute(to_next, 'span', pairs)  3.19 us
    reshape x2, local copies, waits for them, and re-layouts, local(): activated = activated.reshape(FD, RD + 2, W, C)  1.74 us
    another operation x1, local copies, waits for them, and re-layouts, local(): whole.reshape(FD, rows * W, C)  1.35 us
    conv_general_dilated x8, local copies, waits for them, and re-layouts, spatial_conv(): lax.conv_general_dilated(frames, kernel, (1, 1), ((0, 0), (1, 1)), dimens...  0.85 us
  transfers between devices with their start and end apart: 1, of which 1 were waited for; matrix products, arithmetic and copies ran while one was open for 0% of the time, Pallas kernels for 0%

profile of v3, /device:TPU:0, one launch (start us, length us, event | category | flops | bytes accessed | tf_op | source)
XLA Modules:
  0.0 42.3 jit_solution(11511792405187217953)
XLA Ops:
  0.0 0.7 %fusion.29 = s32[1,256]{1,0:T(1,128)S(1)} fusion(s32[1,256]{1,0:T(1,128)} %param.6), kind=kLoop, calls=%fused_computation.47 | loop fusion | flops 10752 | bytes 2048 | tf_op jit(solution)/shard_map/add | solution.py:127
  0.7 0.2 copy-done
  1.0 17.2 %all_gather.3 = bf16[1,256,4,384]{3,2,0,1:T(4,128)(2,1)S(1)} all-gather(bf16[1,32,4,384]{3,2,0,1:T(4,128)(2,1)S(1)} %constant_dynamic-slice_fusion), channel_id=1, replica_groups=mesh['clips'=2,'patch'=4,'span'=2,'chan'=2] {'patch','chan'}, dimensions={1}, use_global_device_ids=true | all-gather | bytes 884736 | tf_op jit(solution)/shard_map/all_gather | solution.py:120
  18.2 0.1 copy.43
  18.3 0.4 convolution_convert_fusion
  18.7 0.5 %reshape.12 = bf16[2,8,64,384]{3,2,1,0:T(8,128)(2,1)S(1)} reshape(bf16[256,1536]{1,0:T(8,128)(2,1)S(1)} %convolution_convert_fusion) | data formatting | bytes 1572864 | tf_op jit(solution)/shard_map/reshape | solution.py:133
  19.2 1.4 %reshape_reshape.3.cells_ref = bf16[2,512,384]{2,1,0:T(8,128)(2,1)} reshape(bf16[256,1536]{1,0:T(8,128)(2,1)S(1)} %convolution_convert_fusion) | data formatting | bytes 1572864 | tf_op jit(solution)/shard_map/reshape;reshape | solution.py:141
  20.6 0.8 %broadcast_in_dim_reshape.4.mask_ref = f32[256,1]{1,0:T(8,128)} reshape(f32[4,64]{1,0:T(4,128)S(1)} %broadcast_in_dim.2) | data formatting | bytes 2048 | tf_op jit(solution)/shard_map/broadcast_in_dim;reshape | solution.py:139
  21.4 0.8 %pad_dynamic-slice_fusion = bf16[2,4,64,384]{3,2,1,0:T(8,128)(2,1)} fusion(s32[]{:T(128)S(6)} %select_n.37, bf16[2,8,64,384]{3,2,1,0:T(8,128)(2,1)S(1)} %reshape.12), kind=kLoop, calls=%fused_computation.14 | loop fusion | bytes 1179652 | tf_op jit(solution)/shard_map/dynamic_slice | solution.py:135
  22.2 5.1 %shard_map.55 = (bf16[2,256,384]{2,1,0:T(8,128)(2,1)}, bf16[2,256,384]{2,1,0:T(8,128)(2,1)}) custom-call(bf16[2,512,384]{2,1,0:T(8,128)(2,1)} %reshape_reshape.3.cells_ref, bf16[2,256,384]{2,1,0:T(8,128)(2,1)} %bitcast.60, f32[256,1]{1,0:T(8,128)} %broadcast_in_dim_reshape.4.mask_ref, bf16[384,384]{1,0:T(8,128)(2,1)} %wq_ref.1, bf16[384,768]{1,0:T(8,128)(2,1)} %wkv_ref.1), custom_call_target="tpu_custom_call" | custom-call | tf_op jit(solution)/shard_map/pallas_call | solution.py:81
  27.4 1.4 %copy.63 = bf16[2,4,64,384]{3,0,2,1:T(2,128)(2,1)S(1)} copy(bf16[2,4,64,384]{3,2,1,0:T(8,128)(2,1)} %bitcast.66) | data formatting | bytes 786432 | tf_op jit(solution)/shard_map/reshape | solution.py:148
  28.8 0.3 pad.5
  29.2 0.5 %fusion.18 = bf16[4,2,8,11,384]{4,1,3,2,0:T(2,128)(2,1)S(1)} fusion(bf16[4,2,7,2,384]{4,1,3,2,0:T(2,128)(2,1)S(1)} %slice.49, bf16[4,2,8,9,384]{4,1,3,2,0:T(2,128)(2,1)S(1)} %bitcast.58), kind=kLoop, calls=%fused_computation.15 | loop fusion | flops 1622016 | bytes 1069056 | tf_op jit(solution)/shard_map/conv_general_dilated | solution.py:100
  29.7 2.2 %fusion.12 = f32[2,16,9,192]{3,1,2,0:T(8,128)S(1)} fusion(bf16[3,3,3,384,192]{3,4,2,1,0:T(8,128)(2,1)} %param.9, bf16[4,2,8,11,384]{4,1,3,2,0:T(2,128)(2,1)S(1)} %fusion.18, pred[16,9]{0,1:T(8,128)(4,1)S(1)} %copy-done.3), kind=kOutput, calls=%fused_computation.12 | convolution fusion | flops 382261248 | bytes 2089104 | tf_op jit(solution)/shard_map/conv_general_dilated | solution.py:100
  31.9 0.3 copy-done.2
  32.2 0.7 %fusion.9 = f32[2,16,9,192]{3,1,2,0:T(8,128)S(1)} fusion(bf16[3,3,3,384,192]{3,4,2,1,0:T(8,128)(2,1)S(1)} %copy-done.2, bf16[4,2,8,11,384]{4,1,3,2,0:T(2,128)(2,1)S(1)} %fusion.18, pred[16,9]{0,1:T(8,128)(4,1)S(1)} %copy-done.3), kind=kOutput, calls=%fused_computation.11 | convolution fusion | flops 382261248 | bytes 2091008 | tf_op jit(solution)/shard_map/conv_general_dilated | solution.py:100
  32.9 0.7 %fusion.30 = (bf16[2,16,9,192]{3,1,2,0:T(8,128)(2,1)S(1)}, f32[2,16,9,192]{3,1,2,0:T(8,128)S(1)}) fusion(bf16[3,3,3,384,192]{3,4,2,1,0:T(8,128)(2,1)S(1)} %copy-done.2, bf16[4,2,8,11,384]{4,1,3,2,0:T(2,128)(2,1)S(1)} %fusion.18, pred[16,9]{0,1:T(8,128)(4,1)S(1)} %copy-done.3), kind=kOutput, calls=%fused_computation.49 | convolution fusion | flops 382316544 | bytes 2201600 | tf_op jit(solution)/shard_map/conv_general_dilated | solution.py:100
  33.7 0.2 copy.33
  33.9 0.1 copy.37
  34.2 0.2 copy.31
  34.5 0.2 copy.35
  34.9 3.4 %collective-permute-start = (bf16[2,2,64,192]{3,2,1,0:T(8,128)(2,1)S(1)}, bf16[2,2,64,192]{3,2,1,0:T(8,128)(2,1)S(1)}, u32[]{:S(2)}, u32[]{:S(2)}) collective-permute-start(bf16[2,2,64,192]{3,2,1,0:T(8,128)(2,1)S(1)} %pad_maximum_fusion), channel_id=1, source_target_pairs={{0,2},{1,3},{4,6},{5,7},{8,10},{9,11},{12,14},{13,15},{16,18},{17,... | collective-permute-start | bytes 294920 | tf_op jit(solution)/shard_map/ppermute | solution.py:152
  38.3 3.2 %collective-permute-done = bf16[2,2,64,192]{3,2,1,0:T(8,128)(2,1)S(1)} collective-permute-done((bf16[2,2,64,192]{3,2,1,0:T(8,128)(2,1)S(1)}, bf16[2,2,64,192]{3,2,1,0:T(8,128)(2,1)S(1)}, u32[]{:S(2)}, u32[]{:S(2)}) %collective-permute-start) | collective-permute-done | bytes 98336 | tf_op jit(solution)/shard_map/ppermute | solution.py:152
  41.5 0.8 %fusion.26 = bf16[2,2,64,192]{3,2,1,0:T(8,128)(2,1)} fusion(f32[1,2,64,192]{3,2,1,0:T(8,128)S(1)} %get-tuple-element.10, f32[1,2,64,192]{3,2,1,0:T(8,128)S(1)} %get-tuple-element.11, bf16[2,2,64,192]{3,2,1,0:T(8,128)(2,1)S(1)} %collective-permute-done, bf16[2,2,64,384]{3,2,1,0:T(8,128)(2,1)S(1)} %slice.48, s32[]{:T(128)S(6)} %select_n.38), kind=kLoop, calls=%fused_computation.25 | loop fusion | flops 294912 | bytes 491524 | tf_op jit(solution)/shard_map/convert_element_type | solution.py:158
  (21 shorter events, 0.5 us)
Async XLA Ops:
  0.0 0.9 %copy-start = (bf16[1,64,4,384]{3,2,1,0:T(4,128)(2,1)S(1)}, bf16[1,64,4,384]{3,2,1,0:T(4,128)(2,1)}, u32[]{:S(2)}) copy-start(bf16[1,64,4,384]{3,2,1,0:T(4,128)(2,1)} %param.5) | copy-start | bytes 589828
  27.4 2.3 %copy-start.3 = (pred[16,9]{0,1:T(8,128)(4,1)S(1)}, pred[16,9]{0,1:T(8,128)(4,1)}, u32[]{:S(2)}) copy-start(pred[16,9]{0,1:T(8,128)(4,1)} %constant.92) | copy-start | bytes 436
  29.7 2.5 %copy-start.2 = (bf16[3,3,3,384,192]{3,4,2,1,0:T(8,128)(2,1)S(1)}, bf16[3,3,3,384,192]{3,4,2,1,0:T(8,128)(2,1)}, u32[]{:S(2)}) copy-start(bf16[3,3,3,384,192]{3,4,2,1,0:T(8,128)(2,1)} %param.9) | copy-start | bytes 11943940
  34.7 3.6 %copy-start.1 = (bf16[2,256,384]{2,1,0:T(8,128)(2,1)S(1)}, bf16[2,256,384]{2,1,0:T(8,128)(2,1)}, u32[]{:S(2)}) copy-start(bf16[2,256,384]{2,1,0:T(8,128)(2,1)} %get-tuple-element.7) | copy-start | bytes 1179652
  34.9 6.7 %collective-permute-start = (bf16[2,2,64,192]{3,2,1,0:T(8,128)(2,1)S(1)}, bf16[2,2,64,192]{3,2,1,0:T(8,128)(2,1)S(1)}, u32[]{:S(2)}, u32[]{:S(2)}) collective-permute-start(bf16[2,2,64,192]{3,2,1,0:T(8,128)(2,1)S(1)} %pad_maximum_fusion), channel_id=1, source_target_pairs={{0,2},{1,3},{4,6},{5,7},{8,10},{9,11},{12,14},{13,15},{16,18},{17,... | collective-permute-start | bytes 294920 | tf_op jit(solution)/shard_map/ppermute | solution.py:152

commit v4 on v3

--- a/solution.py
+++ b/solution.py
@@ -1,4 +1,3 @@
-import functools
 import math
 
 import jax
@@ -22,10 +21,9 @@
     return wide / jnp.sqrt(jnp.mean(wide * wide, axis=-1, keepdims=True) + epsilon)
 
 
-def attention_kernel(cells_ref, query_ref, mask_ref, wq_ref, wkv_ref, mixed_ref, act_ref):
+def attend_frame(cells_ref, frame, feats, wq_ref, wkv_ref):
     width = wq_ref.shape[0]
     scale = 1.0 / math.sqrt(width)
-    feats = query_ref[0].astype(jnp.float32)
     queries = jnp.dot(
         scaled_rms(feats).astype(jnp.bfloat16), wq_ref[...], preferred_element_type=jnp.float32
     ).astype(jnp.bfloat16)
@@ -34,7 +32,7 @@
 
     def fold(step, carry):
         run_max, run_total, run_acc = carry
-        cells = cells_ref[0, pl.ds(step * block, block), :]
+        cells = cells_ref[frame, pl.ds(step * block, block), :]
         keyvals = jnp.dot(
             scaled_rms(cells).astype(jnp.bfloat16), wkv_ref[...], preferred_element_type=jnp.float32
         ).astype(jnp.bfloat16)
@@ -62,49 +60,89 @@
         jnp.zeros((rows, 1), jnp.float32),
         jnp.zeros((rows, width), jnp.float32),
     )
-    steps = count // block
-    if steps == 1:
-        carry = fold(0, carry)
-    else:
-        carry = lax.fori_loop(0, steps, fold, carry)
+    for step in range(count // block):
+        carry = fold(step, carry)
     _, run_total, run_acc = carry
-    mixed = (feats + run_acc / run_total).astype(jnp.bfloat16)
-    mixed_ref[0] = mixed
-    normed = scaled_rms(mixed)
-    act_ref[0] = (normed / (1.0 + jnp.exp(-normed)) * mask_ref[...]).astype(jnp.bfloat16)
-
-
-def attend_frames(cells, query_feats, mask, w_query, w_keyval):
+    return (feats + run_acc / run_total).astype(jnp.bfloat16)
+
+
+def block_kernel(
+    cells_ref, query_ref, mask_ref, wq_ref, wkv_ref, conv_ref, mixed_ref, own_ref, next_ref
+):
+    frames, rows, width = query_ref.shape
+    out_rows = mixed_ref.shape[1]
+    taps = conv_ref.shape[0]
+    line = (rows - out_rows) // 2
+    place = lax.broadcasted_iota(jnp.int32, (rows, rows), 0)
+    source = lax.broadcasted_iota(jnp.int32, (rows, rows), 1)
+    column = place % line
+    shifts = []
+    for c in range(taps):
+        offset = c - 1
+        keep = (source == place + offset) & (column + offset >= 0) & (column + offset < line)
+        shifts.append(keep.astype(jnp.bfloat16))
+    own_acc = [None] * frames
+    next_acc = [None] * frames
+
+    def add(acc, index, value):
+        acc[index] = value if acc[index] is None else acc[index] + value
+
+    for f in range(frames):
+        feats = query_ref[f].astype(jnp.float32)
+        mixed = attend_frame(cells_ref, f, feats, wq_ref, wkv_ref)
+        mixed_ref[f] = mixed[line : line + out_rows]
+        normed = scaled_rms(mixed)
+        activated = (normed / (1.0 + jnp.exp(-normed)) * mask_ref[...]).astype(jnp.bfloat16)
+        moved = [
+            jnp.dot(shifts[c], activated, preferred_element_type=jnp.float32).astype(jnp.bfloat16)
+            for c in range(taps)
+        ]
+        for b in range(taps):
+            for c in range(taps):
+                window = moved[c][b * line : b * line + out_rows]
+                for t in range(frames):
+                    a = f + taps - 1 - t
+                    if 0 <= a < taps:
+                        add(own_acc, t, jnp.dot(window, conv_ref[a, b, c], preferred_element_type=jnp.float32))
+                    a = f - t
+                    if 0 <= a < taps:
+                        add(next_acc, t, jnp.dot(window, conv_ref[a, b, c], preferred_element_type=jnp.float32))
+    for t in range(frames):
+        own_ref[t] = own_acc[t]
+        next_ref[t] = next_acc[t].astype(next_ref.dtype)
+
+
+def fused_block(cells, query_feats, mask, w_query, w_keyval, conv_weight):
     frames, count, width = cells.shape
     rows = query_feats.shape[1]
-    out = jax.ShapeDtypeStruct((frames, rows, width), jnp.bfloat16)
+    out_rows = RD * (rows // (RD + 2))
+    out_width = conv_weight.shape[-1]
+
+    def whole(shape):
+        return pl.BlockSpec(shape, lambda i: (0,) * len(shape))
+
     return pl.pallas_call(
-        attention_kernel,
-        grid=(frames,),
+        block_kernel,
+        grid=(1,),
         in_specs=[
-            pl.BlockSpec((1, count, width), lambda f: (f, 0, 0)),
-            pl.BlockSpec((1, rows, width), lambda f: (f, 0, 0)),
-            pl.BlockSpec((rows, 1), lambda f: (0, 0)),
-            pl.BlockSpec(w_query.shape, lambda f: (0, 0)),
-            pl.BlockSpec(w_keyval.shape, lambda f: (0, 0)),
+            whole(cells.shape),
+            whole(query_feats.shape),
+            whole(mask.shape),
+            whole(w_query.shape),
+            whole(w_keyval.shape),
+            whole(conv_weight.shape),
         ],
         out_specs=[
-            pl.BlockSpec((1, rows, width), lambda f: (f, 0, 0)),
-            pl.BlockSpec((1, rows, width), lambda f: (f, 0, 0)),
+            whole((frames, out_rows, width)),
+            whole((frames, out_rows, out_width)),
+            whole((frames, out_rows, out_width)),
         ],
-        out_shape=[out, out],
-    )(cells, query_feats, mask, w_query, w_keyval)
-
-
-def spatial_conv(frames, kernel):
-    return lax.conv_general_dilated(
-        frames,
-        kernel,
-        (1, 1),
-        ((0, 0), (1, 1)),
-        dimension_numbers=("NHWC", "HWIO", "NHWC"),
-        preferred_element_type=jnp.float32,
-    )
+        out_shape=[
+            jax.ShapeDtypeStruct((frames, out_rows, width), jnp.bfloat16),
+            jax.ShapeDtypeStruct((frames, out_rows, out_width), jnp.float32),
+            jax.ShapeDtypeStruct((frames, out_rows, out_width), jnp.bfloat16),
+        ],
+    )(cells, query_feats, mask, w_query, w_keyval, conv_weight)
 
 
 def local(latent_tiles, route, w_query, w_keyval, conv_weight):
@@ -137,25 +175,20 @@
     row_ids = patch_index * RD - 1 + jnp.arange(RD + 2)
     inside = ((row_ids >= 0) & (row_ids < rows)).astype(jnp.float32)
     mask = jnp.repeat(inside, W)[:, None]
-    mixed, activated = attend_frames(
+    mixed_own, own_sum, to_next = fused_block(
         whole.reshape(FD, rows * W, C),
         features.reshape(FD, ext_cells, C),
         mask,
         w_query,
         w_keyval,
-    )
-    mixed = mixed.reshape(FD, RD + 2, W, C)
-    activated = activated.reshape(FD, RD + 2, W, C)
-    tap_sums = [spatial_conv(activated, conv_weight[a]) for a in range(3)]
-    to_next = jnp.stack([tap_sums[0][0] + tap_sums[1][1], tap_sums[0][1]]).astype(jnp.bfloat16)
+        conv_weight,
+    )
     pairs = [(i, i + 1) for i in range(span_count - 1)]
     from_prev = lax.ppermute(to_next, "span", pairs)
-    own_sum = jnp.stack([tap_sums[2][0], tap_sums[1][0] + tap_sums[2][1]])
     out_width = conv_weight.shape[-1]
-    own_rows = mixed[:, 1 : RD + 1]
-    own_channels = lax.dynamic_slice_in_dim(own_rows, chan_index * out_width, out_width, 3)
+    own_channels = lax.dynamic_slice_in_dim(mixed_own, chan_index * out_width, out_width, 2)
     total = own_channels.astype(jnp.float32) + own_sum + from_prev.astype(jnp.float32)
-    return total.astype(jnp.bfloat16)
+    return total.reshape(FD, RD, W, out_width).astype(jnp.bfloat16)
 
 
 def solution(mesh):

time: 42.5 us -> 49.1 us (1.16)
  local copies, waits for them, and re-layouts: 7.04 us -> 12 us
  Pallas kernels: 5.13 us -> 9.6 us
  matrix products: 4 us -> 0.37 us
    unnamed x11 -> x4, local copies, waits for them, and re-layouts: 0.67 us -> 8.45 us
    pallas_call x1, Pallas kernels: 5.13 us -> 9.6 us  [fused_block(): pl.pallas_call(block_kernel, grid=(1,), in_specs=[whole(cells.shape), who...]
    conv_general_dilated x3 -> x0, matrix products: 3.63 us -> none  [spatial_conv(): lax.conv_general_dilated(frames, kernel, (1, 1), ((0, 0), (1, 1)), dimens...]
    reshape x2 -> x0, local copies, waits for them, and re-layouts: 1.74 us -> none  [local(): activated = activated.reshape(FD, RD + 2, W, C)]
    convert_element_type x1, other arithmetic: 0.77 us -> 1.77 us  [local(): return total.reshape(FD, RD, W, out_width).astype(jnp.bfloat16)]
    conv_general_dilated x8 -> x0, local copies, waits for them, and re-layouts: 0.85 us -> none  [spatial_conv(): lax.conv_general_dilated(frames, kernel, (1, 1), ((0, 0), (1, 1)), dimens...]
where the time goes in v4:
time: 49.1 us; the launch traced here: 48.7 us
  blocking collectives  17.2 us (35%)
  local copies, waits for them, and re-layouts  12 us (24%)
  Pallas kernels  9.6 us (20%)
  waiting for transfers between devices  3.55 us (7%)
  starting transfers between devices  3.39 us (7%)
  other arithmetic  2.51 us (5%)
    all_gather x1, blocking collectives, local(): lax.all_gather(own_share, ('patch', 'chan'), axis=1, tiled=True)[0]  17.2 us
    pallas_call x1, Pallas kernels, fused_block(): pl.pallas_call(block_kernel, grid=(1,), in_specs=[whole(cells.shape), who...  9.6 us
    unnamed x4, local copies, waits for them, and re-layouts  8.45 us
    ppermute x1, waiting for transfers between devices, local(): from_prev = lax.ppermute(to_next, 'span', pairs)  3.55 us
    ppermute x1, starting transfers between devices, local(): from_prev = lax.ppermute(to_next, 'span', pairs)  3.39 us
    convert_element_type x1, other arithmetic, local(): return total.reshape(FD, RD, W, out_width).astype(jnp.bfloat16)  1.77 us
    another operation x1, local copies, waits for them, and re-layouts, local(): whole.reshape(FD, rows * W, C)  1.38 us
  transfers between devices with their start and end apart: 1, of which 1 were waited for; matrix products, arithmetic and copies ran while one was open for 0% of the time, Pallas kernels for 0%

profile of v4, /device:TPU:0, one launch (start us, length us, event | category | flops | bytes accessed | tf_op | source)
XLA Modules:
  0.0 48.7 jit_solution(10065887026397503898)
XLA Ops:
  0.0 0.0 copy-start
  0.0 0.7 %fusion.1 = s32[1,256]{1,0:T(1,128)S(1)} fusion(s32[1,256]{1,0:T(1,128)} %param.6), kind=kLoop, calls=%fused_computation.16 | loop fusion | flops 10752 | bytes 2048 | tf_op jit(solution)/shard_map/add | solution.py:165
  0.7 0.2 copy-done
  1.0 17.2 %all_gather.3 = bf16[1,256,4,384]{3,2,0,1:T(4,128)(2,1)S(1)} all-gather(bf16[1,32,4,384]{3,2,0,1:T(4,128)(2,1)S(1)} %constant_dynamic-slice_fusion), channel_id=1, replica_groups=mesh['clips'=2,'patch'=4,'span'=2,'chan'=2] {'patch','chan'}, dimensions={1}, use_global_device_ids=true | all-gather | bytes 884736 | tf_op jit(solution)/shard_map/all_gather | solution.py:158
  18.2 0.1 copy.12
  18.3 0.4 convolution_convert_fusion
  18.7 0.5 reshape.8
  19.2 1.4 %reshape_reshape.3.cells_ref = bf16[2,512,384]{2,1,0:T(8,128)(2,1)} reshape(bf16[256,1536]{1,0:T(8,128)(2,1)S(1)} %convolution_convert_fusion) | data formatting | bytes 1572864 | tf_op jit(solution)/shard_map/reshape;reshape | solution.py:179
  20.6 0.1 broadcast_in_dim.2
  20.6 0.8 %broadcast_in_dim_reshape.4.mask_ref = f32[256,1]{1,0:T(8,128)} reshape(f32[4,64]{1,0:T(4,128)S(1)} %broadcast_in_dim.2) | data formatting | bytes 2048 | tf_op jit(solution)/shard_map/broadcast_in_dim;reshape | solution.py:177
  21.4 8.1 %copy.11.conv_ref = bf16[3,3,3,384,192]{4,3,2,1,0:T(8,128)(2,1)} copy(bf16[3,3,3,384,192]{3,4,2,1,0:T(8,128)(2,1)} %param.9) | data formatting | bytes 7962624 | tf_op args[4]
  29.6 0.8 %pad_dynamic-slice_fusion = bf16[2,4,64,384]{3,2,1,0:T(8,128)(2,1)} fusion(s32[]{:T(128)S(6)} %select_n.37, bf16[2,8,64,384]{3,2,1,0:T(8,128)(2,1)S(1)} %reshape.8), kind=kLoop, calls=%fused_computation.1 | loop fusion | bytes 1179652 | tf_op jit(solution)/shard_map/dynamic_slice | solution.py:173
  30.4 9.6 %shard_map.55 = (bf16[2,128,384]{2,1,0:T(8,128)(2,1)}, f32[2,128,192]{2,1,0:T(8,128)}, bf16[2,128,192]{2,1,0:T(8,128)(2,1)}) custom-call(bf16[2,512,384]{2,1,0:T(8,128)(2,1)} %reshape_reshape.3.cells_ref, bf16[2,256,384]{2,1,0:T(8,128)(2,1)} %bitcast.12, f32[256,1]{1,0:T(8,128)} %broadcast_in_dim_reshape.4.mask_ref, bf16[384,384]{1,0:T(8,128)(2,1)} %wq_ref.1, ...), custom_call_target="tpu_custom_call" | custom-call | tf_op jit(solution)/shard_map/pallas_call | solution.py:124
  40.0 3.4 %collective-permute-start = (bf16[2,128,192]{2,1,0:T(8,128)(2,1)}, bf16[2,128,192]{2,1,0:T(8,128)(2,1)S(1)}, u32[]{:S(2)}, u32[]{:S(2)}) collective-permute-start(bf16[2,128,192]{2,1,0:T(8,128)(2,1)} %get-tuple-element.10), channel_id=1, source_target_pairs={{0,2},{1,3},{4,6},{5,7},{8,10},{9,11},{12,14},{13,15},{16,18},{17,... | collective-permute-start | bytes 294920 | tf_op jit(solution)/shard_map/ppermute | solution.py:187
  43.4 3.6 %collective-permute-done = bf16[2,128,192]{2,1,0:T(8,128)(2,1)S(1)} collective-permute-done((bf16[2,128,192]{2,1,0:T(8,128)(2,1)}, bf16[2,128,192]{2,1,0:T(8,128)(2,1)S(1)}, u32[]{:S(2)}, u32[]{:S(2)}) %collective-permute-start) | collective-permute-done | bytes 98336 | tf_op jit(solution)/shard_map/ppermute | solution.py:187
  47.0 1.8 %add_convert_fusion = bf16[2,128,192]{2,1,0:T(8,128)(2,1)} fusion(bf16[2,128,192]{2,1,0:T(8,128)(2,1)S(1)} %collective-permute-done, f32[2,128,192]{2,1,0:T(8,128)} %get-tuple-element.9, bf16[2,128,384]{2,1,0:T(8,128)(2,1)} %get-tuple-element.8, s32[]{:T(128)S(6)} %select_n.38), kind=kLoop, calls=%fused_computation.2 | loop fusion | flops 245760 | bytes 491524 | tf_op jit(solution)/shard_map/convert_element_type | solution.py:191
  (2 shorter events, 0.0 us)
Async XLA Ops:
  0.0 0.9 %copy-start = (bf16[1,64,4,384]{3,2,1,0:T(4,128)(2,1)S(1)}, bf16[1,64,4,384]{3,2,1,0:T(4,128)(2,1)}, u32[]{:S(2)}) copy-start(bf16[1,64,4,384]{3,2,1,0:T(4,128)(2,1)} %param.5) | copy-start | bytes 589828
  40.0 7.0 %collective-permute-start = (bf16[2,128,192]{2,1,0:T(8,128)(2,1)}, bf16[2,128,192]{2,1,0:T(8,128)(2,1)S(1)}, u32[]{:S(2)}, u32[]{:S(2)}) collective-permute-start(bf16[2,128,192]{2,1,0:T(8,128)(2,1)} %get-tuple-element.10), channel_id=1, source_target_pairs={{0,2},{1,3},{4,6},{5,7},{8,10},{9,11},{12,14},{13,15},{16,18},{17,... | collective-permute-start | bytes 294920 | tf_op jit(solution)/shard_map/ppermute | solution.py:187

commit v5 on v4

--- a/solution.py
+++ b/solution.py
@@ -4,6 +4,7 @@
 import jax.numpy as jnp
 from jax import lax
 from jax.experimental import pallas as pl
+from jax.experimental.pallas import tpu as pltpu
 from jax.sharding import PartitionSpec as P
 
 C = 384
@@ -67,12 +68,13 @@
 
 
 def block_kernel(
-    cells_ref, query_ref, mask_ref, wq_ref, wkv_ref, conv_ref, mixed_ref, own_ref, next_ref
+    first_ref, cells_ref, query_ref, wq_ref, wkv_ref, conv_ref, mixed_ref, own_ref, next_ref
 ):
     frames, rows, width = query_ref.shape
     out_rows = mixed_ref.shape[1]
     taps = conv_ref.shape[0]
     line = (rows - out_rows) // 2
+    frame_rows = cells_ref.shape[1] // line
     place = lax.broadcasted_iota(jnp.int32, (rows, rows), 0)
     source = lax.broadcasted_iota(jnp.int32, (rows, rows), 1)
     column = place % line
@@ -81,68 +83,88 @@
         offset = c - 1
         keep = (source == place + offset) & (column + offset >= 0) & (column + offset < line)
         shifts.append(keep.astype(jnp.bfloat16))
-    own_acc = [None] * frames
-    next_acc = [None] * frames
-
-    def add(acc, index, value):
-        acc[index] = value if acc[index] is None else acc[index] + value
-
+    row_of = lax.broadcasted_iota(jnp.int32, (rows, width), 0) // line + first_ref[0]
+    inside = (row_of >= 0) & (row_of < frame_rows)
+    moved = []
     for f in range(frames):
         feats = query_ref[f].astype(jnp.float32)
         mixed = attend_frame(cells_ref, f, feats, wq_ref, wkv_ref)
         mixed_ref[f] = mixed[line : line + out_rows]
         normed = scaled_rms(mixed)
-        activated = (normed / (1.0 + jnp.exp(-normed)) * mask_ref[...]).astype(jnp.bfloat16)
-        moved = [
-            jnp.dot(shifts[c], activated, preferred_element_type=jnp.float32).astype(jnp.bfloat16)
-            for c in range(taps)
-        ]
+        activated = jnp.where(inside, normed / (1.0 + jnp.exp(-normed)), 0.0).astype(jnp.bfloat16)
+        moved.append(
+            [
+                jnp.dot(shifts[c], activated, preferred_element_type=jnp.float32).astype(
+                    jnp.bfloat16
+                )
+                for c in range(taps)
+            ]
+        )
+    own_acc = [None] * frames
+    next_acc = [None] * frames
+    for a in range(taps):
+        targets = []
+        for f in range(frames):
+            if 0 <= f + taps - 1 - a < frames:
+                targets.append((f, own_acc, f + taps - 1 - a))
+            if 0 <= f - a < frames:
+                targets.append((f, next_acc, f - a))
+        total = None
         for b in range(taps):
             for c in range(taps):
-                window = moved[c][b * line : b * line + out_rows]
-                for t in range(frames):
-                    a = f + taps - 1 - t
-                    if 0 <= a < taps:
-                        add(own_acc, t, jnp.dot(window, conv_ref[a, b, c], preferred_element_type=jnp.float32))
-                    a = f - t
-                    if 0 <= a < taps:
-                        add(next_acc, t, jnp.dot(window, conv_ref[a, b, c], preferred_element_type=jnp.float32))
+                window = jnp.concatenate(
+                    [moved[f][c][b * line : b * line + out_rows] for f, _, _ in targets], axis=0
+                )
+                part = lax.dot_general(
+                    window,
+                    conv_ref[a, b, c],
+                    (((1,), (1,)), ((), ())),
+                    preferred_element_type=jnp.float32,
+                )
+                total = part if total is None else total + part
+        for k, (_, acc, t) in enumerate(targets):
+            piece = total[k * out_rows : (k + 1) * out_rows]
+            acc[t] = piece if acc[t] is None else acc[t] + piece
     for t in range(frames):
         own_ref[t] = own_acc[t]
         next_ref[t] = next_acc[t].astype(next_ref.dtype)
 
 
-def fused_block(cells, query_feats, mask, w_query, w_keyval, conv_weight):
+def fused_block(first, cells, query_feats, w_query, w_keyval, conv_weight):
     frames, count, width = cells.shape
     rows = query_feats.shape[1]
     out_rows = RD * (rows // (RD + 2))
     out_width = conv_weight.shape[-1]
+    flipped = jnp.swapaxes(conv_weight, 3, 4)
 
     def whole(shape):
-        return pl.BlockSpec(shape, lambda i: (0,) * len(shape))
-
-    return pl.pallas_call(
-        block_kernel,
+        return pl.BlockSpec(shape, lambda i, first_ref: (0,) * len(shape))
+
+    grid_spec = pltpu.PrefetchScalarGridSpec(
+        num_scalar_prefetch=1,
         grid=(1,),
         in_specs=[
             whole(cells.shape),
             whole(query_feats.shape),
-            whole(mask.shape),
             whole(w_query.shape),
             whole(w_keyval.shape),
-            whole(conv_weight.shape),
+            whole(flipped.shape),
         ],
         out_specs=[
             whole((frames, out_rows, width)),
             whole((frames, out_rows, out_width)),
             whole((frames, out_rows, out_width)),
         ],
+    )
+    return pl.pallas_call(
+        block_kernel,
+        grid_spec=grid_spec,
         out_shape=[
             jax.ShapeDtypeStruct((frames, out_rows, width), jnp.bfloat16),
             jax.ShapeDtypeStruct((frames, out_rows, out_width), jnp.float32),
             jax.ShapeDtypeStruct((frames, out_rows, out_width), jnp.bfloat16),
         ],
-    )(cells, query_feats, mask, w_query, w_keyval, conv_weight)
+    )(first, cells, query_feats, w_query, w_keyval, flipped)
 
 
 def local(latent_tiles, route, w_query, w_keyval, conv_weight):
@@ -172,13 +194,11 @@
     padded = jnp.pad(whole, ((0, 0), (1, 1), (0, 0), (0, 0)))
     features = lax.dynamic_slice_in_dim(padded, patch_index * RD, RD + 2, 1)
     ext_cells = (RD + 2) * W
-    row_ids = patch_index * RD - 1 + jnp.arange(RD + 2)
-    inside = ((row_ids >= 0) & (row_ids < rows)).astype(jnp.float32)
-    mask = jnp.repeat(inside, W)[:, None]
+    first = jnp.reshape(patch_index * RD - 1, (1,)).astype(jnp.int32)
     mixed_own, own_sum, to_next = fused_block(
+        first,
         whole.reshape(FD, rows * W, C),
         features.reshape(FD, ext_cells, C),
-        mask,
         w_query,
         w_keyval,
         conv_weight,

time: 49.1 us -> 42.3 us (0.86)
  local copies, waits for them, and re-layouts: 12 us -> 2.96 us
  Pallas kernels: 9.6 us -> 12 us
    unnamed x4 -> x3, local copies, waits for them, and re-layouts: 8.45 us -> 0.31 us
    pallas_call x1, Pallas kernels: 9.6 us -> 12 us  [fused_block(): pl.pallas_call(block_kernel, grid_spec=grid_spec, out_shape=[jax.ShapeDty...]
    another operation x1 -> x0, local copies, waits for them, and re-layouts: 0.8 us -> none  [local(): mask = jnp.repeat(inside, W)[:, None]]
where the time goes in v5:
time: 42.3 us; the launch traced here: 42.1 us
  blocking collectives  17.2 us (41%)
  Pallas kernels  12 us (28%)
  waiting for transfers between devices  3.56 us (8%)
  starting transfers between devices  3.39 us (8%)
  local copies, waits for them, and re-layouts  2.96 us (7%)
  other arithmetic  2.51 us (6%)
    all_gather x1, blocking collectives, local(): lax.all_gather(own_share, ('patch', 'chan'), axis=1, tiled=True)[0]  17.2 us
    pallas_call x1, Pallas kernels, fused_block(): pl.pallas_call(block_kernel, grid_spec=grid_spec, out_shape=[jax.ShapeDty...  12 us
    ppermute x1, waiting for transfers between devices, local(): from_prev = lax.ppermute(to_next, 'span', pairs)  3.56 us
    ppermute x1, starting transfers between devices, local(): from_prev = lax.ppermute(to_next, 'span', pairs)  3.39 us
    convert_element_type x1, other arithmetic, local(): return total.reshape(FD, RD, W, out_width).astype(jnp.bfloat16)  1.77 us
    another operation x1, local copies, waits for them, and re-layouts, local(): whole.reshape(FD, rows * W, C)  1.36 us
  transfers between devices with their start and end apart: 1, of which 1 were waited for; matrix products, arithmetic and copies ran while one was open for 0% of the time, Pallas kernels for 0%

profile of v5, /device:TPU:0, one launch (start us, length us, event | category | flops | bytes accessed | tf_op | source)
XLA Modules:
  0.0 42.1 jit_solution(14940677442317049956)
XLA Ops:
  0.0 0.0 copy-start
  0.0 0.7 %fusion.1 = s32[1,256]{1,0:T(1,128)S(1)} fusion(s32[1,256]{1,0:T(1,128)} %param.6), kind=kLoop, calls=%fused_computation.15 | loop fusion | flops 10752 | bytes 2048 | tf_op jit(solution)/shard_map/add | solution.py:187
  0.7 0.2 copy-done
  1.0 17.2 %all_gather.3 = bf16[1,256,4,384]{3,2,0,1:T(4,128)(2,1)S(1)} all-gather(bf16[1,32,4,384]{3,2,0,1:T(4,128)(2,1)S(1)} %constant_dynamic-slice_fusion), channel_id=1, replica_groups=mesh['clips'=2,'patch'=4,'span'=2,'chan'=2] {'patch','chan'}, dimensions={1}, use_global_device_ids=true | all-gather | bytes 884736 | tf_op jit(solution)/shard_map/all_gather | solution.py:180
  18.2 0.1 copy.7
  18.3 0.4 convolution_convert_fusion
  18.7 0.5 %reshape.12 = bf16[2,8,64,384]{3,2,1,0:T(8,128)(2,1)S(1)} reshape(bf16[256,1536]{1,0:T(8,128)(2,1)S(1)} %convolution_convert_fusion) | data formatting | bytes 1572864 | tf_op jit(solution)/shard_map/reshape | solution.py:193
  19.2 1.4 %reshape_reshape.3.cells_ref = bf16[2,512,384]{2,1,0:T(8,128)(2,1)} reshape(bf16[256,1536]{1,0:T(8,128)(2,1)S(1)} %convolution_convert_fusion) | data formatting | bytes 1572864 | tf_op jit(solution)/shard_map/reshape;reshape | solution.py:200
  20.5 0.8 %pad_dynamic-slice_fusion = bf16[2,4,64,384]{3,2,1,0:T(8,128)(2,1)} fusion(s32[]{:T(128)S(6)} %select_n.37, bf16[2,8,64,384]{3,2,1,0:T(8,128)(2,1)S(1)} %reshape.12), kind=kLoop, calls=%fused_computation.1 | loop fusion | bytes 1179652 | tf_op jit(solution)/shard_map/dynamic_slice | solution.py:195
  21.3 12.0 %shard_map.55 = (bf16[2,128,384]{2,1,0:T(8,128)(2,1)}, f32[2,128,192]{2,1,0:T(8,128)}, bf16[2,128,192]{2,1,0:T(8,128)(2,1)}) custom-call(s32[1]{0:T(128)} %bitcast.first_ref, bf16[2,512,384]{2,1,0:T(8,128)(2,1)} %reshape_reshape.3.cells_ref, bf16[2,256,384]{2,1,0:T(8,128)(2,1)} %bitcast.15, bf16[384,384]{1,0:T(8,128)(2,1)} %wq_ref.1, ...), custom_call_target="tpu_custom_call" | custom-call | tf_op jit(solution)/shard_map/pallas_call | solution.py:159
  33.4 3.4 %collective-permute-start = (bf16[2,128,192]{2,1,0:T(8,128)(2,1)}, bf16[2,128,192]{2,1,0:T(8,128)(2,1)S(1)}, u32[]{:S(2)}, u32[]{:S(2)}) collective-permute-start(bf16[2,128,192]{2,1,0:T(8,128)(2,1)} %get-tuple-element.10), channel_id=1, source_target_pairs={{0,2},{1,3},{4,6},{5,7},{8,10},{9,11},{12,14},{13,15},{16,18},{17,... | collective-permute-start | bytes 294920 | tf_op jit(solution)/shard_map/ppermute | solution.py:207
  36.8 3.6 %collective-permute-done = bf16[2,128,192]{2,1,0:T(8,128)(2,1)S(1)} collective-permute-done((bf16[2,128,192]{2,1,0:T(8,128)(2,1)}, bf16[2,128,192]{2,1,0:T(8,128)(2,1)S(1)}, u32[]{:S(2)}, u32[]{:S(2)}) %collective-permute-start) | collective-permute-done | bytes 98336 | tf_op jit(solution)/shard_map/ppermute | solution.py:207
  40.3 1.8 %add_convert_fusion = bf16[2,128,192]{2,1,0:T(8,128)(2,1)} fusion(bf16[2,128,192]{2,1,0:T(8,128)(2,1)S(1)} %collective-permute-done, f32[2,128,192]{2,1,0:T(8,128)} %get-tuple-element.9, bf16[2,128,384]{2,1,0:T(8,128)(2,1)} %get-tuple-element.8, s32[]{:T(128)S(6)} %select_n.38), kind=kLoop, calls=%fused_computation.2 | loop fusion | flops 245760 | bytes 491524 | tf_op jit(solution)/shard_map/convert_element_type | solution.py:211
  (1 shorter events, 0.0 us)
Async XLA Ops:
  0.0 0.9 %copy-start = (bf16[1,64,4,384]{3,2,1,0:T(4,128)(2,1)S(1)}, bf16[1,64,4,384]{3,2,1,0:T(4,128)(2,1)}, u32[]{:S(2)}) copy-start(bf16[1,64,4,384]{3,2,1,0:T(4,128)(2,1)} %param.5) | copy-start | bytes 589828
  33.4 7.0 %collective-permute-start = (bf16[2,128,192]{2,1,0:T(8,128)(2,1)}, bf16[2,128,192]{2,1,0:T(8,128)(2,1)S(1)}, u32[]{:S(2)}, u32[]{:S(2)}) collective-permute-start(bf16[2,128,192]{2,1,0:T(8,128)(2,1)} %get-tuple-element.10), channel_id=1, source_target_pairs={{0,2},{1,3},{4,6},{5,7},{8,10},{9,11},{12,14},{13,15},{16,18},{17,... | collective-permute-start | bytes 294920 | tf_op jit(solution)/shard_map/ppermute | solution.py:207

commit v6 on v2

--- a/solution.py
+++ b/solution.py
@@ -84,11 +84,14 @@
     row_ids = patch_index * RD - 1 + jnp.arange(RD + 2)
     inside = ((row_ids >= 0) & (row_ids < rows))[None, :, None, None]
     activated = jnp.where(inside, jax.nn.silu(scaled_rms(mixed)), 0.0).astype(jnp.bfloat16)
-    tap_sums = [spatial_conv(activated, conv_weight[a]) for a in range(3)]
-    to_next = jnp.stack([tap_sums[0][0] + tap_sums[1][1], tap_sums[0][1]]).astype(jnp.bfloat16)
+    by_first = spatial_conv(activated, conv_weight[0])
+    by_middle = spatial_conv(activated[1:], conv_weight[1])
+    to_next = jnp.concatenate([by_first[:1] + by_middle, by_first[1:]]).astype(jnp.bfloat16)
     pairs = [(i, i + 1) for i in range(span_count - 1)]
     from_prev = lax.ppermute(to_next, "span", pairs)
-    own_sum = jnp.stack([tap_sums[2][0], tap_sums[1][0] + tap_sums[2][1]])
+    by_last = spatial_conv(activated, conv_weight[2])
+    own_middle = spatial_conv(activated[:1], conv_weight[1])
+    own_sum = jnp.concatenate([by_last[:1], own_middle + by_last[1:]])
     out_width = conv_weight.shape[-1]
     own_rows = mixed[:, 1 : RD + 1]
     own_channels = lax.dynamic_slice_in_dim(own_rows, chan_index * out_width, out_width, 3)

time: 41.8 us -> 41.5 us (level)
  waiting for transfers between devices: 3.2 us -> 1.14 us
  local copies, waits for them, and re-layouts: 4.71 us -> 5.65 us
  matrix products: 8.24 us -> 8.7 us
    ppermute x1, waiting for transfers between devices: 3.2 us -> 1.14 us  [local(): from_prev = lax.ppermute(to_next, 'span', pairs)]
    unnamed x16 -> x21, local copies, waits for them, and re-layouts: 1.74 us -> 2.5 us
    conv_general_dilated x3 -> x4, matrix products: 2.15 us -> 2.61 us  [spatial_conv(): lax.conv_general_dilated(frames, kernel, (1, 1), ((0, 0), (1, 1)), dimens...]
    conv_general_dilated x8 -> x13, local copies, waits for them, and re-layouts: 0.85 us -> 0.82 us  [spatial_conv(): lax.conv_general_dilated(frames, kernel, (1, 1), ((0, 0), (1, 1)), dimens...]
  transfers between devices with their start and end apart: 1 -> 1, of which waited for: 1 -> 1; matrix products, arithmetic and copies ran while one was open for 0% -> 5% of each run, Pallas kernels for 0% -> 0%
where the time goes in v6:
time: 41.5 us; the launch traced here: 41.3 us
  blocking collectives  17.2 us (41%)
  matrix products  8.7 us (21%)
  local copies, waits for them, and re-layouts  5.65 us (14%)
  other arithmetic  4.7 us (11%)
  starting transfers between devices  3.41 us (8%)
  waiting for transfers between devices  1.14 us (3%)
  between operations  0.43 us (1%)
    all_gather x1, blocking collectives, local(): lax.all_gather(own_share, ('patch', 'chan'), axis=1, tiled=True)[0]  17.2 us
    ppermute x1, starting transfers between devices, local(): from_prev = lax.ppermute(to_next, 'span', pairs)  3.41 us
    conv_general_dilated x4, matrix products, spatial_conv(): lax.conv_general_dilated(frames, kernel, (1, 1), ((0, 0), (1, 1)), dimens...  2.61 us
    unnamed x21, local copies, waits for them, and re-layouts  2.5 us
    dot_general x1, matrix products, local(): jnp.einsum('fnc,cd->fnd', normed_all.reshape(FD, rows * W, C), w_keyval,...  2.13 us
    dot_general x1, matrix products, attend(): jnp.einsum('fqc,fkc->fqk', queries, key_rows, preferred_element_type=jnp....  1.93 us
    dot_general x1, matrix products, attend(): jnp.einsum('fqk,fkc->fqc', weights, value_rows, preferred_element_type=jn...  1.65 us
    reshape x1, other arithmetic, local(): placed = placed.reshape(patch_count, FD, RD, W, C)  1.39 us
  transfers between devices with their start and end apart: 1, of which 1 were waited for; matrix products, arithmetic and copies ran while one was open for 5% of the time, Pallas kernels for 0%

profile of v6, /device:TPU:0, one launch (start us, length us, event | category | flops | bytes accessed | tf_op | source)
XLA Modules:
  0.0 41.3 jit_solution(17983313363802852854)
XLA Ops:
  0.0 1.0 %constant_dynamic-slice_fusion = bf16[1,32,4,384]{3,2,0,1:T(4,128)(2,1)S(1)} fusion(bf16[1,64,4,384]{3,2,0,1:T(4,128)(2,1)} %bitcast.114, s32[]{:T(128)S(6)} %select_n.13), kind=kLoop, calls=%fused_computation.87 | loop fusion | bytes 196612 | tf_op jit(solution)/shard_map/dynamic_slice | solution.py:55
  1.0 17.2 %all_gather.3 = bf16[1,256,4,384]{3,2,0,1:T(4,128)(2,1)S(1)} all-gather(bf16[1,32,4,384]{3,2,0,1:T(4,128)(2,1)S(1)} %constant_dynamic-slice_fusion), channel_id=1, replica_groups=mesh['clips'=2,'patch'=4,'span'=2,'chan'=2] {'patch','chan'}, dimensions={1}, use_global_device_ids=true | all-gather | bytes 884736 | tf_op jit(solution)/shard_map/all_gather | solution.py:56
  18.4 0.4 convolution_convert_fusion
  18.7 0.5 %reshape.60 = bf16[4,2,2,64,384]{4,3,2,1,0:T(8,128)(2,1)S(1)} reshape(bf16[256,1536]{1,0:T(8,128)(2,1)S(1)} %convolution_convert_fusion) | data formatting | bytes 1572864 | tf_op jit(solution)/shard_map/reshape | solution.py:64
  19.4 1.4 %fusion.72 = (bf16[4,2,2,64,384]{4,3,2,0,1:T(8,128)(2,1)S(1)}, f32[2,4,2,64,384]{4,3,2,1,0:T(8,128)}) fusion(bf16[4,2,2,64,384]{4,3,2,1,0:T(8,128)(2,1)S(1)} %reshape.60), kind=kLoop, calls=%fused_computation.94 | loop fusion | flops 393216 | bytes 3145728 | tf_op jit(solution)/shard_map/reshape | solution.py:64
  21.3 0.9 %copy-done.1 = f32[2,4,2,64,384]{4,3,2,1,0:T(8,128)S(1)} copy-done((f32[2,4,2,64,384]{4,3,2,1,0:T(8,128)S(1)}, f32[2,4,2,64,384]{4,3,2,1,0:T(8,128)}, u32[]{:S(2)}) %copy-start.1) | copy-done | bytes 1572888
  22.5 2.1 %convolution_convert_fusion.1 = bf16[2,512,768]{2,1,0:T(8,128)(2,1)} fusion(bf16[2,512,384]{2,1,0:T(8,128)(2,1)S(1)} %fusion, bf16[384,768]{1,0:T(8,128)(2,1)S(1)} %copy-done), kind=kOutput, calls=%fused_computation.2 | convolution fusion | flops 604766208 | bytes 2949120 | tf_op jit(solution)/shard_map/fnc,cd->fnd/dot_general | solution.py:74
  24.6 1.9 %fusion.74 = (f32[2,256]{1,0:T(2,128)S(1)}, f32[2,256,512]{2,1,0:T(8,128)S(1)}) fusion(bf16[2,512,768]{2,1,0:T(8,128)(2,1)} %convolution_convert_fusion.1, bf16[2,256,384]{2,1,0:T(8,128)(2,1)S(1)} %bitcast.112, bf16[384,384]{1,0:T(8,128)(2,1)S(1)} %copy-done.4), kind=kOutput, calls=%fused_computation.96 | convolution fusion | flops 353041920 | bytes 2525184 | tf_op jit(solution)/shard_map/fqc,fkc->fqk/dot_general | solution.py:25
  26.5 0.3 fusion.25
  26.9 1.6 %convolution_divide_fusion = f32[2,256,384]{2,1,0:T(8,128)S(1)} fusion(bf16[2,512,768]{2,1,0:T(8,128)(2,1)} %convolution_convert_fusion.1, f32[2,256,512]{2,1,0:T(8,128)S(1)} %get-tuple-element.14, f32[2,256]{1,0:T(2,128)S(1)} %get-tuple-element.13, f32[2,256]{1,0:T(2,128)S(1)} %fusion.25), kind=kOutput, calls=%fused_computation.17 | convolution fusion | flops 202047488 | bytes 2625536 | tf_op jit(solution)/shard_map/fqk,fkc->fqc/dot_general | solution.py:31
  28.8 0.3 fusion.81
  29.1 0.3 select_convert_fusion
  29.5 0.4 copy.116
  30.2 0.7 %copy-done.3 = bf16[3,3,3,384,192]{3,4,2,1,0:T(8,128)(2,1)S(1)} copy-done((bf16[3,3,3,384,192]{3,4,2,1,0:T(8,128)(2,1)S(1)}, bf16[3,3,3,384,192]{3,4,2,1,0:T(8,128)(2,1)}, u32[]{:S(2)}) %copy-start.3) | copy-done | bytes 3981336
  30.9 0.6 %fusion.22 = f32[2,8,9,192]{3,1,2,0:T(8,128)S(1)} fusion(bf16[3,3,3,384,192]{3,4,2,1,0:T(8,128)(2,1)S(1)} %copy-done.3, bf16[4,1,7,2,384]{4,2,3,0,1:T(8,128)(2,1)S(1)} %slice.72, bf16[4,1,8,9,384]{4,2,3,0,1:T(8,128)(2,1)S(1)} %copy.105, pred[8,9]{0,1:T(8,128)(4,1)S(1)} %copy-done.5), kind=kOutput, calls=%fused_computation.27 | convolution fusion | flops 191941632 | bytes 1710080 | tf_op jit(solution)/shard_map/conv_general_dilated | solution.py:36
  31.6 0.3 pad.5.clone
  32.0 0.5 %fusion.34 = bf16[4,2,8,11,384]{4,1,3,2,0:T(2,128)(2,1)S(1)} fusion(bf16[4,2,7,2,384]{4,1,3,2,0:T(2,128)(2,1)S(1)} %slice.62, bf16[4,2,8,9,384]{4,1,3,2,0:T(2,128)(2,1)S(1)} %bitcast.101), kind=kLoop, calls=%fused_computation.43 | loop fusion | flops 1622016 | bytes 1069056 | tf_op jit(solution)/shard_map/conv_general_dilated | solution.py:36
  32.5 0.7 %fusion.77 = (bf16[2,16,9,192]{3,1,2,0:T(8,128)(2,1)S(1)}, f32[2,16,9,192]{3,1,2,0:T(8,128)S(1)}) fusion(bf16[3,3,3,384,192]{3,4,2,1,0:T(8,128)(2,1)S(1)} %copy-done.3, bf16[4,2,8,11,384]{4,1,3,2,0:T(2,128)(2,1)S(1)} %fusion.34, pred[16,9]{0,1:T(8,128)(4,1)S(1)} %copy-done.6), kind=kOutput, calls=%fused_computation.97 | convolution fusion | flops 382316544 | bytes 2201600 | tf_op jit(solution)/shard_map/conv_general_dilated | solution.py:36
  33.5 0.2 copy.101
  33.8 3.4 %collective-permute-start = (bf16[2,2,64,192]{3,2,1,0:T(8,128)(2,1)S(1)}, bf16[2,2,64,192]{3,2,1,0:T(8,128)(2,1)S(1)}, u32[]{:S(2)}, u32[]{:S(2)}) collective-permute-start(bf16[2,2,64,192]{3,2,1,0:T(8,128)(2,1)S(1)} %pad_maximum_fusion), channel_id=1, source_target_pairs={{0,2},{1,3},{4,6},{5,7},{8,10},{9,11},{12,14},{13,15},{16,18},{17,... | collective-permute-start | bytes 294920 | tf_op jit(solution)/shard_map/ppermute | solution.py:91
  37.3 0.7 %fusion.11 = f32[2,16,9,192]{3,1,2,0:T(8,128)S(1)} fusion(bf16[3,3,3,384,192]{3,4,2,1,0:T(8,128)(2,1)S(1)} %copy-done.3, bf16[4,2,8,11,384]{4,1,3,2,0:T(2,128)(2,1)S(1)} %fusion.34, pred[16,9]{0,1:T(8,128)(4,1)S(1)} %copy-done.6), kind=kOutput, calls=%fused_computation.22 | convolution fusion | flops 382261248 | bytes 2091008 | tf_op jit(solution)/shard_map/conv_general_dilated | solution.py:36
  38.3 0.6 %fusion.19 = f32[2,8,9,192]{3,1,2,0:T(8,128)S(1)} fusion(bf16[3,3,3,384,192]{3,4,2,1,0:T(8,128)(2,1)S(1)} %copy-done.3, bf16[4,1,7,2,384]{4,2,3,0,1:T(8,128)(2,1)S(1)} %slice.66, bf16[4,1,8,9,384]{4,2,3,0,1:T(8,128)(2,1)S(1)} %copy.98, pred[8,9]{0,1:T(8,128)(4,1)S(1)} %copy-done.5), kind=kOutput, calls=%fused_computation.26 | convolution fusion | flops 191941632 | bytes 1710080 | tf_op jit(solution)/shard_map/conv_general_dilated | solution.py:36
  39.4 1.1 %collective-permute-done = bf16[2,2,64,192]{3,2,1,0:T(8,128)(2,1)S(1)} collective-permute-done((bf16[2,2,64,192]{3,2,1,0:T(8,128)(2,1)S(1)}, bf16[2,2,64,192]{3,2,1,0:T(8,128)(2,1)S(1)}, u32[]{:S(2)}, u32[]{:S(2)}) %collective-permute-start) | collective-permute-done | bytes 98336 | tf_op jit(solution)/shard_map/ppermute | solution.py:91
  40.5 0.8 %fusion.58 = bf16[2,2,64,192]{3,2,1,0:T(8,128)(2,1)} fusion(f32[1,2,64,192]{3,2,1,0:T(8,128)S(1)} %get-tuple-element.12, f32[1,2,64,192]{3,2,1,0:T(8,128)S(1)} %get-tuple-element.11, bf16[2,2,64,192]{3,2,1,0:T(8,128)(2,1)S(1)} %collective-permute-done, bf16[2,2,64,384]{3,2,1,0:T(8,128)(2,1)S(1)} %slice.61, s32[]{:T(128)S(6)} %select_n.15), kind=kLoop, calls=%fused_computation.65 | loop fusion | flops 294912 | bytes 491524 | tf_op jit(solution)/shard_map/convert_element_type | solution.py:98
  (51 shorter events, 2.7 us)
Async XLA Ops:
  0.0 22.5 %copy-start = (bf16[384,768]{1,0:T(8,128)(2,1)S(1)}, bf16[384,768]{1,0:T(8,128)(2,1)}, u32[]{:S(2)}) copy-start(bf16[384,768]{1,0:T(8,128)(2,1)} %param.8) | copy-start | bytes 1769476
  0.0 18.4 %copy-start.2 = (s32[1,256]{1,0:T(1,128)S(1)}, s32[1,256]{1,0:T(1,128)}, u32[]{:S(2)}) copy-start(s32[1,256]{1,0:T(1,128)} %param.6) | copy-start | bytes 3076
  20.8 1.4 %copy-start.1 = (f32[2,4,2,64,384]{4,3,2,1,0:T(8,128)S(1)}, f32[2,4,2,64,384]{4,3,2,1,0:T(8,128)}, u32[]{:S(2)}) copy-start(f32[2,4,2,64,384]{4,3,2,1,0:T(8,128)} %get-tuple-element.8) | copy-start | bytes 4718596
  22.5 2.1 %copy-start.4 = (bf16[384,384]{1,0:T(8,128)(2,1)S(1)}, bf16[384,384]{1,0:T(8,128)(2,1)}, u32[]{:S(2)}) copy-start(bf16[384,384]{1,0:T(8,128)(2,1)} %param.7) | copy-start | bytes 884740
  28.8 2.1 %copy-start.3 = (bf16[3,3,3,384,192]{3,4,2,1,0:T(8,128)(2,1)S(1)}, bf16[3,3,3,384,192]{3,4,2,1,0:T(8,128)(2,1)}, u32[]{:S(2)}) copy-start(bf16[3,3,3,384,192]{3,4,2,1,0:T(8,128)(2,1)} %param.9) | copy-start | bytes 11943940
  29.4 1.4 %copy-start.5 = (pred[8,9]{0,1:T(8,128)(4,1)S(1)}, pred[8,9]{0,1:T(8,128)(4,1)}, u32[]{:S(2)}) copy-start(pred[8,9]{0,1:T(8,128)(4,1)} %constant.70) | copy-start | bytes 220
  31.5 1.0 %copy-start.6 = (pred[16,9]{0,1:T(8,128)(4,1)S(1)}, pred[16,9]{0,1:T(8,128)(4,1)}, u32[]{:S(2)}) copy-start(pred[16,9]{0,1:T(8,128)(4,1)} %constant.69) | copy-start | bytes 436
  33.8 6.7 %collective-permute-start = (bf16[2,2,64,192]{3,2,1,0:T(8,128)(2,1)S(1)}, bf16[2,2,64,192]{3,2,1,0:T(8,128)(2,1)S(1)}, u32[]{:S(2)}, u32[]{:S(2)}) collective-permute-start(bf16[2,2,64,192]{3,2,1,0:T(8,128)(2,1)S(1)} %pad_maximum_fusion), channel_id=1, source_target_pairs={{0,2},{1,3},{4,6},{5,7},{8,10},{9,11},{12,14},{13,15},{16,18},{17,... | collective-permute-start | bytes 294920 | tf_op jit(solution)/shard_map/ppermute | solution.py:91

commit v7 on v3

--- a/solution.py
+++ b/solution.py
@@ -1,10 +1,10 @@
-import functools
 import math
 
 import jax
 import jax.numpy as jnp
 from jax import lax
 from jax.experimental import pallas as pl
+from jax.experimental.pallas import tpu as pltpu
 from jax.sharding import PartitionSpec as P
 
 C = 384
@@ -22,14 +22,27 @@
     return wide / jnp.sqrt(jnp.mean(wide * wide, axis=-1, keepdims=True) + epsilon)
 
 
-def attention_kernel(cells_ref, query_ref, mask_ref, wq_ref, wkv_ref, mixed_ref, act_ref):
+def attention_kernel(first_ref, cells_ref, wq_ref, wkv_ref, mixed_ref, act_ref):
     width = wq_ref.shape[0]
     scale = 1.0 / math.sqrt(width)
-    feats = query_ref[0].astype(jnp.float32)
+    count = cells_ref.shape[1]
+    own = mixed_ref.shape[1]
+    line = (act_ref.shape[1] - own) // 2
+    frame_rows = count // line
+    first = first_ref[0]
+    top = jnp.maximum(first, 0) * line
+    below = jnp.minimum(first + 1 + own // line, frame_rows - 1) * line
+    feats = jnp.concatenate(
+        [
+            cells_ref[0, pl.ds(top, line), :],
+            cells_ref[0, pl.ds((first + 1) * line, own), :],
+            cells_ref[0, pl.ds(below, line), :],
+        ],
+        axis=0,
+    ).astype(jnp.float32)
     queries = jnp.dot(
         scaled_rms(feats).astype(jnp.bfloat16), wq_ref[...], preferred_element_type=jnp.float32
     ).astype(jnp.bfloat16)
-    count = cells_ref.shape[1]
     block = min(count, KEY_BLOCK)
 
     def fold(step, carry):
@@ -62,38 +75,43 @@
         jnp.zeros((rows, 1), jnp.float32),
         jnp.zeros((rows, width), jnp.float32),
     )
-    steps = count // block
-    if steps == 1:
-        carry = fold(0, carry)
-    else:
-        carry = lax.fori_loop(0, steps, fold, carry)
+    for step in range(count // block):
+        carry = fold(step, carry)
     _, run_total, run_acc = carry
     mixed = (feats + run_acc / run_total).astype(jnp.bfloat16)
-    mixed_ref[0] = mixed
+    mixed_ref[0] = mixed[line : line + own]
     normed = scaled_rms(mixed)
-    act_ref[0] = (normed / (1.0 + jnp.exp(-normed)) * mask_ref[...]).astype(jnp.bfloat16)
+    row_of = lax.broadcasted_iota(jnp.int32, (rows, width), 0) // line + first
+    inside = (row_of >= 0) & (row_of < frame_rows)
+    act_ref[0] = jnp.where(inside, normed / (1.0 + jnp.exp(-normed)), 0.0).astype(jnp.bfloat16)
 
 
-def attend_frames(cells, query_feats, mask, w_query, w_keyval):
+def attend_frames(first, cells, ext_rows, w_query, w_keyval):
     frames, count, width = cells.shape
-    rows = query_feats.shape[1]
-    out = jax.ShapeDtypeStruct((frames, rows, width), jnp.bfloat16)
+    own = ext_rows - 2 * (ext_rows // (RD + 2))
+    fixed = lambda f, first_ref: (0, 0)
+    per_frame = lambda f, first_ref: (f, 0, 0)
+    grid_spec = pltpu.PrefetchScalarGridSpec(
+        num_scalar_prefetch=1,
+        grid=(frames,),
+        in_specs=[
+            pl.BlockSpec((1, count, width), per_frame),
+            pl.BlockSpec(w_query.shape, fixed),
+            pl.BlockSpec(w_keyval.shape, fixed),
+        ],
+        out_specs=[
+            pl.BlockSpec((1, own, width), per_frame),
+            pl.BlockSpec((1, ext_rows, width), per_frame),
+        ],
+    )
     return pl.pallas_call(
         attention_kernel,
-        grid=(frames,),
-        in_specs=[
-            pl.BlockSpec((1, count, width), lambda f: (f, 0, 0)),
-            pl.BlockSpec((1, rows, width), lambda f: (f, 0, 0)),
-            pl.BlockSpec((rows, 1), lambda f: (0, 0)),
-            pl.BlockSpec(w_query.shape, lambda f: (0, 0)),
-            pl.BlockSpec(w_keyval.shape, lambda f: (0, 0)),
+        grid_spec=grid_spec,
+        out_shape=[
+            jax.ShapeDtypeStruct((frames, own, width), jnp.bfloat16),
+            jax.ShapeDtypeStruct((frames, ext_rows, width), jnp.bfloat16),
         ],
-        out_specs=[
-            pl.BlockSpec((1, rows, width), lambda f: (f, 0, 0)),
-            pl.BlockSpec((1, rows, width), lambda f: (f, 0, 0)),
-        ],
-        out_shape=[out, out],
-    )(cells, query_feats, mask, w_query, w_keyval)
+    )(first, cells, w_query, w_keyval)
 
 
 def spatial_conv(frames, kernel):
@@ -131,28 +149,21 @@
         one_hot, every_tile.reshape(tile_total, -1), preferred_element_type=jnp.float32
     ).astype(jnp.bfloat16)
     whole = placed.reshape(FD, rows, W, C)
-    padded = jnp.pad(whole, ((0, 0), (1, 1), (0, 0), (0, 0)))
-    features = lax.dynamic_slice_in_dim(padded, patch_index * RD, RD + 2, 1)
-    ext_cells = (RD + 2) * W
-    row_ids = patch_index * RD - 1 + jnp.arange(RD + 2)
-    inside = ((row_ids >= 0) & (row_ids < rows)).astype(jnp.float32)
-    mask = jnp.repeat(inside, W)[:, None]
-    mixed, activated = attend_frames(
-        whole.reshape(FD, rows * W, C),
-        features.reshape(FD, ext_cells, C),
-        mask,
-        w_query,
-        w_keyval,
+    first = jnp.reshape(patch_index * RD - 1, (1,)).astype(jnp.int32)
+    mixed_own, activated = attend_frames(
+        first, whole.reshape(FD, rows * W, C), (RD + 2) * W, w_query, w_keyval
     )
-    mixed = mixed.reshape(FD, RD + 2, W, C)
     activated = activated.reshape(FD, RD + 2, W, C)
-    tap_sums = [spatial_conv(activated, conv_weight[a]) for a in range(3)]
-    to_next = jnp.stack([tap_sums[0][0] + tap_sums[1][1], tap_sums[0][1]]).astype(jnp.bfloat16)
+    by_first = spatial_conv(activated, conv_weight[0])
+    by_middle = spatial_conv(activated[1:], conv_weight[1])
+    to_next = jnp.concatenate([by_first[:1] + by_middle, by_first[1:]]).astype(jnp.bfloat16)
     pairs = [(i, i + 1) for i in range(span_count - 1)]
     from_prev = lax.ppermute(to_next, "span", pairs)
-    own_sum = jnp.stack([tap_sums[2][0], tap_sums[1][0] + tap_sums[2][1]])
+    by_last = spatial_conv(activated, conv_weight[2])
+    own_middle = spatial_conv(activated[:1], conv_weight[1])
+    own_sum = jnp.concatenate([by_last[:1], own_middle + by_last[1:]])
     out_width = conv_weight.shape[-1]
-    own_rows = mixed[:, 1 : RD + 1]
+    own_rows = mixed_own.reshape(FD, RD, W, C)
     own_channels = lax.dynamic_slice_in_dim(own_rows, chan_index * out_width, out_width, 3)
     total = own_channels.astype(jnp.float32) + own_sum + from_prev.astype(jnp.float32)
     return total.astype(jnp.bfloat16)

time: 42.5 us -> 40.3 us (0.948)
  waiting for transfers between devices: 3.19 us -> 1.15 us
  other arithmetic: 2.06 us -> 1.34 us
  matrix products: 4 us -> 4.47 us
    ppermute x1, waiting for transfers between devices: 3.19 us -> 1.15 us  [local(): from_prev = lax.ppermute(to_next, 'span', pairs)]
    slice x2 -> x6, local copies, waits for them, and re-layouts: 0.03 us -> 1.54 us  [the longest x3 1.3 us: local(): by_middle = spatial_conv(activated[1:], conv_weight[1])]
    dynamic_slice x1 -> x0, local copies, waits for them, and re-layouts: 0.82 us -> none  [local(): features = lax.dynamic_slice_in_dim(padded, patch_index * RD, RD + 2, 1)]
    another operation x3 -> x2, local copies, waits for them, and re-layouts: 1.01 us -> 0.21 us  [the longest x1 0.8 us: local(): mask = jnp.repeat(inside, W)[:, None]]
    unnamed x11 -> x16, local copies, waits for them, and re-layouts: 0.67 us -> 1.41 us
    add x1, other arithmetic: 0.74 us -> 0.02 us  [local(): spot // per_frame * (tile_total // FD) + owner * per_frame]
    conv_general_dilated x3 -> x4, matrix products: 3.63 us -> 4.1 us  [spatial_conv(): lax.conv_general_dilated(frames, kernel, (1, 1), ((0, 0), (1, 1)), dimens...]
    reshape x1 -> x0, local copies, waits for them, and re-layouts: 0.47 us -> none  [local(): whole = placed.reshape(FD, rows, W, C)]
  transfers between devices with their start and end apart: 1 -> 1, of which waited for: 1 -> 1; matrix products, arithmetic and copies ran while one was open for 0% -> 5% of each run, Pallas kernels for 0% -> 0%
where the time goes in v7:
time: 40.3 us; the launch traced here: 40 us
  blocking collectives  17.2 us (43%)
  local copies, waits for them, and re-layouts  7.09 us (18%)
  Pallas kernels  5.02 us (12%)
  matrix products  4.47 us (11%)
  starting transfers between devices  3.4 us (8%)
  other arithmetic  1.34 us (3%)
  waiting for transfers between devices  1.15 us (3%)
    all_gather x1, blocking collectives, local(): lax.all_gather(own_share, ('patch', 'chan'), axis=1, tiled=True)[0]  17.2 us
    pallas_call x1, Pallas kernels, attend_frames(): pl.pallas_call(attention_kernel, grid_spec=grid_spec, out_shape=[jax.Shap...  5.02 us
    conv_general_dilated x4, matrix products, spatial_conv(): lax.conv_general_dilated(frames, kernel, (1, 1), ((0, 0), (1, 1)), dimens...  4.1 us
    ppermute x1, starting transfers between devices, local(): from_prev = lax.ppermute(to_next, 'span', pairs)  3.4 us
    reshape x2, local copies, waits for them, and re-layouts, local(): activated = activated.reshape(FD, RD + 2, W, C)  1.73 us
    unnamed x16, local copies, waits for them, and re-layouts  1.41 us
    another operation x1, local copies, waits for them, and re-layouts, local(): whole.reshape(FD, rows * W, C)  1.34 us
    slice x3, local copies, waits for them, and re-layouts, local(): by_middle = spatial_conv(activated[1:], conv_weight[1])  1.3 us
  transfers between devices with their start and end apart: 1, of which 1 were waited for; matrix products, arithmetic and copies ran while one was open for 5% of the time, Pallas kernels for 0%

profile of v7, /device:TPU:0, one launch (start us, length us, event | category | flops | bytes accessed | tf_op | source)
XLA Modules:
  0.0 40.0 jit_solution(5582434886552354587)
XLA Ops:
  0.0 0.9 %copy-done = bf16[1,64,4,384]{3,2,1,0:T(4,128)(2,1)S(1)} copy-done((bf16[1,64,4,384]{3,2,1,0:T(4,128)(2,1)S(1)}, bf16[1,64,4,384]{3,2,1,0:T(4,128)(2,1)}, u32[]{:S(2)}) %copy-start) | copy-done | bytes 196632
  1.0 17.2 %all_gather.3 = bf16[1,256,4,384]{3,2,0,1:T(4,128)(2,1)S(1)} all-gather(bf16[1,32,4,384]{3,2,0,1:T(4,128)(2,1)S(1)} %constant_dynamic-slice_fusion), channel_id=1, replica_groups=mesh['clips'=2,'patch'=4,'span'=2,'chan'=2] {'patch','chan'}, dimensions={1}, use_global_device_ids=true | all-gather | bytes 884736 | tf_op jit(solution)/shard_map/all_gather | solution.py:138
  18.2 0.1 copy.63
  18.3 0.4 convolution_convert_fusion
  18.7 1.3 %reshape_reshape.3.cells_ref = bf16[2,512,384]{2,1,0:T(8,128)(2,1)} reshape(bf16[256,1536]{1,0:T(8,128)(2,1)S(1)} %convolution_convert_fusion) | data formatting | bytes 1572864 | tf_op jit(solution)/shard_map/reshape;reshape | solution.py:154
  20.1 5.0 %shard_map.55 = (bf16[2,128,384]{2,1,0:T(8,128)(2,1)}, bf16[2,256,384]{2,1,0:T(8,128)(2,1)}) custom-call(s32[1]{0:T(128)} %bitcast.first_ref, bf16[2,512,384]{2,1,0:T(8,128)(2,1)} %reshape_reshape.3.cells_ref, bf16[384,384]{1,0:T(8,128)(2,1)} %wq_ref.1, bf16[384,768]{1,0:T(8,128)(2,1)} %wkv_ref.1), custom_call_target="tpu_custom_call" | custom-call | tf_op jit(solution)/shard_map/pallas_call | solution.py:107
  25.1 1.1 %fusion.56 = (bf16[1,256,384]{2,1,0:T(8,128)(2,1)S(1)}, bf16[1,256,384]{2,1,0:T(8,128)(2,1)S(1)}) fusion(bf16[2,256,384]{2,1,0:T(8,128)(2,1)} %get-tuple-element.8), kind=kLoop, calls=%fused_computation.71 | loop fusion | bytes 786432 | tf_op jit(solution)/shard_map/slice | solution.py:158
  26.2 1.4 %copy.84 = bf16[2,4,64,384]{3,0,2,1:T(2,128)(2,1)S(1)} copy(bf16[2,4,64,384]{3,2,1,0:T(8,128)(2,1)} %bitcast.79) | data formatting | bytes 786432 | tf_op jit(solution)/shard_map/reshape | solution.py:156
  27.6 0.3 pad
  28.0 0.5 %fusion.24 = bf16[4,2,8,11,384]{4,1,3,2,0:T(2,128)(2,1)S(1)} fusion(bf16[4,2,7,2,384]{4,1,3,2,0:T(2,128)(2,1)S(1)} %slice.55, bf16[4,2,8,9,384]{4,1,3,2,0:T(2,128)(2,1)S(1)} %bitcast.78), kind=kLoop, calls=%fused_computation.18 | loop fusion | flops 1622016 | bytes 1069056 | tf_op jit(solution)/shard_map/conv_general_dilated | solution.py:118
  28.5 2.2 %fusion.58 = (bf16[2,16,9,192]{3,1,2,0:T(8,128)(2,1)S(1)}, f32[2,16,9,192]{3,1,2,0:T(8,128)S(1)}) fusion(bf16[3,3,3,384,192]{3,4,2,1,0:T(8,128)(2,1)} %param.9, bf16[4,2,8,11,384]{4,1,3,2,0:T(2,128)(2,1)S(1)} %fusion.24, pred[16,9]{0,1:T(8,128)(4,1)S(1)} %copy-done.5), kind=kOutput, calls=%fused_computation.73 | convolution fusion | flops 382316544 | bytes 2199696 | tf_op jit(solution)/shard_map/conv_general_dilated | solution.py:118
  30.7 0.1 copy.56
  30.8 0.1 slice.65
  31.0 0.2 copy.49
  31.3 0.2 copy.51
  31.6 0.3 copy-done.4
  31.9 0.6 %fusion.21 = f32[2,8,9,192]{3,1,2,0:T(8,128)S(1)} fusion(bf16[3,3,3,384,192]{3,4,2,1,0:T(8,128)(2,1)S(1)} %copy-done.3, bf16[4,1,7,2,384]{4,2,3,0,1:T(8,128)(2,1)S(1)} %slice.63, bf16[4,1,8,9,384]{4,2,3,0,1:T(8,128)(2,1)S(1)} %copy.53, pred[8,9]{0,1:T(8,128)(4,1)S(1)} %copy-done.4), kind=kOutput, calls=%fused_computation.17 | convolution fusion | flops 191941632 | bytes 1710080 | tf_op jit(solution)/shard_map/conv_general_dilated | solution.py:118
  32.6 3.4 %collective-permute-start = (bf16[2,2,64,192]{3,2,1,0:T(8,128)(2,1)S(1)}, bf16[2,2,64,192]{3,2,1,0:T(8,128)(2,1)S(1)}, u32[]{:S(2)}, u32[]{:S(2)}) collective-permute-start(bf16[2,2,64,192]{3,2,1,0:T(8,128)(2,1)S(1)} %pad_maximum_fusion), channel_id=1, source_target_pairs={{0,2},{1,3},{4,6},{5,7},{8,10},{9,11},{12,14},{13,15},{16,18},{17,... | collective-permute-start | bytes 294920 | tf_op jit(solution)/shard_map/ppermute | solution.py:161
  36.0 0.7 %fusion.10 = f32[2,16,9,192]{3,1,2,0:T(8,128)S(1)} fusion(bf16[3,3,3,384,192]{3,4,2,1,0:T(8,128)(2,1)S(1)} %copy-done.3, bf16[4,2,8,11,384]{4,1,3,2,0:T(2,128)(2,1)S(1)} %fusion.24, pred[16,9]{0,1:T(8,128)(4,1)S(1)} %copy-done.5), kind=kOutput, calls=%fused_computation.12 | convolution fusion | flops 382261248 | bytes 2091008 | tf_op jit(solution)/shard_map/conv_general_dilated | solution.py:118
  36.8 0.2 copy.42
  37.1 0.2 copy.44
  37.4 0.6 %fusion.18 = f32[2,8,9,192]{3,1,2,0:T(8,128)S(1)} fusion(bf16[3,3,3,384,192]{3,4,2,1,0:T(8,128)(2,1)S(1)} %copy-done.3, bf16[4,1,7,2,384]{4,2,3,0,1:T(8,128)(2,1)S(1)} %slice.58, bf16[4,1,8,9,384]{4,2,3,0,1:T(8,128)(2,1)S(1)} %copy.46, pred[8,9]{0,1:T(8,128)(4,1)S(1)} %copy-done.4), kind=kOutput, calls=%fused_computation.16 | convolution fusion | flops 191941632 | bytes 1710080 | tf_op jit(solution)/shard_map/conv_general_dilated | solution.py:118
  38.1 1.2 %collective-permute-done = bf16[2,2,64,192]{3,2,1,0:T(8,128)(2,1)S(1)} collective-permute-done((bf16[2,2,64,192]{3,2,1,0:T(8,128)(2,1)S(1)}, bf16[2,2,64,192]{3,2,1,0:T(8,128)(2,1)S(1)}, u32[]{:S(2)}, u32[]{:S(2)}) %collective-permute-start) | collective-permute-done | bytes 98336 | tf_op jit(solution)/shard_map/ppermute | solution.py:161
  39.3 0.8 %fusion.44 = bf16[2,2,64,192]{3,2,1,0:T(8,128)(2,1)} fusion(f32[1,2,64,192]{3,2,1,0:T(8,128)S(1)} %get-tuple-element.12, f32[1,2,64,192]{3,2,1,0:T(8,128)S(1)} %get-tuple-element.11, bf16[2,2,64,192]{3,2,1,0:T(8,128)(2,1)S(1)} %collective-permute-done, bf16[2,2,64,384]{3,2,1,0:T(8,128)(2,1)S(1)} %bitcast.93, s32[]{:T(128)S(6)} %select_n.34), kind=kLoop, calls=%fused_computation.39 | loop fusion | flops 294912 | bytes 491524 | tf_op jit(solution)/shard_map/convert_element_type | solution.py:169
  (32 shorter events, 0.7 us)
Async XLA Ops:
  0.0 0.9 %copy-start = (bf16[1,64,4,384]{3,2,1,0:T(4,128)(2,1)S(1)}, bf16[1,64,4,384]{3,2,1,0:T(4,128)(2,1)}, u32[]{:S(2)}) copy-start(bf16[1,64,4,384]{3,2,1,0:T(4,128)(2,1)} %param.5) | copy-start | bytes 589828
  0.9 17.4 %copy-start.2 = (s32[1,256]{1,0:T(1,128)S(1)}, s32[1,256]{1,0:T(1,128)}, u32[]{:S(2)}) copy-start(s32[1,256]{1,0:T(1,128)} %param.6) | copy-start | bytes 3076
  26.2 2.3 %copy-start.5 = (pred[16,9]{0,1:T(8,128)(4,1)S(1)}, pred[16,9]{0,1:T(8,128)(4,1)}, u32[]{:S(2)}) copy-start(pred[16,9]{0,1:T(8,128)(4,1)} %constant.87) | copy-start | bytes 436
  28.5 3.1 %copy-start.3 = (bf16[3,3,3,384,192]{3,4,2,1,0:T(8,128)(2,1)S(1)}, bf16[3,3,3,384,192]{3,4,2,1,0:T(8,128)(2,1)}, u32[]{:S(2)}) copy-start(bf16[3,3,3,384,192]{3,4,2,1,0:T(8,128)(2,1)} %param.9) | copy-start | bytes 11943940
  31.2 0.7 %copy-start.4 = (pred[8,9]{0,1:T(8,128)(4,1)S(1)}, pred[8,9]{0,1:T(8,128)(4,1)}, u32[]{:S(2)}) copy-start(pred[8,9]{0,1:T(8,128)(4,1)} %constant.88) | copy-start | bytes 220
  32.6 6.6 %collective-permute-start = (bf16[2,2,64,192]{3,2,1,0:T(8,128)(2,1)S(1)}, bf16[2,2,64,192]{3,2,1,0:T(8,128)(2,1)S(1)}, u32[]{:S(2)}, u32[]{:S(2)}) collective-permute-start(bf16[2,2,64,192]{3,2,1,0:T(8,128)(2,1)S(1)} %pad_maximum_fusion), channel_id=1, source_target_pairs={{0,2},{1,3},{4,6},{5,7},{8,10},{9,11},{12,14},{13,15},{16,18},{17,... | collective-permute-start | bytes 294920 | tf_op jit(solution)/shard_map/ppermute | solution.py:161
  37.4 1.9 %copy-start.1 = (bf16[2,128,384]{2,1,0:T(8,128)(2,1)S(1)}, bf16[2,128,384]{2,1,0:T(8,128)(2,1)}, u32[]{:S(2)}) copy-start(bf16[2,128,384]{2,1,0:T(8,128)(2,1)} %get-tuple-element.7) | copy-start | bytes 589828

commit v8 on v7

--- a/solution.py
+++ b/solution.py
@@ -114,15 +114,15 @@
     )(first, cells, w_query, w_keyval)
 
 
-def spatial_conv(frames, kernel):
+def timed_conv(frames, kernel, time_pad):
     return lax.conv_general_dilated(
-        frames,
+        frames[None],
         kernel,
-        (1, 1),
-        ((0, 0), (1, 1)),
-        dimension_numbers=("NHWC", "HWIO", "NHWC"),
+        (1, 1, 1),
+        (time_pad, (0, 0), (1, 1)),
+        dimension_numbers=("NDHWC", "DHWIO", "NDHWC"),
         preferred_element_type=jnp.float32,
-    )
+    )[0]
 
 
 def local(latent_tiles, route, w_query, w_keyval, conv_weight):
@@ -154,14 +154,10 @@
         first, whole.reshape(FD, rows * W, C), (RD + 2) * W, w_query, w_keyval
     )
     activated = activated.reshape(FD, RD + 2, W, C)
-    by_first = spatial_conv(activated, conv_weight[0])
-    by_middle = spatial_conv(activated[1:], conv_weight[1])
-    to_next = jnp.concatenate([by_first[:1] + by_middle, by_first[1:]]).astype(jnp.bfloat16)
+    to_next = timed_conv(activated, conv_weight[:2], (0, 1)).astype(jnp.bfloat16)
     pairs = [(i, i + 1) for i in range(span_count - 1)]
     from_prev = lax.ppermute(to_next, "span", pairs)
-    by_last = spatial_conv(activated, conv_weight[2])
-    own_middle = spatial_conv(activated[:1], conv_weight[1])
-    own_sum = jnp.concatenate([by_last[:1], own_middle + by_last[1:]])
+    own_sum = timed_conv(activated, conv_weight[1:], (1, 0))
     out_width = conv_weight.shape[-1]
     own_rows = mixed_own.reshape(FD, RD, W, C)
     own_channels = lax.dynamic_slice_in_dim(own_rows, chan_index * out_width, out_width, 3)

time: 40.3 us -> 38 us (0.943)
  local copies, waits for them, and re-layouts: 7.09 us -> 4.42 us
  waiting for transfers between devices: 1.15 us -> 1.7 us
    reshape x2 -> x0, local copies, waits for them, and re-layouts: 1.73 us -> none  [local(): activated = activated.reshape(FD, RD + 2, W, C)]
    slice x6 -> x0, local copies, waits for them, and re-layouts: 1.54 us -> none  [the longest x3 1.3 us: local(): by_middle = spatial_conv(activated[1:], conv_weight[1])]
    another operation x2, local copies, waits for them, and re-layouts: 0.21 us -> 1.48 us  [timed_conv(): frames[None]]
    unnamed x16 -> x9, local copies, waits for them, and re-layouts: 1.41 us -> 0.32 us
    convert_element_type x0 -> x3, local copies, waits for them, and re-layouts: none -> 0.88 us  [the longest x1 0.67 us: local(): return total.astype(jnp.bfloat16)]
    add x1, other arithmetic: 0.02 us -> 0.74 us  [local(): spot // per_frame * (tile_total // FD) + owner * per_frame]
    conv_general_dilated x13 -> x3, local copies, waits for them, and re-layouts: 0.82 us -> 0.24 us  [timed_conv(): lax.conv_general_dilated(frames[None], kernel, (1, 1, 1), (time_pad, (0,...]
    ppermute x1, waiting for transfers between devices: 1.15 us -> 1.7 us  [local(): from_prev = lax.ppermute(to_next, 'span', pairs)]
  transfers between devices with their start and end apart: 1 -> 1, of which waited for: 1 -> 1; matrix products, arithmetic and copies ran while one was open for 5% -> 4% of each run, Pallas kernels for 0% -> 0%
where the time goes in v8:
time: 38 us; the launch traced here: 37.8 us
  blocking collectives  17.2 us (45%)
  Pallas kernels  5.02 us (13%)
  matrix products  4.73 us (12%)
  local copies, waits for them, and re-layouts  4.42 us (12%)
  starting transfers between devices  3.55 us (9%)
  waiting for transfers between devices  1.7 us (4%)
  other arithmetic  0.97 us (3%)
    all_gather x1, blocking collectives, local(): lax.all_gather(own_share, ('patch', 'chan'), axis=1, tiled=True)[0]  17.2 us
    pallas_call x1, Pallas kernels, attend_frames(): pl.pallas_call(attention_kernel, grid_spec=grid_spec, out_shape=[jax.Shap...  5.02 us
    conv_general_dilated x2, matrix products, timed_conv(): lax.conv_general_dilated(frames[None], kernel, (1, 1, 1), (time_pad, (0,...  4.36 us
    ppermute x1, starting transfers between devices, local(): from_prev = lax.ppermute(to_next, 'span', pairs)  3.55 us
    ppermute x1, waiting for transfers between devices, local(): from_prev = lax.ppermute(to_next, 'span', pairs)  1.7 us
    another operation x2, local copies, waits for them, and re-layouts, timed_conv(): frames[None]  1.48 us
    another operation x1, local copies, waits for them, and re-layouts, local(): whole.reshape(FD, rows * W, C)  1.36 us
  transfers between devices with their start and end apart: 1, of which 1 were waited for; matrix products, arithmetic and copies ran while one was open for 4% of the time, Pallas kernels for 0%

profile of v8, /device:TPU:0, one launch (start us, length us, event | category | flops | bytes accessed | tf_op | source)
XLA Modules:
  0.0 37.8 jit_solution(10518323804707512159)
XLA Ops:
  0.0 0.0 copy-start
  0.0 0.7 %fusion.22 = s32[1,256]{1,0:T(1,128)S(1)} fusion(s32[1,256]{1,0:T(1,128)} %param.6), kind=kLoop, calls=%fused_computation.29 | loop fusion | flops 10752 | bytes 2048 | tf_op jit(solution)/shard_map/add | solution.py:145
  0.7 0.2 copy-done
  1.0 17.2 %all_gather.3 = bf16[1,256,4,384]{3,2,0,1:T(4,128)(2,1)S(1)} all-gather(bf16[1,32,4,384]{3,2,0,1:T(4,128)(2,1)S(1)} %constant_dynamic-slice_fusion.1), channel_id=1, replica_groups=mesh['clips'=2,'patch'=4,'span'=2,'chan'=2] {'patch','chan'}, dimensions={1}, use_global_device_ids=true | all-gather | bytes 884736 | tf_op jit(solution)/shard_map/all_gather | solution.py:138
  18.2 0.1 copy.22
  18.3 0.4 convolution_convert_fusion
  18.7 1.4 %reshape_reshape.3.cells_ref = bf16[2,512,384]{2,1,0:T(8,128)(2,1)} reshape(bf16[256,1536]{1,0:T(8,128)(2,1)S(1)} %convolution_convert_fusion) | data formatting | bytes 1572864 | tf_op jit(solution)/shard_map/reshape;reshape | solution.py:154
  20.1 5.0 %shard_map.55 = (bf16[2,128,384]{2,1,0:T(8,128)(2,1)}, bf16[2,256,384]{2,1,0:T(8,128)(2,1)}) custom-call(s32[1]{0:T(128)} %bitcast.first_ref, bf16[2,512,384]{2,1,0:T(8,128)(2,1)} %reshape_reshape.3.cells_ref, bf16[384,384]{1,0:T(8,128)(2,1)} %wq_ref.1, bf16[384,768]{1,0:T(8,128)(2,1)} %wkv_ref.1), custom_call_target="tpu_custom_call" | custom-call | tf_op jit(solution)/shard_map/pallas_call | solution.py:107
  25.1 1.3 %copy.15 = bf16[2,4,1,64,384]{4,1,3,0,2:T(4,128)(2,1)S(1)} copy(bf16[2,4,1,64,384]{4,3,1,0,2:T(8,128)(2,1)} %bitcast.33) | data formatting | bytes 786432 | tf_op jit(solution)/shard_map/broadcast_in_dim;reshape | solution.py:119
  26.4 0.2 pad
  26.6 0.1 copy.17
  26.7 0.0 copy-done.3
  26.7 0.0 copy-start.2
  26.7 3.1 %fusion.10 = bf16[2,2,8,9,192]{4,2,3,1,0:T(8,128)(2,1)S(1)} fusion(bf16[3,3,3,384,192]{3,4,2,1,0:T(8,128)(2,1)} %param.9, bf16[2,4,1,7,2,384]{5,3,4,1,0,2:T(8,128)(2,1)S(1)} %slice.12, bf16[2,4,1,8,9,384]{5,3,4,1,0,2:T(8,128)(2,1)S(1)} %copy.17, pred[8,9]{0,1:T(8,128)(4,1)S(1)} %copy-done.3), kind=kOutput, calls=%fused_computation.7 | convolution fusion | flops 575041536 | bytes 3293256 | tf_op jit(solution)/shard_map/conv_general_dilated | solution.py:118
  29.8 0.1 copy.19
  30.0 0.1 slice_bitcast_fusion.1
  30.1 0.0 copy-start.1
  30.1 3.5 %collective-permute-start = (bf16[2,2,64,192]{3,1,2,0:T(2,128)(2,1)S(1)}, bf16[2,2,64,192]{3,1,2,0:T(2,128)(2,1)S(1)}, u32[]{:S(2)}, u32[]{:S(2)}) collective-permute-start(bf16[2,2,64,192]{3,1,2,0:T(2,128)(2,1)S(1)} %slice_bitcast_fusion.1), channel_id=1, source_target_pairs={{0,2},{1,3},{4,6},{5,7},{8,10},{9,11},{12,14},{13,15},{16,18},{17,... | collective-permute-start | bytes 294920 | tf_op jit(solution)/shard_map/ppermute | solution.py:159
  33.6 1.2 %fusion.4 = f32[2,2,8,9,192]{4,2,3,1,0:T(8,128)S(1)} fusion(bf16[3,3,3,384,192]{3,4,2,1,0:T(8,128)(2,1)S(1)} %copy-done.2, bf16[2,4,1,7,2,384]{5,3,4,1,0,2:T(8,128)(2,1)S(1)} %slice.12, bf16[2,4,1,8,9,384]{5,3,4,1,0,2:T(8,128)(2,1)S(1)} %copy.17, pred[8,9]{0,1:T(8,128)(4,1)S(1)} %copy-done.3), kind=kOutput, calls=%fused_computation.5 | convolution fusion | flops 574986240 | bytes 3418112 | tf_op jit(solution)/shard_map/conv_general_dilated | solution.py:118
  34.9 0.2 copy.18
  35.0 0.1 constant_dynamic-slice_fusion
  35.2 1.7 %collective-permute-done = bf16[2,2,64,192]{3,1,2,0:T(2,128)(2,1)S(1)} collective-permute-done((bf16[2,2,64,192]{3,1,2,0:T(2,128)(2,1)S(1)}, bf16[2,2,64,192]{3,1,2,0:T(2,128)(2,1)S(1)}, u32[]{:S(2)}, u32[]{:S(2)}) %collective-permute-start) | collective-permute-done | bytes 98336 | tf_op jit(solution)/shard_map/ppermute | solution.py:159
  36.9 0.2 fusion.18
  37.1 0.7 %copy.20 = bf16[2,2,64,192]{3,2,1,0:T(8,128)(2,1)} copy(bf16[2,2,64,192]{3,1,2,0:T(2,128)(2,1)S(1)} %fusion.18) | data formatting | bytes 196608 | tf_op jit(solution)/shard_map/convert_element_type | solution.py:165
  (5 shorter events, 0.1 us)
Async XLA Ops:
  0.0 0.9 %copy-start = (bf16[1,64,4,384]{3,2,1,0:T(4,128)(2,1)S(1)}, bf16[1,64,4,384]{3,2,1,0:T(4,128)(2,1)}, u32[]{:S(2)}) copy-start(bf16[1,64,4,384]{3,2,1,0:T(4,128)(2,1)} %param.5) | copy-start | bytes 589828
  25.1 1.6 %copy-start.3 = (pred[8,9]{0,1:T(8,128)(4,1)S(1)}, pred[8,9]{0,1:T(8,128)(4,1)}, u32[]{:S(2)}) copy-start(pred[8,9]{0,1:T(8,128)(4,1)} %constant.79) | copy-start | bytes 220
  26.7 6.9 %copy-start.2 = (bf16[3,3,3,384,192]{3,4,2,1,0:T(8,128)(2,1)S(1)}, bf16[3,3,3,384,192]{3,4,2,1,0:T(8,128)(2,1)}, u32[]{:S(2)}) copy-start(bf16[3,3,3,384,192]{3,4,2,1,0:T(8,128)(2,1)} %param.9) | copy-start | bytes 11943940
  30.1 5.0 %copy-start.1 = (bf16[2,128,384]{2,1,0:T(8,128)(2,1)S(1)}, bf16[2,128,384]{2,1,0:T(8,128)(2,1)}, u32[]{:S(2)}) copy-start(bf16[2,128,384]{2,1,0:T(8,128)(2,1)} %get-tuple-element.7) | copy-start | bytes 589828
  30.1 6.8 %collective-permute-start = (bf16[2,2,64,192]{3,1,2,0:T(2,128)(2,1)S(1)}, bf16[2,2,64,192]{3,1,2,0:T(2,128)(2,1)S(1)}, u32[]{:S(2)}, u32[]{:S(2)}) collective-permute-start(bf16[2,2,64,192]{3,1,2,0:T(2,128)(2,1)S(1)} %slice_bitcast_fusion.1), channel_id=1, source_target_pairs={{0,2},{1,3},{4,6},{5,7},{8,10},{9,11},{12,14},{13,15},{16,18},{17,... | collective-permute-start | bytes 294920 | tf_op jit(solution)/shard_map/ppermute | solution.py:159

commit v9 on v8

--- a/solution.py
+++ b/solution.py
@@ -22,32 +22,48 @@
     return wide / jnp.sqrt(jnp.mean(wide * wide, axis=-1, keepdims=True) + epsilon)
 
 
-def attention_kernel(first_ref, cells_ref, wq_ref, wkv_ref, mixed_ref, act_ref):
+def attention_kernel(first_ref, tiles_ref, wq_ref, wkv_ref, mixed_ref, act_ref):
     width = wq_ref.shape[0]
     scale = 1.0 / math.sqrt(width)
-    count = cells_ref.shape[1]
+    cell = tiles_ref.shape[2] // width
     own = mixed_ref.shape[1]
     line = (act_ref.shape[1] - own) // 2
+    across = line // cell
+    count = tiles_ref.shape[1] * cell
     frame_rows = count // line
     first = first_ref[0]
-    top = jnp.maximum(first, 0) * line
-    below = jnp.minimum(first + 1 + own // line, frame_rows - 1) * line
-    feats = jnp.concatenate(
+    top = jnp.maximum(first, 0) * across
+    below = jnp.minimum(first + 1 + own // line, frame_rows - 1) * across
+    picked = jnp.concatenate(
         [
-            cells_ref[0, pl.ds(top, line), :],
-            cells_ref[0, pl.ds((first + 1) * line, own), :],
-            cells_ref[0, pl.ds(below, line), :],
+            tiles_ref[0, pl.ds(top, across), :],
+            tiles_ref[0, pl.ds((first + 1) * across, own // cell), :],
+            tiles_ref[0, pl.ds(below, across), :],
         ],
         axis=0,
-    ).astype(jnp.float32)
+    )
+    rows = act_ref.shape[1]
+    target = lax.broadcasted_iota(jnp.int32, (rows, rows // cell), 0)
+    source = lax.broadcasted_iota(jnp.int32, (rows, rows // cell), 1)
+    feats = None
+    for i in range(cell):
+        spread = ((source == target // cell) & (target % cell == i)).astype(jnp.bfloat16)
+        part = jnp.dot(
+            spread, picked[:, i * width : (i + 1) * width], preferred_element_type=jnp.float32
+        )
+        feats = part if feats is None else feats + part
     queries = jnp.dot(
         scaled_rms(feats).astype(jnp.bfloat16), wq_ref[...], preferred_element_type=jnp.float32
     ).astype(jnp.bfloat16)
     block = min(count, KEY_BLOCK)
+    chunk = block // cell
 
     def fold(step, carry):
         run_max, run_total, run_acc = carry
-        cells = cells_ref[0, pl.ds(step * block, block), :]
+        group = tiles_ref[0, pl.ds(step * chunk, chunk), :]
+        cells = jnp.concatenate(
+            [group[:, i * width : (i + 1) * width] for i in range(cell)], axis=0
+        )
         keyvals = jnp.dot(
             scaled_rms(cells).astype(jnp.bfloat16), wkv_ref[...], preferred_element_type=jnp.float32
         ).astype(jnp.bfloat16)
@@ -69,7 +85,6 @@
         )
         return new_max, run_total, run_acc
 
-    rows = feats.shape[0]
     carry = (
         jnp.full((rows, 1), -jnp.inf, jnp.float32),
         jnp.zeros((rows, 1), jnp.float32),
@@ -86,8 +101,9 @@
     act_ref[0] = jnp.where(inside, normed / (1.0 + jnp.exp(-normed)), 0.0).astype(jnp.bfloat16)
 
 
-def attend_frames(first, cells, ext_rows, w_query, w_keyval):
-    frames, count, width = cells.shape
+def attend_frames(first, tiles, ext_rows, w_query, w_keyval):
+    frames, count, packed = tiles.shape
+    width = w_query.shape[0]
     own = ext_rows - 2 * (ext_rows // (RD + 2))
     fixed = lambda f, first_ref: (0, 0)
     per_frame = lambda f, first_ref: (f, 0, 0)
@@ -95,7 +111,7 @@
         num_scalar_prefetch=1,
         grid=(frames,),
         in_specs=[
-            pl.BlockSpec((1, count, width), per_frame),
+            pl.BlockSpec((1, count, packed), per_frame),
             pl.BlockSpec(w_query.shape, fixed),
             pl.BlockSpec(w_keyval.shape, fixed),
         ],
@@ -111,7 +127,7 @@
             jax.ShapeDtypeStruct((frames, own, width), jnp.bfloat16),
             jax.ShapeDtypeStruct((frames, ext_rows, width), jnp.bfloat16),
         ],
-    )(first, cells, w_query, w_keyval)
+    )(first, tiles, w_query, w_keyval)
 
 
 def timed_conv(frames, kernel, time_pad):
@@ -148,10 +164,9 @@
     placed = jnp.dot(
         one_hot, every_tile.reshape(tile_total, -1), preferred_element_type=jnp.float32
     ).astype(jnp.bfloat16)
-    whole = placed.reshape(FD, rows, W, C)
     first = jnp.reshape(patch_index * RD - 1, (1,)).astype(jnp.int32)
     mixed_own, activated = attend_frames(
-        first, whole.reshape(FD, rows * W, C), (RD + 2) * W, w_query, w_keyval
+        first, placed.reshape(FD, tile_total // FD, -1), (RD + 2) * W, w_query, w_keyval
     )
     activated = activated.reshape(FD, RD + 2, W, C)
     to_next = timed_conv(activated, conv_weight[:2], (0, 1)).astype(jnp.bfloat16)

time: 38 us -> 38.3 us (level)
  local copies, waits for them, and re-layouts: 4.42 us -> 3.06 us
  matrix products: 4.73 us -> 5.63 us
  Pallas kernels: 5.02 us -> 5.78 us
    another operation x1 -> x0, local copies, waits for them, and re-layouts: 1.36 us -> none  [local(): whole.reshape(FD, rows * W, C)]
    dot_general x1, matrix products: 0.37 us -> 1.27 us  [local(): jnp.dot(one_hot, every_tile.reshape(tile_total, -1), preferred_element_ty...]
    pallas_call x1, Pallas kernels: 5.02 us -> 5.78 us  [attend_frames(): pl.pallas_call(attention_kernel, grid_spec=grid_spec, out_shape=[jax.Shap...]
where the time goes in v9:
time: 38.3 us; the launch traced here: 38.1 us
  blocking collectives  17.2 us (45%)
  Pallas kernels  5.78 us (15%)
  matrix products  5.63 us (15%)
  starting transfers between devices  3.55 us (9%)
  local copies, waits for them, and re-layouts  3.06 us (8%)
  waiting for transfers between devices  1.7 us (4%)
  other arithmetic  0.97 us (3%)
    all_gather x1, blocking collectives, local(): lax.all_gather(own_share, ('patch', 'chan'), axis=1, tiled=True)[0]  17.2 us
    pallas_call x1, Pallas kernels, attend_frames(): pl.pallas_call(attention_kernel, grid_spec=grid_spec, out_shape=[jax.Shap...  5.78 us
    conv_general_dilated x2, matrix products, timed_conv(): lax.conv_general_dilated(frames[None], kernel, (1, 1, 1), (time_pad, (0,...  4.36 us
    ppermute x1, starting transfers between devices, local(): from_prev = lax.ppermute(to_next, 'span', pairs)  3.55 us
    ppermute x1, waiting for transfers between devices, local(): from_prev = lax.ppermute(to_next, 'span', pairs)  1.7 us
    another operation x2, local copies, waits for them, and re-layouts, timed_conv(): frames[None]  1.48 us
    dot_general x1, matrix products, local(): jnp.dot(one_hot, every_tile.reshape(tile_total, -1), preferred_element_ty...  1.27 us
  transfers between devices with their start and end apart: 1, of which 1 were waited for; matrix products, arithmetic and copies ran while one was open for 4% of the time, Pallas kernels for 0%

profile of v9, /device:TPU:0, one launch (start us, length us, event | category | flops | bytes accessed | tf_op | source)
XLA Modules:
  0.0 38.1 jit_solution(2347610131473746699)
XLA Ops:
  0.0 0.0 copy-start
  0.0 0.7 %fusion.22 = s32[1,256]{1,0:T(1,128)S(1)} fusion(s32[1,256]{1,0:T(1,128)} %param.6), kind=kLoop, calls=%fused_computation.29 | loop fusion | flops 10752 | bytes 2048 | tf_op jit(solution)/shard_map/add | solution.py:161
  0.7 0.2 copy-done
  1.0 17.2 %all_gather.3 = bf16[1,256,4,384]{3,2,0,1:T(4,128)(2,1)S(1)} all-gather(bf16[1,32,4,384]{3,2,0,1:T(4,128)(2,1)S(1)} %constant_dynamic-slice_fusion.1), channel_id=1, replica_groups=mesh['clips'=2,'patch'=4,'span'=2,'chan'=2] {'patch','chan'}, dimensions={1}, use_global_device_ids=true | all-gather | bytes 884736 | tf_op jit(solution)/shard_map/all_gather | solution.py:154
  18.2 0.1 copy.22
  18.3 1.3 %convolution_convert_fusion = bf16[256,1536]{1,0:T(8,128)(2,1)} fusion(bf16[256,1536]{1,0:T(8,128)(2,1)S(1)} %bitcast.30, s32[256]{0:T(256)S(1)} %bitcast.37), kind=kOutput, calls=%fused_computation.4 | convolution fusion | flops 201785344 | bytes 1573888 | tf_op jit(solution)/shard_map/dot_general | solution.py:164
  19.6 5.8 %shard_map.55 = (bf16[2,128,384]{2,1,0:T(8,128)(2,1)}, bf16[2,256,384]{2,1,0:T(8,128)(2,1)}) custom-call(s32[1]{0:T(128)} %bitcast.first_ref, bf16[2,128,1536]{2,1,0:T(8,128)(2,1)} %bitcast.31, bf16[384,384]{1,0:T(8,128)(2,1)} %wq_ref.1, bf16[384,768]{1,0:T(8,128)(2,1)} %wkv_ref.1), custom_call_target="tpu_custom_call" | custom-call | tf_op jit(solution)/shard_map/pallas_call | solution.py:123
  25.4 1.3 %copy.15 = bf16[2,4,1,64,384]{4,1,3,0,2:T(4,128)(2,1)S(1)} copy(bf16[2,4,1,64,384]{4,3,1,0,2:T(8,128)(2,1)} %bitcast.35) | data formatting | bytes 786432 | tf_op jit(solution)/shard_map/broadcast_in_dim;reshape | solution.py:135
  26.7 0.2 pad
  26.9 0.1 copy.17
  27.0 0.0 copy-done.3
  27.0 0.0 copy-start.2
  27.0 3.1 %fusion.10 = bf16[2,2,8,9,192]{4,2,3,1,0:T(8,128)(2,1)S(1)} fusion(bf16[3,3,3,384,192]{3,4,2,1,0:T(8,128)(2,1)} %param.9, bf16[2,4,1,7,2,384]{5,3,4,1,0,2:T(8,128)(2,1)S(1)} %slice.12, bf16[2,4,1,8,9,384]{5,3,4,1,0,2:T(8,128)(2,1)S(1)} %copy.17, pred[8,9]{0,1:T(8,128)(4,1)S(1)} %copy-done.3), kind=kOutput, calls=%fused_computation.7 | convolution fusion | flops 575041536 | bytes 3293256 | tf_op jit(solution)/shard_map/conv_general_dilated | solution.py:134
  30.1 0.1 copy.19
  30.2 0.1 slice_bitcast_fusion.1
  30.3 0.0 copy-start.1
  30.4 3.5 %collective-permute-start = (bf16[2,2,64,192]{3,1,2,0:T(2,128)(2,1)S(1)}, bf16[2,2,64,192]{3,1,2,0:T(2,128)(2,1)S(1)}, u32[]{:S(2)}, u32[]{:S(2)}) collective-permute-start(bf16[2,2,64,192]{3,1,2,0:T(2,128)(2,1)S(1)} %slice_bitcast_fusion.1), channel_id=1, source_target_pairs={{0,2},{1,3},{4,6},{5,7},{8,10},{9,11},{12,14},{13,15},{16,18},{17,... | collective-permute-start | bytes 294920 | tf_op jit(solution)/shard_map/ppermute | solution.py:174
  33.9 1.2 %fusion.4 = f32[2,2,8,9,192]{4,2,3,1,0:T(8,128)S(1)} fusion(bf16[3,3,3,384,192]{3,4,2,1,0:T(8,128)(2,1)S(1)} %copy-done.2, bf16[2,4,1,7,2,384]{5,3,4,1,0,2:T(8,128)(2,1)S(1)} %slice.12, bf16[2,4,1,8,9,384]{5,3,4,1,0,2:T(8,128)(2,1)S(1)} %copy.17, pred[8,9]{0,1:T(8,128)(4,1)S(1)} %copy-done.3), kind=kOutput, calls=%fused_computation.5 | convolution fusion | flops 574986240 | bytes 3418112 | tf_op jit(solution)/shard_map/conv_general_dilated | solution.py:134
  35.2 0.2 copy.18
  35.3 0.0 copy-done.1
  35.3 0.1 constant_dynamic-slice_fusion
  35.5 1.7 %collective-permute-done = bf16[2,2,64,192]{3,1,2,0:T(2,128)(2,1)S(1)} collective-permute-done((bf16[2,2,64,192]{3,1,2,0:T(2,128)(2,1)S(1)}, bf16[2,2,64,192]{3,1,2,0:T(2,128)(2,1)S(1)}, u32[]{:S(2)}, u32[]{:S(2)}) %collective-permute-start) | collective-permute-done | bytes 98336 | tf_op jit(solution)/shard_map/ppermute | solution.py:174
  37.2 0.2 fusion.18
  37.4 0.7 %copy.20 = bf16[2,2,64,192]{3,2,1,0:T(8,128)(2,1)} copy(bf16[2,2,64,192]{3,1,2,0:T(2,128)(2,1)S(1)} %fusion.18) | data formatting | bytes 196608 | tf_op jit(solution)/shard_map/convert_element_type | solution.py:180
  (4 shorter events, 0.1 us)
Async XLA Ops:
  0.0 0.9 %copy-start = (bf16[1,64,4,384]{3,2,1,0:T(4,128)(2,1)S(1)}, bf16[1,64,4,384]{3,2,1,0:T(4,128)(2,1)}, u32[]{:S(2)}) copy-start(bf16[1,64,4,384]{3,2,1,0:T(4,128)(2,1)} %param.5) | copy-start | bytes 589828
  25.4 1.6 %copy-start.3 = (pred[8,9]{0,1:T(8,128)(4,1)S(1)}, pred[8,9]{0,1:T(8,128)(4,1)}, u32[]{:S(2)}) copy-start(pred[8,9]{0,1:T(8,128)(4,1)} %constant.79) | copy-start | bytes 220
  27.0 6.9 %copy-start.2 = (bf16[3,3,3,384,192]{3,4,2,1,0:T(8,128)(2,1)S(1)}, bf16[3,3,3,384,192]{3,4,2,1,0:T(8,128)(2,1)}, u32[]{:S(2)}) copy-start(bf16[3,3,3,384,192]{3,4,2,1,0:T(8,128)(2,1)} %param.9) | copy-start | bytes 11943940
  30.3 5.0 %copy-start.1 = (bf16[2,128,384]{2,1,0:T(8,128)(2,1)S(1)}, bf16[2,128,384]{2,1,0:T(8,128)(2,1)}, u32[]{:S(2)}) copy-start(bf16[2,128,384]{2,1,0:T(8,128)(2,1)} %get-tuple-element.7) | copy-start | bytes 589828
  30.4 6.8 %collective-permute-start = (bf16[2,2,64,192]{3,1,2,0:T(2,128)(2,1)S(1)}, bf16[2,2,64,192]{3,1,2,0:T(2,128)(2,1)S(1)}, u32[]{:S(2)}, u32[]{:S(2)}) collective-permute-start(bf16[2,2,64,192]{3,1,2,0:T(2,128)(2,1)S(1)} %slice_bitcast_fusion.1), channel_id=1, source_target_pairs={{0,2},{1,3},{4,6},{5,7},{8,10},{9,11},{12,14},{13,15},{16,18},{17,... | collective-permute-start | bytes 294920 | tf_op jit(solution)/shard_map/ppermute | solution.py:174

commit v10 on v8

--- a/solution.py
+++ b/solution.py
@@ -161,8 +161,8 @@
     out_width = conv_weight.shape[-1]
     own_rows = mixed_own.reshape(FD, RD, W, C)
     own_channels = lax.dynamic_slice_in_dim(own_rows, chan_index * out_width, out_width, 3)
-    total = own_channels.astype(jnp.float32) + own_sum + from_prev.astype(jnp.float32)
-    return total.astype(jnp.bfloat16)
+    base = lax.optimization_barrier(own_channels.astype(jnp.float32) + own_sum)
+    return (base + from_prev.astype(jnp.float32)).astype(jnp.bfloat16)
 
 
 def solution(mesh):

time: 38 us -> 37.8 us (level)
  local copies, waits for them, and re-layouts: 4.42 us -> 3.68 us
  other arithmetic: 0.97 us -> 1.54 us
    convert_element_type x1 -> x0, local copies, waits for them, and re-layouts: 0.67 us -> none  [local(): return total.astype(jnp.bfloat16)]
    convert_element_type x1, other arithmetic: 0.23 us -> 0.69 us  [local(): return (base + from_prev.astype(jnp.float32)).astype(jnp.bfloat16)]
where the time goes in v10:
time: 37.8 us; the launch traced here: 37.6 us
  blocking collectives  17.2 us (46%)
  Pallas kernels  5.02 us (13%)
  matrix products  4.74 us (13%)
  local copies, waits for them, and re-layouts  3.68 us (10%)
  starting transfers between devices  3.55 us (9%)
  waiting for transfers between devices  1.68 us (4%)
  other arithmetic  1.54 us (4%)
    all_gather x1, blocking collectives, local(): lax.all_gather(own_share, ('patch', 'chan'), axis=1, tiled=True)[0]  17.2 us
    pallas_call x1, Pallas kernels, attend_frames(): pl.pallas_call(attention_kernel, grid_spec=grid_spec, out_shape=[jax.Shap...  5.02 us
    conv_general_dilated x2, matrix products, timed_conv(): lax.conv_general_dilated(frames[None], kernel, (1, 1, 1), (time_pad, (0,...  4.36 us
    ppermute x1, starting transfers between devices, local(): from_prev = lax.ppermute(to_next, 'span', pairs)  3.55 us
    ppermute x1, waiting for transfers between devices, local(): from_prev = lax.ppermute(to_next, 'span', pairs)  1.68 us
    another operation x2, local copies, waits for them, and re-layouts, timed_conv(): frames[None]  1.48 us
    another operation x1, local copies, waits for them, and re-layouts, local(): whole.reshape(FD, rows * W, C)  1.36 us
  transfers between devices with their start and end apart: 1, of which 1 were waited for; matrix products, arithmetic and copies ran while one was open for 4% of the time, Pallas kernels for 0%

profile of v10, /device:TPU:0, one launch (start us, length us, event | category | flops | bytes accessed | tf_op | source)
XLA Modules:
  0.0 37.6 jit_solution(4932744398575766913)
XLA Ops:
  0.0 0.0 copy-start
  0.0 0.7 %fusion.20 = s32[1,256]{1,0:T(1,128)S(1)} fusion(s32[1,256]{1,0:T(1,128)} %param.6), kind=kLoop, calls=%fused_computation.28 | loop fusion | flops 10752 | bytes 2048 | tf_op jit(solution)/shard_map/add | solution.py:145
  0.7 0.2 copy-done
  1.0 17.2 %all_gather.3 = bf16[1,256,4,384]{3,2,0,1:T(4,128)(2,1)S(1)} all-gather(bf16[1,32,4,384]{3,2,0,1:T(4,128)(2,1)S(1)} %constant_dynamic-slice_fusion), channel_id=1, replica_groups=mesh['clips'=2,'patch'=4,'span'=2,'chan'=2] {'patch','chan'}, dimensions={1}, use_global_device_ids=true | all-gather | bytes 884736 | tf_op jit(solution)/shard_map/all_gather | solution.py:138
  18.2 0.1 copy.31
  18.3 0.4 convolution_convert_fusion
  18.7 1.4 %reshape_reshape.3.cells_ref = bf16[2,512,384]{2,1,0:T(8,128)(2,1)} reshape(bf16[256,1536]{1,0:T(8,128)(2,1)S(1)} %convolution_convert_fusion) | data formatting | bytes 1572864 | tf_op jit(solution)/shard_map/reshape;reshape | solution.py:154
  20.1 5.0 %shard_map.55 = (bf16[2,128,384]{2,1,0:T(8,128)(2,1)}, bf16[2,256,384]{2,1,0:T(8,128)(2,1)}) custom-call(s32[1]{0:T(128)} %bitcast.first_ref, bf16[2,512,384]{2,1,0:T(8,128)(2,1)} %reshape_reshape.3.cells_ref, bf16[384,384]{1,0:T(8,128)(2,1)} %wq_ref.1, bf16[384,768]{1,0:T(8,128)(2,1)} %wkv_ref.1), custom_call_target="tpu_custom_call" | custom-call | tf_op jit(solution)/shard_map/pallas_call | solution.py:107
  25.1 1.3 %copy.22 = bf16[2,4,1,64,384]{4,1,3,0,2:T(4,128)(2,1)S(1)} copy(bf16[2,4,1,64,384]{4,3,1,0,2:T(8,128)(2,1)} %bitcast.30) | data formatting | bytes 786432 | tf_op jit(solution)/shard_map/broadcast_in_dim;reshape | solution.py:119
  26.4 0.2 pad
  26.6 0.1 copy.24
  26.7 0.0 copy-done.3
  26.7 0.0 copy-start.2
  26.7 3.1 %fusion.10 = bf16[2,2,8,9,192]{4,2,3,1,0:T(8,128)(2,1)S(1)} fusion(bf16[3,3,3,384,192]{3,4,2,1,0:T(8,128)(2,1)} %param.9, bf16[2,4,1,7,2,384]{5,3,4,1,0,2:T(8,128)(2,1)S(1)} %slice.12, bf16[2,4,1,8,9,384]{5,3,4,1,0,2:T(8,128)(2,1)S(1)} %copy.24, pred[8,9]{0,1:T(8,128)(4,1)S(1)} %copy-done.3), kind=kOutput, calls=%fused_computation.7 | convolution fusion | flops 575041536 | bytes 3293256 | tf_op jit(solution)/shard_map/conv_general_dilated | solution.py:118
  29.8 0.1 copy.27
  30.0 0.1 slice.14
  30.1 0.0 copy-start.1
  30.1 3.5 %collective-permute-start = (bf16[2,2,64,192]{3,2,1,0:T(8,128)(2,1)S(1)}, bf16[2,2,64,192]{3,2,1,0:T(8,128)(2,1)S(1)}, u32[]{:S(2)}, u32[]{:S(2)}) collective-permute-start(bf16[2,2,64,192]{3,2,1,0:T(8,128)(2,1)S(1)} %bitcast.31), channel_id=1, source_target_pairs={{0,2},{1,3},{4,6},{5,7},{8,10},{9,11},{12,14},{13,15},{16,18},{17,... | collective-permute-start | bytes 294920 | tf_op jit(solution)/shard_map/ppermute | solution.py:159
  33.7 0.0 copy-done.2
  33.7 1.2 %fusion.4 = f32[2,2,8,9,192]{4,2,3,1,0:T(8,128)S(1)} fusion(bf16[3,3,3,384,192]{3,4,2,1,0:T(8,128)(2,1)S(1)} %copy-done.2, bf16[2,4,1,7,2,384]{5,3,4,1,0,2:T(8,128)(2,1)S(1)} %slice.12, bf16[2,4,1,8,9,384]{5,3,4,1,0,2:T(8,128)(2,1)S(1)} %copy.24, pred[8,9]{0,1:T(8,128)(4,1)S(1)} %copy-done.3), kind=kOutput, calls=%fused_computation.5 | convolution fusion | flops 574986240 | bytes 3418112 | tf_op jit(solution)/shard_map/conv_general_dilated | solution.py:118
  34.9 0.2 copy.25
  35.1 0.1 fusion.16
  35.2 1.7 %collective-permute-done = bf16[2,2,64,192]{3,2,1,0:T(8,128)(2,1)S(1)} collective-permute-done((bf16[2,2,64,192]{3,2,1,0:T(8,128)(2,1)S(1)}, bf16[2,2,64,192]{3,2,1,0:T(8,128)(2,1)S(1)}, u32[]{:S(2)}, u32[]{:S(2)}) %collective-permute-start) | collective-permute-done | bytes 98336 | tf_op jit(solution)/shard_map/ppermute | solution.py:159
  36.9 0.7 %add_convert_fusion = bf16[2,2,64,192]{3,2,1,0:T(8,128)(2,1)} fusion(f32[2,2,64,192]{3,2,1,0:T(8,128)S(1)} %fusion.16, bf16[2,2,64,192]{3,2,1,0:T(8,128)(2,1)S(1)} %collective-permute-done), kind=kLoop, calls=%fused_computation.14 | loop fusion | flops 147456 | bytes 393216 | tf_op jit(solution)/shard_map/convert_element_type | solution.py:165
  (6 shorter events, 0.1 us)
Async XLA Ops:
  0.0 0.9 %copy-start = (bf16[1,64,4,384]{3,2,1,0:T(4,128)(2,1)S(1)}, bf16[1,64,4,384]{3,2,1,0:T(4,128)(2,1)}, u32[]{:S(2)}) copy-start(bf16[1,64,4,384]{3,2,1,0:T(4,128)(2,1)} %param.5) | copy-start | bytes 589828
  25.1 1.6 %copy-start.3 = (pred[8,9]{0,1:T(8,128)(4,1)S(1)}, pred[8,9]{0,1:T(8,128)(4,1)}, u32[]{:S(2)}) copy-start(pred[8,9]{0,1:T(8,128)(4,1)} %constant.79) | copy-start | bytes 220
  26.7 7.0 %copy-start.2 = (bf16[3,3,3,384,192]{3,4,2,1,0:T(8,128)(2,1)S(1)}, bf16[3,3,3,384,192]{3,4,2,1,0:T(8,128)(2,1)}, u32[]{:S(2)}) copy-start(bf16[3,3,3,384,192]{3,4,2,1,0:T(8,128)(2,1)} %param.9) | copy-start | bytes 11943940
  30.1 5.0 %copy-start.1 = (bf16[2,128,384]{2,1,0:T(8,128)(2,1)S(1)}, bf16[2,128,384]{2,1,0:T(8,128)(2,1)}, u32[]{:S(2)}) copy-start(bf16[2,128,384]{2,1,0:T(8,128)(2,1)} %get-tuple-element.7) | copy-start | bytes 589828
  30.1 6.8 %collective-permute-start = (bf16[2,2,64,192]{3,2,1,0:T(8,128)(2,1)S(1)}, bf16[2,2,64,192]{3,2,1,0:T(8,128)(2,1)S(1)}, u32[]{:S(2)}, u32[]{:S(2)}) collective-permute-start(bf16[2,2,64,192]{3,2,1,0:T(8,128)(2,1)S(1)} %bitcast.31), channel_id=1, source_target_pairs={{0,2},{1,3},{4,6},{5,7},{8,10},{9,11},{12,14},{13,15},{16,18},{17,... | collective-permute-start | bytes 294920 | tf_op jit(solution)/shard_map/ppermute | solution.py:159

commit v11 on v10

--- a/solution.py
+++ b/solution.py
@@ -104,9 +104,11 @@
             pl.BlockSpec((1, ext_rows, width), per_frame),
         ],
     )
+    block_bytes = count * width * 2
     return pl.pallas_call(
         attention_kernel,
         grid_spec=grid_spec,
+        compiler_params=pltpu.CompilerParams(vmem_limit_bytes=6 * block_bytes + (6 << 20)),
         out_shape=[
             jax.ShapeDtypeStruct((frames, own, width), jnp.bfloat16),
             jax.ShapeDtypeStruct((frames, ext_rows, width), jnp.bfloat16),

time: 37.8 us -> 32.3 us (0.85)
  Pallas kernels: 5.02 us -> 3.06 us
  matrix products: 4.74 us -> 2.85 us
  local copies, waits for them, and re-layouts: 3.68 us -> 2.11 us
    pallas_call x1, Pallas kernels: 5.02 us -> 3.06 us  [attend_frames(): pl.pallas_call(attention_kernel, grid_spec=grid_spec, compiler_params=plt...]
    conv_general_dilated x2, matrix products: 4.36 us -> 2.48 us  [timed_conv(): lax.conv_general_dilated(frames[None], kernel, (1, 1, 1), (time_pad, (0,...]
    another operation x2, local copies, waits for them, and re-layouts: 1.48 us -> 0.47 us  [timed_conv(): frames[None]]
    another operation x1, local copies, waits for them, and re-layouts: 1.36 us -> 0.47 us  [local(): whole.reshape(FD, rows * W, C)]
  transfers between devices with their start and end apart: 1 -> 1, of which waited for: 1 -> 1; matrix products, arithmetic and copies ran while one was open for 4% -> 5% of each run, Pallas kernels for 0% -> 0%
where the time goes in v11:
time: 32.3 us; the launch traced here: 32.1 us
  blocking collectives  17.2 us (53%)
  starting transfers between devices  3.39 us (10%)
  Pallas kernels  3.06 us (9%)
  matrix products  2.85 us (9%)
  local copies, waits for them, and re-layouts  2.11 us (7%)
  waiting for transfers between devices  1.71 us (5%)
  other arithmetic  1.53 us (5%)
    all_gather x1, blocking collectives, local(): lax.all_gather(own_share, ('patch', 'chan'), axis=1, tiled=True)[0]  17.2 us
    ppermute x1, starting transfers between devices, local(): from_prev = lax.ppermute(to_next, 'span', pairs)  3.39 us
    pallas_call x1, Pallas kernels, attend_frames(): pl.pallas_call(attention_kernel, grid_spec=grid_spec, compiler_params=plt...  3.06 us
    conv_general_dilated x2, matrix products, timed_conv(): lax.conv_general_dilated(frames[None], kernel, (1, 1, 1), (time_pad, (0,...  2.48 us
    ppermute x1, waiting for transfers between devices, local(): from_prev = lax.ppermute(to_next, 'span', pairs)  1.71 us
    add x1, other arithmetic, local(): spot // per_frame * (tile_total // FD) + owner * per_frame  0.74 us
    convert_element_type x1, other arithmetic, local(): return (base + from_prev.astype(jnp.float32)).astype(jnp.bfloat16)  0.68 us
    unnamed x12, local copies, waits for them, and re-layouts  0.68 us
  transfers between devices with their start and end apart: 1, of which 1 were waited for; matrix products, arithmetic and copies ran while one was open for 5% of the time, Pallas kernels for 0%

profile of v11, /device:TPU:0, one launch (start us, length us, event | category | flops | bytes accessed | tf_op | source)
XLA Modules:
  0.0 32.1 jit_solution(1887555137377834564)
XLA Ops:
  0.0 0.7 %fusion.20 = s32[1,256]{1,0:T(1,128)S(1)} fusion(s32[1,256]{1,0:T(1,128)} %param.6), kind=kLoop, calls=%fused_computation.28 | loop fusion | flops 10752 | bytes 2048 | tf_op jit(solution)/shard_map/add | solution.py:147
  0.7 0.2 copy-done
  1.0 17.2 %all_gather.3 = bf16[1,256,4,384]{3,2,0,1:T(4,128)(2,1)S(1)} all-gather(bf16[1,32,4,384]{3,2,0,1:T(4,128)(2,1)S(1)} %constant_dynamic-slice_fusion), channel_id=1, replica_groups=mesh['clips'=2,'patch'=4,'span'=2,'chan'=2] {'patch','chan'}, dimensions={1}, use_global_device_ids=true | all-gather | bytes 884736 | tf_op jit(solution)/shard_map/all_gather | solution.py:140
  18.2 0.1 copy.31
  18.3 0.0 copy-start.2
  18.3 0.4 %convolution_convert_fusion = bf16[256,1536]{1,0:T(8,128)(2,1)S(1)} fusion(bf16[256,1536]{1,0:T(8,128)(2,1)S(1)} %bitcast.28, s32[256]{0:T(256)S(1)} %bitcast.33), kind=kOutput, calls=%fused_computation.4 | convolution fusion | flops 201785344 | bytes 1573888 | tf_op jit(solution)/shard_map/dot_general | solution.py:150
  18.7 0.5 %reshape_reshape.3.cells_ref = bf16[2,512,384]{2,1,0:T(8,128)(2,1)S(1)} reshape(bf16[256,1536]{1,0:T(8,128)(2,1)S(1)} %convolution_convert_fusion) | data formatting | bytes 1572864 | tf_op jit(solution)/shard_map/reshape;reshape | solution.py:156
  19.2 0.2 copy-done.1
  19.4 0.1 copy-done.2
  19.5 3.1 %shard_map.55 = (bf16[2,128,384]{2,1,0:T(8,128)(2,1)S(1)}, bf16[2,256,384]{2,1,0:T(8,128)(2,1)S(1)}) custom-call(s32[1]{0:T(128)} %bitcast.first_ref, bf16[2,512,384]{2,1,0:T(8,128)(2,1)S(1)} %reshape_reshape.3.cells_ref, bf16[384,384]{1,0:T(8,128)(2,1)S(1)} %copy-done.2, bf16[384,768]{1,0:T(8,128)(2,1)S(1)} %copy-done.1), custom_call_target="tpu_custom_call" | custom-call | tf_op jit(solution)/shard_map/pallas_call | solution.py:108
  22.5 0.0 copy-start.4
  22.5 0.3 copy.22
  22.9 0.2 pad
  23.0 0.1 copy.24
  23.1 0.1 copy-done.4
  23.2 1.2 %fusion.10 = bf16[2,2,8,9,192]{4,2,3,1,0:T(8,128)(2,1)S(1)} fusion(bf16[3,3,3,384,192]{3,4,2,1,0:T(8,128)(2,1)S(1)} %copy-done.3, bf16[2,4,1,7,2,384]{5,3,4,1,0,2:T(8,128)(2,1)S(1)} %slice.12, bf16[2,4,1,8,9,384]{5,3,4,1,0,2:T(8,128)(2,1)S(1)} %copy.24, pred[8,9]{0,1:T(8,128)(4,1)S(1)} %copy-done.4), kind=kOutput, calls=%fused_computation.7 | convolution fusion | flops 575041536 | bytes 3307520 | tf_op jit(solution)/shard_map/conv_general_dilated | solution.py:120
  24.5 0.1 copy.27
  24.6 0.1 slice.14
  24.7 3.4 %collective-permute-start = (bf16[2,2,64,192]{3,2,1,0:T(8,128)(2,1)S(1)}, bf16[2,2,64,192]{3,2,1,0:T(8,128)(2,1)S(1)}, u32[]{:S(2)}, u32[]{:S(2)}) collective-permute-start(bf16[2,2,64,192]{3,2,1,0:T(8,128)(2,1)S(1)} %bitcast.32), channel_id=1, source_target_pairs={{0,2},{1,3},{4,6},{5,7},{8,10},{9,11},{12,14},{13,15},{16,18},{17,... | collective-permute-start | bytes 294920 | tf_op jit(solution)/shard_map/ppermute | solution.py:161
  28.1 1.2 %fusion.4 = f32[2,2,8,9,192]{4,2,3,1,0:T(8,128)S(1)} fusion(bf16[3,3,3,384,192]{3,4,2,1,0:T(8,128)(2,1)S(1)} %copy-done.3, bf16[2,4,1,7,2,384]{5,3,4,1,0,2:T(8,128)(2,1)S(1)} %slice.12, bf16[2,4,1,8,9,384]{5,3,4,1,0,2:T(8,128)(2,1)S(1)} %copy.24, pred[8,9]{0,1:T(8,128)(4,1)S(1)} %copy-done.4), kind=kOutput, calls=%fused_computation.5 | convolution fusion | flops 574986240 | bytes 3418112 | tf_op jit(solution)/shard_map/conv_general_dilated | solution.py:120
  29.4 0.2 copy.25
  29.5 0.1 fusion.16
  29.7 1.7 %collective-permute-done = bf16[2,2,64,192]{3,2,1,0:T(8,128)(2,1)S(1)} collective-permute-done((bf16[2,2,64,192]{3,2,1,0:T(8,128)(2,1)S(1)}, bf16[2,2,64,192]{3,2,1,0:T(8,128)(2,1)S(1)}, u32[]{:S(2)}, u32[]{:S(2)}) %collective-permute-start) | collective-permute-done | bytes 98336 | tf_op jit(solution)/shard_map/ppermute | solution.py:161
  31.4 0.7 %add_convert_fusion = bf16[2,2,64,192]{3,2,1,0:T(8,128)(2,1)} fusion(f32[2,2,64,192]{3,2,1,0:T(8,128)S(1)} %fusion.16, bf16[2,2,64,192]{3,2,1,0:T(8,128)(2,1)S(1)} %collective-permute-done), kind=kLoop, calls=%fused_computation.14 | loop fusion | flops 147456 | bytes 393216 | tf_op jit(solution)/shard_map/convert_element_type | solution.py:167
  (8 shorter events, 0.1 us)
Async XLA Ops:
  0.0 0.9 %copy-start = (bf16[1,64,4,384]{3,2,1,0:T(4,128)(2,1)S(1)}, bf16[1,64,4,384]{3,2,1,0:T(4,128)(2,1)}, u32[]{:S(2)}) copy-start(bf16[1,64,4,384]{3,2,1,0:T(4,128)(2,1)} %param.5) | copy-start | bytes 589828
  18.3 1.1 %copy-start.1 = (bf16[384,768]{1,0:T(8,128)(2,1)S(1)}, bf16[384,768]{1,0:T(8,128)(2,1)}, u32[]{:S(2)}) copy-start(bf16[384,768]{1,0:T(8,128)(2,1)} %wkv_ref.1) | copy-start | bytes 1769476
  18.3 1.1 %copy-start.2 = (bf16[384,384]{1,0:T(8,128)(2,1)S(1)}, bf16[384,384]{1,0:T(8,128)(2,1)}, u32[]{:S(2)}) copy-start(bf16[384,384]{1,0:T(8,128)(2,1)} %wq_ref.1) | copy-start | bytes 884740
  19.5 3.7 %copy-start.3 = (bf16[3,3,3,384,192]{3,4,2,1,0:T(8,128)(2,1)S(1)}, bf16[3,3,3,384,192]{3,4,2,1,0:T(8,128)(2,1)}, u32[]{:S(2)}) copy-start(bf16[3,3,3,384,192]{3,4,2,1,0:T(8,128)(2,1)} %param.9) | copy-start | bytes 11943940
  22.5 0.7 %copy-start.4 = (pred[8,9]{0,1:T(8,128)(4,1)S(1)}, pred[8,9]{0,1:T(8,128)(4,1)}, u32[]{:S(2)}) copy-start(pred[8,9]{0,1:T(8,128)(4,1)} %constant.79) | copy-start | bytes 220
  24.7 6.7 %collective-permute-start = (bf16[2,2,64,192]{3,2,1,0:T(8,128)(2,1)S(1)}, bf16[2,2,64,192]{3,2,1,0:T(8,128)(2,1)S(1)}, u32[]{:S(2)}, u32[]{:S(2)}) collective-permute-start(bf16[2,2,64,192]{3,2,1,0:T(8,128)(2,1)S(1)} %bitcast.32), channel_id=1, source_target_pairs={{0,2},{1,3},{4,6},{5,7},{8,10},{9,11},{12,14},{13,15},{16,18},{17,... | collective-permute-start | bytes 294920 | tf_op jit(solution)/shard_map/ppermute | solution.py:161

commit v12 on v11

--- a/solution.py
+++ b/solution.py
@@ -127,6 +127,20 @@
     )[0]
 
 
+def gather_tiles(share, patch_count, patch_index):
+    if patch_count <= 4:
+        got = [share]
+        for d in range(1, patch_count):
+            shift = [(i, (i + d) % patch_count) for i in range(patch_count)]
+            got.append(lax.ppermute(share, "patch", shift))
+        order = (patch_index - jnp.arange(patch_count)) % patch_count
+        by_patch = jnp.take(jnp.stack(got), order, axis=0)
+    else:
+        by_patch = lax.all_gather(share, "patch", axis=0, tiled=False)
+    both = lax.all_gather(by_patch, "chan", axis=1, tiled=False)
+    return both.reshape((-1,) + share.shape[1:])
+
+
 def local(latent_tiles, route, w_query, w_keyval, conv_weight):
     patch_count = lax.axis_size("patch")
     patch_index = lax.axis_index("patch")
@@ -137,7 +151,7 @@
     block = latent_tiles.shape[1]
     share = block // chan_count
     own_share = lax.dynamic_slice_in_dim(latent_tiles, chan_index * share, share, 1)
-    every_tile = lax.all_gather(own_share, ("patch", "chan"), axis=1, tiled=True)[0]
+    every_tile = gather_tiles(own_share[0], patch_count, patch_index)
     tile_total = every_tile.shape[0]
     rows = patch_count * RD
     per_owner = tile_total // patch_count

time: 32.3 us -> 32.7 us (1.012)
  blocking collectives: 17.2 us -> 2.37 us
  starting transfers between devices: 3.39 us -> 11.4 us
  waiting for transfers between devices: 1.71 us -> 6.95 us
  local copies, waits for them, and re-layouts: 2.11 us -> 3.9 us
    all_gather x1, blocking collectives: 17.2 us -> 2.37 us  [gather_tiles(): both = lax.all_gather(by_patch, 'chan', axis=1, tiled=False)]
    ppermute x0 -> x3, starting transfers between devices: none -> 7.93 us  [gather_tiles(): got.append(lax.ppermute(share, 'patch', shift))]
    ppermute x0 -> x3, waiting for transfers between devices: none -> 4.02 us  [gather_tiles(): got.append(lax.ppermute(share, 'patch', shift))]
    ppermute x1, waiting for transfers between devices: 1.71 us -> 2.93 us  [local(): from_prev = lax.ppermute(to_next, 'span', pairs)]
    unnamed x12 -> x13, local copies, waits for them, and re-layouts: 0.68 us -> 1.42 us
    gather x0 -> x1, local copies, waits for them, and re-layouts: none -> 0.63 us  [gather_tiles(): by_patch = jnp.take(jnp.stack(got), order, axis=0)]
    all_gather x0 -> x1, local copies, waits for them, and re-layouts: none -> 0.41 us  [gather_tiles(): both = lax.all_gather(by_patch, 'chan', axis=1, tiled=False)]
  transfers between devices with their start and end apart: 1 -> 4, of which waited for: 1 -> 3; matrix products, arithmetic and copies ran while one was open for 5% -> 3% of each run, Pallas kernels for 0% -> 0%
where the time goes in v12:
time: 32.7 us; the launch traced here: 32.4 us
  starting transfers between devices  11.4 us (35%)
  waiting for transfers between devices  6.95 us (21%)
  local copies, waits for them, and re-layouts  3.9 us (12%)
  Pallas kernels  3.04 us (9%)
  matrix products  2.84 us (9%)
  blocking collectives  2.37 us (7%)
  other arithmetic  1.71 us (5%)
    ppermute x3, starting transfers between devices, gather_tiles(): got.append(lax.ppermute(share, 'patch', shift))  7.93 us
    ppermute x3, waiting for transfers between devices, gather_tiles(): got.append(lax.ppermute(share, 'patch', shift))  4.02 us
    ppermute x1, starting transfers between devices, local(): from_prev = lax.ppermute(to_next, 'span', pairs)  3.45 us
    pallas_call x1, Pallas kernels, attend_frames(): pl.pallas_call(attention_kernel, grid_spec=grid_spec, compiler_params=plt...  3.04 us
    ppermute x1, waiting for transfers between devices, local(): from_prev = lax.ppermute(to_next, 'span', pairs)  2.93 us
    conv_general_dilated x2, matrix products, timed_conv(): lax.conv_general_dilated(frames[None], kernel, (1, 1, 1), (time_pad, (0,...  2.47 us
    all_gather x1, blocking collectives, gather_tiles(): both = lax.all_gather(by_patch, 'chan', axis=1, tiled=False)  2.37 us
    unnamed x13, local copies, waits for them, and re-layouts  1.42 us
  transfers between devices with their start and end apart: 4, of which 3 were waited for; matrix products, arithmetic and copies ran while one was open for 3% of the time, Pallas kernels for 0%

profile of v12, /device:TPU:0, one launch (start us, length us, event | category | flops | bytes accessed | tf_op | source)
XLA Modules:
  0.0 32.4 jit_solution(8837849543253288224)
XLA Ops:
  0.0 0.9 %copy-done = bf16[1,64,4,384]{3,2,1,0:T(4,128)(2,1)S(1)} copy-done((bf16[1,64,4,384]{3,2,1,0:T(4,128)(2,1)S(1)}, bf16[1,64,4,384]{3,2,1,0:T(4,128)(2,1)}, u32[]{:S(2)}) %copy-start) | copy-done | bytes 196632
  1.0 4.1 %collective-permute-start.1 = (bf16[32,4,384]{2,0,1:T(8,128)(2,1)S(1)}, bf16[32,4,384]{2,0,1:T(8,128)(2,1)S(1)}, u32[]{:S(2)}, u32[]{:S(2)}) collective-permute-start(bf16[32,4,384]{2,0,1:T(8,128)(2,1)S(1)} %bitcast.38), channel_id=1, source_target_pairs={{0,8},{4,12},{8,0},{12,4},{1,9},{5,13},{9,1},{13,5},{2,10},{6,14},... | collective-permute-start | bytes 294920 | tf_op jit(solution)/shard_map/ppermute | solution.py:135
  5.1 1.6 %collective-permute-start = (bf16[32,4,384]{2,0,1:T(8,128)(2,1)S(1)}, bf16[32,4,384]{2,0,1:T(8,128)(2,1)S(1)}, u32[]{:S(2)}, u32[]{:S(2)}) collective-permute-start(bf16[32,4,384]{2,0,1:T(8,128)(2,1)S(1)} %bitcast.39), channel_id=1, source_target_pairs={{0,4},{4,8},{8,12},{12,0},{1,5},{5,9},{9,13},{13,1},{2,6},{6,10},{... | collective-permute-start | bytes 294920 | tf_op jit(solution)/shard_map/ppermute | solution.py:135
  6.7 2.2 %collective-permute-start.2 = (bf16[32,4,384]{2,0,1:T(8,128)(2,1)S(1)}, bf16[32,4,384]{2,0,1:T(8,128)(2,1)S(1)}, u32[]{:S(2)}, u32[]{:S(2)}) collective-permute-start(bf16[32,4,384]{2,0,1:T(8,128)(2,1)S(1)} %bitcast.40), channel_id=1, source_target_pairs={{0,12},{4,0},{8,4},{12,8},{1,13},{5,1},{9,5},{13,9},{2,14},{6,2},{... | collective-permute-start | bytes 294920 | tf_op jit(solution)/shard_map/ppermute | solution.py:135
  8.9 0.7 %fusion.20 = s32[1,256]{1,0:T(1,128)S(1)} fusion(s32[1,256]{1,0:T(1,128)} %param.6), kind=kLoop, calls=%fused_computation.41 | loop fusion | flops 10752 | bytes 2048 | tf_op jit(solution)/shard_map/add | solution.py:161
  9.7 3.3 %collective-permute-done.1 = bf16[32,4,384]{2,0,1:T(8,128)(2,1)S(1)} collective-permute-done((bf16[32,4,384]{2,0,1:T(8,128)(2,1)S(1)}, bf16[32,4,384]{2,0,1:T(8,128)(2,1)S(1)}, u32[]{:S(2)}, u32[]{:S(2)}) %collective-permute-start.1) | collective-permute-done | bytes 98336 | tf_op jit(solution)/shard_map/ppermute | solution.py:135
  13.0 0.7 %collective-permute-done.2 = bf16[32,4,384]{2,0,1:T(8,128)(2,1)S(1)} collective-permute-done((bf16[32,4,384]{2,0,1:T(8,128)(2,1)S(1)}, bf16[32,4,384]{2,0,1:T(8,128)(2,1)S(1)}, u32[]{:S(2)}, u32[]{:S(2)}) %collective-permute-start.2) | collective-permute-done | bytes 98336 | tf_op jit(solution)/shard_map/ppermute | solution.py:135
  13.8 0.6 %gather_fusion = bf16[4,32,4,384]{3,1,2,0:T(8,128)(2,1)S(1)} fusion(bf16[4,32,4,384]{3,1,2,0:T(8,128)(2,1)S(1)} %pad_maximum_fusion, s32[1024]{0:T(1024)S(1)} %pad_clamp_fusion), kind=kCustom, calls=%fused_computation | custom fusion | bytes 786448 | tf_op jit(solution)/shard_map/jit(_take)/gather | solution.py:137
  14.4 0.1 bitcast_select_fusion
  14.5 2.4 %all_gather.4 = bf16[4,2,32,4,384]{4,2,3,0,1:T(8,128)(2,1)S(1)} all-gather(bf16[4,1,32,4,384]{4,2,3,0,1:T(8,128)(2,1)S(1)} %bitcast_select_fusion), channel_id=1, replica_groups=mesh['clips'=2,'patch'=4,'span'=2,'chan'=2] {'chan'}, dimensions={1}, use_global_device_ids=true | all-gather | bytes 1179648 | tf_op jit(solution)/shard_map/all_gather | solution.py:140
  16.9 0.4 %copy.32 = bf16[4,2,32,4,384]{4,3,2,1,0:T(4,128)(2,1)S(1)} copy(bf16[4,2,32,4,384]{4,2,3,0,1:T(8,128)(2,1)S(1)} %all_gather.4) | data formatting | bytes 1572864 | tf_op jit(solution)/shard_map/all_gather | solution.py:140
  17.4 0.4 %convolution_convert_fusion = bf16[256,1536]{1,0:T(8,128)(2,1)S(1)} fusion(bf16[256,1536]{1,0:T(8,128)(2,1)S(1)} %bitcast.34, s32[256]{0:T(256)S(1)} %bitcast.45), kind=kOutput, calls=%fused_computation.5 | convolution fusion | flops 201785344 | bytes 1573888 | tf_op jit(solution)/shard_map/dot_general | solution.py:164
  17.8 0.5 %reshape_reshape.7.cells_ref = bf16[2,512,384]{2,1,0:T(8,128)(2,1)S(1)} reshape(bf16[256,1536]{1,0:T(8,128)(2,1)S(1)} %convolution_convert_fusion) | data formatting | bytes 1572864 | tf_op jit(solution)/shard_map/reshape;reshape | solution.py:170
  18.3 0.2 copy-done.1
  18.6 3.0 %shard_map.55 = (bf16[2,128,384]{2,1,0:T(8,128)(2,1)S(1)}, bf16[2,256,384]{2,1,0:T(8,128)(2,1)S(1)}) custom-call(s32[1]{0:T(128)} %bitcast.first_ref, bf16[2,512,384]{2,1,0:T(8,128)(2,1)S(1)} %reshape_reshape.7.cells_ref, bf16[384,384]{1,0:T(8,128)(2,1)S(1)} %copy-done.2, bf16[384,768]{1,0:T(8,128)(2,1)S(1)} %copy-done.1), custom_call_target="tpu_custom_call" | custom-call | tf_op jit(solution)/shard_map/pallas_call | solution.py:108
  21.6 0.3 copy.33
  21.9 0.2 pad
  22.3 1.2 %fusion.10 = bf16[2,2,8,9,192]{4,2,3,1,0:T(8,128)(2,1)S(1)} fusion(bf16[3,3,3,384,192]{3,4,2,1,0:T(8,128)(2,1)S(1)} %copy-done.3, bf16[2,4,1,7,2,384]{5,3,4,1,0,2:T(8,128)(2,1)S(1)} %slice.14, bf16[2,4,1,8,9,384]{5,3,4,1,0,2:T(8,128)(2,1)S(1)} %copy.35, pred[8,9]{0,1:T(8,128)(4,1)S(1)} %copy-done.4), kind=kOutput, calls=%fused_computation.8 | convolution fusion | flops 575041536 | bytes 3307520 | tf_op jit(solution)/shard_map/conv_general_dilated | solution.py:120
  23.5 1.2 %fusion.4 = f32[2,2,8,9,192]{4,2,3,1,0:T(8,128)S(1)} fusion(bf16[3,3,3,384,192]{3,4,2,1,0:T(8,128)(2,1)S(1)} %copy-done.3, bf16[2,4,1,7,2,384]{5,3,4,1,0,2:T(8,128)(2,1)S(1)} %slice.14, bf16[2,4,1,8,9,384]{5,3,4,1,0,2:T(8,128)(2,1)S(1)} %copy.35, pred[8,9]{0,1:T(8,128)(4,1)S(1)} %copy-done.4), kind=kOutput, calls=%fused_computation.6 | convolution fusion | flops 574986240 | bytes 3418112 | tf_op jit(solution)/shard_map/conv_general_dilated | solution.py:120
  24.8 0.2 copy.36
  25.0 0.1 copy.38
  25.2 3.5 %collective-permute-start.3 = (bf16[2,2,64,192]{3,2,1,0:T(8,128)(2,1)S(1)}, bf16[2,2,64,192]{3,2,1,0:T(8,128)(2,1)S(1)}, u32[]{:S(2)}, u32[]{:S(2)}) collective-permute-start(bf16[2,2,64,192]{3,2,1,0:T(8,128)(2,1)S(1)} %bitcast.41), channel_id=1, source_target_pairs={{0,2},{1,3},{4,6},{5,7},{8,10},{9,11},{12,14},{13,15},{16,18},{17,... | collective-permute-start | bytes 294920 | tf_op jit(solution)/shard_map/ppermute | solution.py:175
  28.8 2.9 %collective-permute-done.3 = bf16[2,2,64,192]{3,2,1,0:T(8,128)(2,1)S(1)} collective-permute-done((bf16[2,2,64,192]{3,2,1,0:T(8,128)(2,1)S(1)}, bf16[2,2,64,192]{3,2,1,0:T(8,128)(2,1)S(1)}, u32[]{:S(2)}, u32[]{:S(2)}) %collective-permute-start.3) | collective-permute-done | bytes 98336 | tf_op jit(solution)/shard_map/ppermute | solution.py:175
  31.7 0.7 %add_convert_fusion = bf16[2,2,64,192]{3,2,1,0:T(8,128)(2,1)} fusion(f32[2,2,64,192]{3,2,1,0:T(8,128)S(1)} %fusion.16, bf16[2,2,64,192]{3,2,1,0:T(8,128)(2,1)S(1)} %collective-permute-done.3), kind=kLoop, calls=%fused_computation.17 | loop fusion | flops 147456 | bytes 393216 | tf_op jit(solution)/shard_map/convert_element_type | solution.py:181
  (22 shorter events, 0.8 us)
Async XLA Ops:
  0.0 0.9 %copy-start = (bf16[1,64,4,384]{3,2,1,0:T(4,128)(2,1)S(1)}, bf16[1,64,4,384]{3,2,1,0:T(4,128)(2,1)}, u32[]{:S(2)}) copy-start(bf16[1,64,4,384]{3,2,1,0:T(4,128)(2,1)} %param.5) | copy-start | bytes 589828
  1.0 12.0 %collective-permute-start.1 = (bf16[32,4,384]{2,0,1:T(8,128)(2,1)S(1)}, bf16[32,4,384]{2,0,1:T(8,128)(2,1)S(1)}, u32[]{:S(2)}, u32[]{:S(2)}) collective-permute-start(bf16[32,4,384]{2,0,1:T(8,128)(2,1)S(1)} %bitcast.38), channel_id=1, source_target_pairs={{0,8},{4,12},{8,0},{12,4},{1,9},{5,13},{9,1},{13,5},{2,10},{6,14},... | collective-permute-start | bytes 294920 | tf_op jit(solution)/shard_map/ppermute | solution.py:135
  5.1 7.9 %collective-permute-start = (bf16[32,4,384]{2,0,1:T(8,128)(2,1)S(1)}, bf16[32,4,384]{2,0,1:T(8,128)(2,1)S(1)}, u32[]{:S(2)}, u32[]{:S(2)}) collective-permute-start(bf16[32,4,384]{2,0,1:T(8,128)(2,1)S(1)} %bitcast.39), channel_id=1, source_target_pairs={{0,4},{4,8},{8,12},{12,0},{1,5},{5,9},{9,13},{13,1},{2,6},{6,10},{... | collective-permute-start | bytes 294920 | tf_op jit(solution)/shard_map/ppermute | solution.py:135
  6.7 7.0 %collective-permute-start.2 = (bf16[32,4,384]{2,0,1:T(8,128)(2,1)S(1)}, bf16[32,4,384]{2,0,1:T(8,128)(2,1)S(1)}, u32[]{:S(2)}, u32[]{:S(2)}) collective-permute-start(bf16[32,4,384]{2,0,1:T(8,128)(2,1)S(1)} %bitcast.40), channel_id=1, source_target_pairs={{0,12},{4,0},{8,4},{12,8},{1,13},{5,1},{9,5},{13,9},{2,14},{6,2},{... | collective-permute-start | bytes 294920 | tf_op jit(solution)/shard_map/ppermute | solution.py:135
  17.4 1.1 %copy-start.1 = (bf16[384,768]{1,0:T(8,128)(2,1)S(1)}, bf16[384,768]{1,0:T(8,128)(2,1)}, u32[]{:S(2)}) copy-start(bf16[384,768]{1,0:T(8,128)(2,1)} %wkv_ref.1) | copy-start | bytes 1769476
  17.4 1.1 %copy-start.2 = (bf16[384,384]{1,0:T(8,128)(2,1)S(1)}, bf16[384,384]{1,0:T(8,128)(2,1)}, u32[]{:S(2)}) copy-start(bf16[384,384]{1,0:T(8,128)(2,1)} %wq_ref.1) | copy-start | bytes 884740
  18.6 3.6 %copy-start.3 = (bf16[3,3,3,384,192]{3,4,2,1,0:T(8,128)(2,1)S(1)}, bf16[3,3,3,384,192]{3,4,2,1,0:T(8,128)(2,1)}, u32[]{:S(2)}) copy-start(bf16[3,3,3,384,192]{3,4,2,1,0:T(8,128)(2,1)} %param.9) | copy-start | bytes 11943940
  21.6 0.7 %copy-start.4 = (pred[8,9]{0,1:T(8,128)(4,1)S(1)}, pred[8,9]{0,1:T(8,128)(4,1)}, u32[]{:S(2)}) copy-start(pred[8,9]{0,1:T(8,128)(4,1)} %constant.108) | copy-start | bytes 220
  25.2 6.5 %collective-permute-start.3 = (bf16[2,2,64,192]{3,2,1,0:T(8,128)(2,1)S(1)}, bf16[2,2,64,192]{3,2,1,0:T(8,128)(2,1)S(1)}, u32[]{:S(2)}, u32[]{:S(2)}) collective-permute-start(bf16[2,2,64,192]{3,2,1,0:T(8,128)(2,1)S(1)} %bitcast.41), channel_id=1, source_target_pairs={{0,2},{1,3},{4,6},{5,7},{8,10},{9,11},{12,14},{13,15},{16,18},{17,... | collective-permute-start | bytes 294920 | tf_op jit(solution)/shard_map/ppermute | solution.py:175

commit v13 on v11

--- a/solution.py
+++ b/solution.py
@@ -138,6 +138,7 @@
     share = block // chan_count
     own_share = lax.dynamic_slice_in_dim(latent_tiles, chan_index * share, share, 1)
     every_tile = lax.all_gather(own_share, ("patch", "chan"), axis=1, tiled=True)[0]
+    every_tile, table = lax.optimization_barrier((every_tile, table))
     tile_total = every_tile.shape[0]
     rows = patch_count * RD
     per_owner = tile_total // patch_count

time: 32.3 us -> 32.2 us (level)
  local copies, waits for them, and re-layouts: 2.11 us -> 2.84 us
  other arithmetic: 1.53 us -> 0.82 us
    unnamed x12 -> x14, local copies, waits for them, and re-layouts: 0.68 us -> 1.41 us
    add x1, other arithmetic: 0.74 us -> 0.02 us  [local(): spot // per_frame * (tile_total // FD) + owner * per_frame]
where the time goes in v13:
time: 32.2 us; the launch traced here: 32 us
  blocking collectives  17.2 us (53%)
  starting transfers between devices  3.4 us (11%)
  Pallas kernels  3.03 us (9%)
  matrix products  2.85 us (9%)
  local copies, waits for them, and re-layouts  2.84 us (9%)
  waiting for transfers between devices  1.7 us (5%)
  other arithmetic  0.82 us (3%)
    all_gather x1, blocking collectives, local(): lax.all_gather(own_share, ('patch', 'chan'), axis=1, tiled=True)[0]  17.2 us
    ppermute x1, starting transfers between devices, local(): from_prev = lax.ppermute(to_next, 'span', pairs)  3.4 us
    pallas_call x1, Pallas kernels, attend_frames(): pl.pallas_call(attention_kernel, grid_spec=grid_spec, compiler_params=plt...  3.03 us
    conv_general_dilated x2, matrix products, timed_conv(): lax.conv_general_dilated(frames[None], kernel, (1, 1, 1), (time_pad, (0,...  2.47 us
    ppermute x1, waiting for transfers between devices, local(): from_prev = lax.ppermute(to_next, 'span', pairs)  1.7 us
    unnamed x14, local copies, waits for them, and re-layouts  1.41 us
    convert_element_type x1, other arithmetic, local(): return (base + from_prev.astype(jnp.float32)).astype(jnp.bfloat16)  0.68 us
  transfers between devices with their start and end apart: 1, of which 1 were waited for; matrix products, arithmetic and copies ran while one was open for 5% of the time, Pallas kernels for 0%

profile of v13, /device:TPU:0, one launch (start us, length us, event | category | flops | bytes accessed | tf_op | source)
XLA Modules:
  0.0 32.0 jit_solution(10363513913897308893)
XLA Ops:
  0.0 0.9 %copy-done = bf16[1,64,4,384]{3,2,1,0:T(4,128)(2,1)S(1)} copy-done((bf16[1,64,4,384]{3,2,1,0:T(4,128)(2,1)S(1)}, bf16[1,64,4,384]{3,2,1,0:T(4,128)(2,1)}, u32[]{:S(2)}) %copy-start) | copy-done | bytes 196632
  1.0 17.2 %all_gather.3 = bf16[1,256,4,384]{3,2,0,1:T(4,128)(2,1)S(1)} all-gather(bf16[1,32,4,384]{3,2,0,1:T(4,128)(2,1)S(1)} %constant_dynamic-slice_fusion), channel_id=1, replica_groups=mesh['clips'=2,'patch'=4,'span'=2,'chan'=2] {'patch','chan'}, dimensions={1}, use_global_device_ids=true | all-gather | bytes 884736 | tf_op jit(solution)/shard_map/all_gather | solution.py:140
  18.2 0.1 copy.31
  18.3 0.0 copy-start.1
  18.4 0.0 copy-start.2
  18.4 0.4 %convolution_convert_fusion = bf16[256,1536]{1,0:T(8,128)(2,1)S(1)} fusion(bf16[256,1536]{1,0:T(8,128)(2,1)S(1)} %bitcast.27, s32[256]{0:T(256)S(1)} %fusion.20), kind=kOutput, calls=%fused_computation.4 | convolution fusion | flops 201785344 | bytes 1573888 | tf_op jit(solution)/shard_map/dot_general | solution.py:151
  18.7 0.5 %reshape_reshape.3.cells_ref = bf16[2,512,384]{2,1,0:T(8,128)(2,1)S(1)} reshape(bf16[256,1536]{1,0:T(8,128)(2,1)S(1)} %convolution_convert_fusion) | data formatting | bytes 1572864 | tf_op jit(solution)/shard_map/reshape;reshape | solution.py:157
  19.2 0.2 copy-done.1
  19.4 0.1 copy-done.2
  19.5 3.0 %shard_map.55 = (bf16[2,128,384]{2,1,0:T(8,128)(2,1)S(1)}, bf16[2,256,384]{2,1,0:T(8,128)(2,1)S(1)}) custom-call(s32[1]{0:T(128)} %bitcast.first_ref, bf16[2,512,384]{2,1,0:T(8,128)(2,1)S(1)} %reshape_reshape.3.cells_ref, bf16[384,384]{1,0:T(8,128)(2,1)S(1)} %copy-done.2, bf16[384,768]{1,0:T(8,128)(2,1)S(1)} %copy-done.1), custom_call_target="tpu_custom_call" | custom-call | tf_op jit(solution)/shard_map/pallas_call | solution.py:108
  22.5 0.0 copy-start.5
  22.5 0.3 copy.22
  22.9 0.2 pad
  23.0 0.1 copy.24
  23.1 0.1 copy-done.5
  23.2 1.2 %fusion.10 = bf16[2,2,8,9,192]{4,2,3,1,0:T(8,128)(2,1)S(1)} fusion(bf16[3,3,3,384,192]{3,4,2,1,0:T(8,128)(2,1)S(1)} %copy-done.4, bf16[2,4,1,7,2,384]{5,3,4,1,0,2:T(8,128)(2,1)S(1)} %slice.12, bf16[2,4,1,8,9,384]{5,3,4,1,0,2:T(8,128)(2,1)S(1)} %copy.24, pred[8,9]{0,1:T(8,128)(4,1)S(1)} %copy-done.5), kind=kOutput, calls=%fused_computation.7 | convolution fusion | flops 575041536 | bytes 3307520 | tf_op jit(solution)/shard_map/conv_general_dilated | solution.py:120
  24.5 0.1 copy.27
  24.6 0.1 slice.14
  24.7 3.4 %collective-permute-start = (bf16[2,2,64,192]{3,2,1,0:T(8,128)(2,1)S(1)}, bf16[2,2,64,192]{3,2,1,0:T(8,128)(2,1)S(1)}, u32[]{:S(2)}, u32[]{:S(2)}) collective-permute-start(bf16[2,2,64,192]{3,2,1,0:T(8,128)(2,1)S(1)} %bitcast.31), channel_id=1, source_target_pairs={{0,2},{1,3},{4,6},{5,7},{8,10},{9,11},{12,14},{13,15},{16,18},{17,... | collective-permute-start | bytes 294920 | tf_op jit(solution)/shard_map/ppermute | solution.py:162
  28.1 1.2 %fusion.4 = f32[2,2,8,9,192]{4,2,3,1,0:T(8,128)S(1)} fusion(bf16[3,3,3,384,192]{3,4,2,1,0:T(8,128)(2,1)S(1)} %copy-done.4, bf16[2,4,1,7,2,384]{5,3,4,1,0,2:T(8,128)(2,1)S(1)} %slice.12, bf16[2,4,1,8,9,384]{5,3,4,1,0,2:T(8,128)(2,1)S(1)} %copy.24, pred[8,9]{0,1:T(8,128)(4,1)S(1)} %copy-done.5), kind=kOutput, calls=%fused_computation.5 | convolution fusion | flops 574986240 | bytes 3418112 | tf_op jit(solution)/shard_map/conv_general_dilated | solution.py:120
  29.4 0.2 copy.25
  29.5 0.1 fusion.16
  29.7 1.7 %collective-permute-done = bf16[2,2,64,192]{3,2,1,0:T(8,128)(2,1)S(1)} collective-permute-done((bf16[2,2,64,192]{3,2,1,0:T(8,128)(2,1)S(1)}, bf16[2,2,64,192]{3,2,1,0:T(8,128)(2,1)S(1)}, u32[]{:S(2)}, u32[]{:S(2)}) %collective-permute-start) | collective-permute-done | bytes 98336 | tf_op jit(solution)/shard_map/ppermute | solution.py:162
  31.4 0.7 %add_convert_fusion = bf16[2,2,64,192]{3,2,1,0:T(8,128)(2,1)} fusion(f32[2,2,64,192]{3,2,1,0:T(8,128)S(1)} %fusion.16, bf16[2,2,64,192]{3,2,1,0:T(8,128)(2,1)S(1)} %collective-permute-done), kind=kLoop, calls=%fused_computation.14 | loop fusion | flops 147456 | bytes 393216 | tf_op jit(solution)/shard_map/convert_element_type | solution.py:168
  (10 shorter events, 0.1 us)
Async XLA Ops:
  0.0 0.9 %copy-start = (bf16[1,64,4,384]{3,2,1,0:T(4,128)(2,1)S(1)}, bf16[1,64,4,384]{3,2,1,0:T(4,128)(2,1)}, u32[]{:S(2)}) copy-start(bf16[1,64,4,384]{3,2,1,0:T(4,128)(2,1)} %param.5) | copy-start | bytes 589828
  0.0 18.3 %copy-start.3 = (s32[1,256]{1,0:T(1,128)S(1)}, s32[1,256]{1,0:T(1,128)}, u32[]{:S(2)}) copy-start(s32[1,256]{1,0:T(1,128)} %param.6) | copy-start | bytes 3076
  18.3 1.1 %copy-start.1 = (bf16[384,768]{1,0:T(8,128)(2,1)S(1)}, bf16[384,768]{1,0:T(8,128)(2,1)}, u32[]{:S(2)}) copy-start(bf16[384,768]{1,0:T(8,128)(2,1)} %wkv_ref.1) | copy-start | bytes 1769476
  18.4 1.1 %copy-start.2 = (bf16[384,384]{1,0:T(8,128)(2,1)S(1)}, bf16[384,384]{1,0:T(8,128)(2,1)}, u32[]{:S(2)}) copy-start(bf16[384,384]{1,0:T(8,128)(2,1)} %wq_ref.1) | copy-start | bytes 884740
  19.5 3.6 %copy-start.4 = (bf16[3,3,3,384,192]{3,4,2,1,0:T(8,128)(2,1)S(1)}, bf16[3,3,3,384,192]{3,4,2,1,0:T(8,128)(2,1)}, u32[]{:S(2)}) copy-start(bf16[3,3,3,384,192]{3,4,2,1,0:T(8,128)(2,1)} %param.9) | copy-start | bytes 11943940
  22.5 0.7 %copy-start.5 = (pred[8,9]{0,1:T(8,128)(4,1)S(1)}, pred[8,9]{0,1:T(8,128)(4,1)}, u32[]{:S(2)}) copy-start(pred[8,9]{0,1:T(8,128)(4,1)} %constant.79) | copy-start | bytes 220
  24.7 6.7 %collective-permute-start = (bf16[2,2,64,192]{3,2,1,0:T(8,128)(2,1)S(1)}, bf16[2,2,64,192]{3,2,1,0:T(8,128)(2,1)S(1)}, u32[]{:S(2)}, u32[]{:S(2)}) collective-permute-start(bf16[2,2,64,192]{3,2,1,0:T(8,128)(2,1)S(1)} %bitcast.31), channel_id=1, source_target_pairs={{0,2},{1,3},{4,6},{5,7},{8,10},{9,11},{12,14},{13,15},{16,18},{17,... | collective-permute-start | bytes 294920 | tf_op jit(solution)/shard_map/ppermute | solution.py:162

commit v14 on v11

--- a/solution.py
+++ b/solution.py
@@ -23,6 +23,11 @@
 
 
 def attention_kernel(first_ref, cells_ref, wq_ref, wkv_ref, mixed_ref, act_ref):
+    for frame in range(cells_ref.shape[0]):
+        attend_frame(first_ref, cells_ref, wq_ref, wkv_ref, mixed_ref, act_ref, frame)
+
+
+def attend_frame(first_ref, cells_ref, wq_ref, wkv_ref, mixed_ref, act_ref, frame):
     width = wq_ref.shape[0]
     scale = 1.0 / math.sqrt(width)
     count = cells_ref.shape[1]
@@ -34,9 +39,9 @@
     below = jnp.minimum(first + 1 + own // line, frame_rows - 1) * line
     feats = jnp.concatenate(
         [
-            cells_ref[0, pl.ds(top, line), :],
-            cells_ref[0, pl.ds((first + 1) * line, own), :],
-            cells_ref[0, pl.ds(below, line), :],
+            cells_ref[frame, pl.ds(top, line), :],
+            cells_ref[frame, pl.ds((first + 1) * line, own), :],
+            cells_ref[frame, pl.ds(below, line), :],
         ],
         axis=0,
     ).astype(jnp.float32)
@@ -47,7 +52,7 @@
 
     def fold(step, carry):
         run_max, run_total, run_acc = carry
-        cells = cells_ref[0, pl.ds(step * block, block), :]
+        cells = cells_ref[frame, pl.ds(step * block, block), :]
         keyvals = jnp.dot(
             scaled_rms(cells).astype(jnp.bfloat16), wkv_ref[...], preferred_element_type=jnp.float32
         ).astype(jnp.bfloat16)
@@ -79,11 +84,11 @@
         carry = fold(step, carry)
     _, run_total, run_acc = carry
     mixed = (feats + run_acc / run_total).astype(jnp.bfloat16)
-    mixed_ref[0] = mixed[line : line + own]
+    mixed_ref[frame] = mixed[line : line + own]
     normed = scaled_rms(mixed)
     row_of = lax.broadcasted_iota(jnp.int32, (rows, width), 0) // line + first
     inside = (row_of >= 0) & (row_of < frame_rows)
-    act_ref[0] = jnp.where(inside, normed / (1.0 + jnp.exp(-normed)), 0.0).astype(jnp.bfloat16)
+    act_ref[frame] = jnp.where(inside, normed / (1.0 + jnp.exp(-normed)), 0.0).astype(jnp.bfloat16)
 
 
 def attend_frames(first, cells, ext_rows, w_query, w_keyval):
@@ -93,22 +98,22 @@
     per_frame = lambda f, first_ref: (f, 0, 0)
     grid_spec = pltpu.PrefetchScalarGridSpec(
         num_scalar_prefetch=1,
-        grid=(frames,),
+        grid=(1,),
         in_specs=[
-            pl.BlockSpec((1, count, width), per_frame),
+            pl.BlockSpec((frames, count, width), per_frame),
             pl.BlockSpec(w_query.shape, fixed),
             pl.BlockSpec(w_keyval.shape, fixed),
         ],
         out_specs=[
-            pl.BlockSpec((1, own, width), per_frame),
-            pl.BlockSpec((1, ext_rows, width), per_frame),
+            pl.BlockSpec((frames, own, width), per_frame),
+            pl.BlockSpec((frames, ext_rows, width), per_frame),
         ],
     )
     block_bytes = count * width * 2
     return pl.pallas_call(
         attention_kernel,
         grid_spec=grid_spec,
-        compiler_params=pltpu.CompilerParams(vmem_limit_bytes=6 * block_bytes + (6 << 20)),
+        compiler_params=pltpu.CompilerParams(vmem_limit_bytes=6 * frames * block_bytes + (6 << 20)),
         out_shape=[
             jax.ShapeDtypeStruct((frames, own, width), jnp.bfloat16),
             jax.ShapeDtypeStruct((frames, ext_rows, width), jnp.bfloat16),

time: 32.3 us -> 31.9 us (0.988)
  no operation moved by 1% of the time
where the time goes in v14:
time: 31.9 us; the launch traced here: 31.7 us
  blocking collectives  17.2 us (54%)
  starting transfers between devices  3.4 us (11%)
  matrix products  2.85 us (9%)
  Pallas kernels  2.74 us (9%)
  local copies, waits for them, and re-layouts  2.11 us (7%)
  waiting for transfers between devices  1.69 us (5%)
  other arithmetic  1.53 us (5%)
    all_gather x1, blocking collectives, local(): lax.all_gather(own_share, ('patch', 'chan'), axis=1, tiled=True)[0]  17.2 us
    ppermute x1, starting transfers between devices, local(): from_prev = lax.ppermute(to_next, 'span', pairs)  3.4 us
    pallas_call x1, Pallas kernels, attend_frames(): pl.pallas_call(attention_kernel, grid_spec=grid_spec, compiler_params=plt...  2.74 us
    conv_general_dilated x2, matrix products, timed_conv(): lax.conv_general_dilated(frames[None], kernel, (1, 1, 1), (time_pad, (0,...  2.48 us
    ppermute x1, waiting for transfers between devices, local(): from_prev = lax.ppermute(to_next, 'span', pairs)  1.69 us
    add x1, other arithmetic, local(): spot // per_frame * (tile_total // FD) + owner * per_frame  0.74 us
    convert_element_type x1, other arithmetic, local(): return (base + from_prev.astype(jnp.float32)).astype(jnp.bfloat16)  0.68 us
    unnamed x12, local copies, waits for them, and re-layouts  0.68 us
  transfers between devices with their start and end apart: 1, of which 1 were waited for; matrix products, arithmetic and copies ran while one was open for 5% of the time, Pallas kernels for 0%

profile of v14, /device:TPU:0, one launch (start us, length us, event | category | flops | bytes accessed | tf_op | source)
XLA Modules:
  0.0 31.7 jit_solution(8311909398755272279)
XLA Ops:
  0.0 0.7 %fusion.20 = s32[1,256]{1,0:T(1,128)S(1)} fusion(s32[1,256]{1,0:T(1,128)} %param.6), kind=kLoop, calls=%fused_computation.28 | loop fusion | flops 10752 | bytes 2048 | tf_op jit(solution)/shard_map/add | solution.py:152
  0.7 0.2 copy-done
  1.0 17.2 %all_gather.3 = bf16[1,256,4,384]{3,2,0,1:T(4,128)(2,1)S(1)} all-gather(bf16[1,32,4,384]{3,2,0,1:T(4,128)(2,1)S(1)} %constant_dynamic-slice_fusion), channel_id=1, replica_groups=mesh['clips'=2,'patch'=4,'span'=2,'chan'=2] {'patch','chan'}, dimensions={1}, use_global_device_ids=true | all-gather | bytes 884736 | tf_op jit(solution)/shard_map/all_gather | solution.py:145
  18.2 0.1 copy.31
  18.3 0.0 copy-start.1
  18.3 0.4 %convolution_convert_fusion = bf16[256,1536]{1,0:T(8,128)(2,1)S(1)} fusion(bf16[256,1536]{1,0:T(8,128)(2,1)S(1)} %bitcast.28, s32[256]{0:T(256)S(1)} %bitcast.33), kind=kOutput, calls=%fused_computation.4 | convolution fusion | flops 201785344 | bytes 1573888 | tf_op jit(solution)/shard_map/dot_general | solution.py:155
  18.7 0.5 %reshape_reshape.3.cells_ref = bf16[2,512,384]{2,1,0:T(8,128)(2,1)S(1)} reshape(bf16[256,1536]{1,0:T(8,128)(2,1)S(1)} %convolution_convert_fusion) | data formatting | bytes 1572864 | tf_op jit(solution)/shard_map/reshape;reshape | solution.py:161
  19.2 0.2 copy-done.1
  19.4 0.1 copy-done.2
  19.5 2.7 %shard_map.55 = (bf16[2,128,384]{2,1,0:T(8,128)(2,1)S(1)}, bf16[2,256,384]{2,1,0:T(8,128)(2,1)S(1)}) custom-call(s32[1]{0:T(128)} %bitcast.first_ref, bf16[2,512,384]{2,1,0:T(8,128)(2,1)S(1)} %reshape_reshape.3.cells_ref, bf16[384,384]{1,0:T(8,128)(2,1)S(1)} %copy-done.2, bf16[384,768]{1,0:T(8,128)(2,1)S(1)} %copy-done.1), custom_call_target="tpu_custom_call" | custom-call | tf_op jit(solution)/shard_map/pallas_call | solution.py:113
  22.2 0.0 copy-start.4
  22.2 0.3 copy.22
  22.5 0.2 pad
  22.7 0.1 copy.24
  22.8 0.1 copy-done.4
  22.9 1.2 %fusion.10 = bf16[2,2,8,9,192]{4,2,3,1,0:T(8,128)(2,1)S(1)} fusion(bf16[3,3,3,384,192]{3,4,2,1,0:T(8,128)(2,1)S(1)} %copy-done.3, bf16[2,4,1,7,2,384]{5,3,4,1,0,2:T(8,128)(2,1)S(1)} %slice.12, bf16[2,4,1,8,9,384]{5,3,4,1,0,2:T(8,128)(2,1)S(1)} %copy.24, pred[8,9]{0,1:T(8,128)(4,1)S(1)} %copy-done.4), kind=kOutput, calls=%fused_computation.7 | convolution fusion | flops 575041536 | bytes 3307520 | tf_op jit(solution)/shard_map/conv_general_dilated | solution.py:125
  24.2 0.1 copy.27
  24.3 0.1 slice.14
  24.4 3.4 %collective-permute-start = (bf16[2,2,64,192]{3,2,1,0:T(8,128)(2,1)S(1)}, bf16[2,2,64,192]{3,2,1,0:T(8,128)(2,1)S(1)}, u32[]{:S(2)}, u32[]{:S(2)}) collective-permute-start(bf16[2,2,64,192]{3,2,1,0:T(8,128)(2,1)S(1)} %bitcast.32), channel_id=1, source_target_pairs={{0,2},{1,3},{4,6},{5,7},{8,10},{9,11},{12,14},{13,15},{16,18},{17,... | collective-permute-start | bytes 294920 | tf_op jit(solution)/shard_map/ppermute | solution.py:166
  27.8 1.2 %fusion.4 = f32[2,2,8,9,192]{4,2,3,1,0:T(8,128)S(1)} fusion(bf16[3,3,3,384,192]{3,4,2,1,0:T(8,128)(2,1)S(1)} %copy-done.3, bf16[2,4,1,7,2,384]{5,3,4,1,0,2:T(8,128)(2,1)S(1)} %slice.12, bf16[2,4,1,8,9,384]{5,3,4,1,0,2:T(8,128)(2,1)S(1)} %copy.24, pred[8,9]{0,1:T(8,128)(4,1)S(1)} %copy-done.4), kind=kOutput, calls=%fused_computation.5 | convolution fusion | flops 574986240 | bytes 3418112 | tf_op jit(solution)/shard_map/conv_general_dilated | solution.py:125
  29.1 0.2 copy.25
  29.2 0.1 fusion.16
  29.4 1.7 %collective-permute-done = bf16[2,2,64,192]{3,2,1,0:T(8,128)(2,1)S(1)} collective-permute-done((bf16[2,2,64,192]{3,2,1,0:T(8,128)(2,1)S(1)}, bf16[2,2,64,192]{3,2,1,0:T(8,128)(2,1)S(1)}, u32[]{:S(2)}, u32[]{:S(2)}) %collective-permute-start) | collective-permute-done | bytes 98336 | tf_op jit(solution)/shard_map/ppermute | solution.py:166
  31.1 0.7 %add_convert_fusion = bf16[2,2,64,192]{3,2,1,0:T(8,128)(2,1)} fusion(f32[2,2,64,192]{3,2,1,0:T(8,128)S(1)} %fusion.16, bf16[2,2,64,192]{3,2,1,0:T(8,128)(2,1)S(1)} %collective-permute-done), kind=kLoop, calls=%fused_computation.14 | loop fusion | flops 147456 | bytes 393216 | tf_op jit(solution)/shard_map/convert_element_type | solution.py:172
  (8 shorter events, 0.1 us)
Async XLA Ops:
  0.0 0.9 %copy-start = (bf16[1,64,4,384]{3,2,1,0:T(4,128)(2,1)S(1)}, bf16[1,64,4,384]{3,2,1,0:T(4,128)(2,1)}, u32[]{:S(2)}) copy-start(bf16[1,64,4,384]{3,2,1,0:T(4,128)(2,1)} %param.5) | copy-start | bytes 589828
  18.3 1.1 %copy-start.1 = (bf16[384,768]{1,0:T(8,128)(2,1)S(1)}, bf16[384,768]{1,0:T(8,128)(2,1)}, u32[]{:S(2)}) copy-start(bf16[384,768]{1,0:T(8,128)(2,1)} %wkv_ref.1) | copy-start | bytes 1769476
  18.3 1.1 %copy-start.2 = (bf16[384,384]{1,0:T(8,128)(2,1)S(1)}, bf16[384,384]{1,0:T(8,128)(2,1)}, u32[]{:S(2)}) copy-start(bf16[384,384]{1,0:T(8,128)(2,1)} %wq_ref.1) | copy-start | bytes 884740
  19.5 3.3 %copy-start.3 = (bf16[3,3,3,384,192]{3,4,2,1,0:T(8,128)(2,1)S(1)}, bf16[3,3,3,384,192]{3,4,2,1,0:T(8,128)(2,1)}, u32[]{:S(2)}) copy-start(bf16[3,3,3,384,192]{3,4,2,1,0:T(8,128)(2,1)} %param.9) | copy-start | bytes 11943940
  22.2 0.7 %copy-start.4 = (pred[8,9]{0,1:T(8,128)(4,1)S(1)}, pred[8,9]{0,1:T(8,128)(4,1)}, u32[]{:S(2)}) copy-start(pred[8,9]{0,1:T(8,128)(4,1)} %constant.79) | copy-start | bytes 220
  24.4 6.7 %collective-permute-start = (bf16[2,2,64,192]{3,2,1,0:T(8,128)(2,1)S(1)}, bf16[2,2,64,192]{3,2,1,0:T(8,128)(2,1)S(1)}, u32[]{:S(2)}, u32[]{:S(2)}) collective-permute-start(bf16[2,2,64,192]{3,2,1,0:T(8,128)(2,1)S(1)} %bitcast.32), channel_id=1, source_target_pairs={{0,2},{1,3},{4,6},{5,7},{8,10},{9,11},{12,14},{13,15},{16,18},{17,... | collective-permute-start | bytes 294920 | tf_op jit(solution)/shard_map/ppermute | solution.py:166

commit v15 on v9

--- a/solution.py
+++ b/solution.py
@@ -23,6 +23,11 @@
 
 
 def attention_kernel(first_ref, tiles_ref, wq_ref, wkv_ref, mixed_ref, act_ref):
+    for frame in range(tiles_ref.shape[0]):
+        attend_frame(first_ref, tiles_ref, wq_ref, wkv_ref, mixed_ref, act_ref, frame)
+
+
+def attend_frame(first_ref, tiles_ref, wq_ref, wkv_ref, mixed_ref, act_ref, frame):
     width = wq_ref.shape[0]
     scale = 1.0 / math.sqrt(width)
     cell = tiles_ref.shape[2] // width
@@ -36,9 +41,9 @@
     below = jnp.minimum(first + 1 + own // line, frame_rows - 1) * across
     picked = jnp.concatenate(
         [
-            tiles_ref[0, pl.ds(top, across), :],
-            tiles_ref[0, pl.ds((first + 1) * across, own // cell), :],
-            tiles_ref[0, pl.ds(below, across), :],
+            tiles_ref[frame, pl.ds(top, across), :],
+            tiles_ref[frame, pl.ds((first + 1) * across, own // cell), :],
+            tiles_ref[frame, pl.ds(below, across), :],
         ],
         axis=0,
     )
@@ -60,7 +65,7 @@
 
     def fold(step, carry):
         run_max, run_total, run_acc = carry
-        group = tiles_ref[0, pl.ds(step * chunk, chunk), :]
+        group = tiles_ref[frame, pl.ds(step * chunk, chunk), :]
         cells = jnp.concatenate(
             [group[:, i * width : (i + 1) * width] for i in range(cell)], axis=0
         )
@@ -94,11 +99,11 @@
         carry = fold(step, carry)
     _, run_total, run_acc = carry
     mixed = (feats + run_acc / run_total).astype(jnp.bfloat16)
-    mixed_ref[0] = mixed[line : line + own]
+    mixed_ref[frame] = mixed[line : line + own]
     normed = scaled_rms(mixed)
     row_of = lax.broadcasted_iota(jnp.int32, (rows, width), 0) // line + first
     inside = (row_of >= 0) & (row_of < frame_rows)
-    act_ref[0] = jnp.where(inside, normed / (1.0 + jnp.exp(-normed)), 0.0).astype(jnp.bfloat16)
+    act_ref[frame] = jnp.where(inside, normed / (1.0 + jnp.exp(-normed)), 0.0).astype(jnp.bfloat16)
 
 
 def attend_frames(first, tiles, ext_rows, w_query, w_keyval):
@@ -109,20 +114,22 @@
     per_frame = lambda f, first_ref: (f, 0, 0)
     grid_spec = pltpu.PrefetchScalarGridSpec(
         num_scalar_prefetch=1,
-        grid=(frames,),
+        grid=(1,),
         in_specs=[
-            pl.BlockSpec((1, count, packed), per_frame),
+            pl.BlockSpec((frames, count, packed), per_frame),
             pl.BlockSpec(w_query.shape, fixed),
             pl.BlockSpec(w_keyval.shape, fixed),
         ],
         out_specs=[
-            pl.BlockSpec((1, own, width), per_frame),
-            pl.BlockSpec((1, ext_rows, width), per_frame),
-        ],
-    )
+            pl.BlockSpec((frames, own, width), per_frame),
+            pl.BlockSpec((frames, ext_rows, width), per_frame),
+        ],
+    )
+    block_bytes = count * packed * 2
     return pl.pallas_call(
         attention_kernel,
         grid_spec=grid_spec,
+        compiler_params=pltpu.CompilerParams(vmem_limit_bytes=6 * frames * block_bytes + (6 << 20)),
         out_shape=[
             jax.ShapeDtypeStruct((frames, own, width), jnp.bfloat16),
             jax.ShapeDtypeStruct((frames, ext_rows, width), jnp.bfloat16),
@@ -176,8 +183,8 @@
     out_width = conv_weight.shape[-1]
     own_rows = mixed_own.reshape(FD, RD, W, C)
     own_channels = lax.dynamic_slice_in_dim(own_rows, chan_index * out_width, out_width, 3)
-    total = own_channels.astype(jnp.float32) + own_sum + from_prev.astype(jnp.float32)
-    return total.astype(jnp.bfloat16)
+    base = lax.optimization_barrier(own_channels.astype(jnp.float32) + own_sum)
+    return (base + from_prev.astype(jnp.float32)).astype(jnp.bfloat16)
 
 
 def solution(mesh):

time: 38.3 us -> 32.7 us (0.85)
  matrix products: 5.63 us -> 2.85 us
  Pallas kernels: 5.78 us -> 3.66 us
  local copies, waits for them, and re-layouts: 3.06 us -> 2.02 us
  other arithmetic: 0.97 us -> 1.53 us
    pallas_call x1, Pallas kernels: 5.78 us -> 3.66 us  [attend_frames(): pl.pallas_call(attention_kernel, grid_spec=grid_spec, compiler_params=plt...]
    conv_general_dilated x2, matrix products: 4.36 us -> 2.48 us  [timed_conv(): lax.conv_general_dilated(frames[None], kernel, (1, 1, 1), (time_pad, (0,...]
    another operation x2, local copies, waits for them, and re-layouts: 1.48 us -> 0.47 us  [timed_conv(): frames[None]]
    dot_general x1, matrix products: 1.27 us -> 0.37 us  [local(): jnp.dot(one_hot, every_tile.reshape(tile_total, -1), preferred_element_ty...]
    unnamed x9 -> x12, local copies, waits for them, and re-layouts: 0.32 us -> 1.05 us
    convert_element_type x1 -> x0, local copies, waits for them, and re-layouts: 0.67 us -> none  [local(): return total.astype(jnp.bfloat16)]
    convert_element_type x1, other arithmetic: 0.23 us -> 0.68 us  [local(): return (base + from_prev.astype(jnp.float32)).astype(jnp.bfloat16)]
  transfers between devices with their start and end apart: 1 -> 1, of which waited for: 1 -> 1; matrix products, arithmetic and copies ran while one was open for 4% -> 5% of each run, Pallas kernels for 0% -> 0%
where the time goes in v15:
time: 32.7 us; the launch traced here: 32.5 us
  blocking collectives  17.2 us (53%)
  Pallas kernels  3.66 us (11%)
  starting transfers between devices  3.41 us (10%)
  matrix products  2.85 us (9%)
  local copies, waits for them, and re-layouts  2.02 us (6%)
  waiting for transfers between devices  1.69 us (5%)
  other arithmetic  1.53 us (5%)
    all_gather x1, blocking collectives, local(): lax.all_gather(own_share, ('patch', 'chan'), axis=1, tiled=True)[0]  17.2 us
    pallas_call x1, Pallas kernels, attend_frames(): pl.pallas_call(attention_kernel, grid_spec=grid_spec, compiler_params=plt...  3.66 us
    ppermute x1, starting transfers between devices, local(): from_prev = lax.ppermute(to_next, 'span', pairs)  3.41 us
    conv_general_dilated x2, matrix products, timed_conv(): lax.conv_general_dilated(frames[None], kernel, (1, 1, 1), (time_pad, (0,...  2.48 us
    ppermute x1, waiting for transfers between devices, local(): from_prev = lax.ppermute(to_next, 'span', pairs)  1.69 us
    unnamed x12, local copies, waits for them, and re-layouts  1.05 us
    add x1, other arithmetic, local(): spot // per_frame * (tile_total // FD) + owner * per_frame  0.74 us
    convert_element_type x1, other arithmetic, local(): return (base + from_prev.astype(jnp.float32)).astype(jnp.bfloat16)  0.68 us
  transfers between devices with their start and end apart: 1, of which 1 were waited for; matrix products, arithmetic and copies ran while one was open for 5% of the time, Pallas kernels for 0%

profile of v15, /device:TPU:0, one launch (start us, length us, event | category | flops | bytes accessed | tf_op | source)
XLA Modules:
  0.0 32.5 jit_solution(2872300143378130442)
XLA Ops:
  0.0 0.0 copy-start
  0.0 0.7 %fusion.20 = s32[1,256]{1,0:T(1,128)S(1)} fusion(s32[1,256]{1,0:T(1,128)} %param.6), kind=kLoop, calls=%fused_computation.28 | loop fusion | flops 10752 | bytes 2048 | tf_op jit(solution)/shard_map/add | solution.py:168
  0.7 0.2 copy-done
  1.0 17.2 %all_gather.3 = bf16[1,256,4,384]{3,2,0,1:T(4,128)(2,1)S(1)} all-gather(bf16[1,32,4,384]{3,2,0,1:T(4,128)(2,1)S(1)} %constant_dynamic-slice_fusion), channel_id=1, replica_groups=mesh['clips'=2,'patch'=4,'span'=2,'chan'=2] {'patch','chan'}, dimensions={1}, use_global_device_ids=true | all-gather | bytes 884736 | tf_op jit(solution)/shard_map/all_gather | solution.py:161
  18.2 0.1 copy.31
  18.3 0.4 %convolution_convert_fusion = bf16[256,1536]{1,0:T(8,128)(2,1)S(1)} fusion(bf16[256,1536]{1,0:T(8,128)(2,1)S(1)} %bitcast.30, s32[256]{0:T(256)S(1)} %bitcast.35), kind=kOutput, calls=%fused_computation.4 | convolution fusion | flops 201785344 | bytes 1573888 | tf_op jit(solution)/shard_map/dot_general | solution.py:171
  18.7 0.6 %copy-done.1 = bf16[384,768]{1,0:T(8,128)(2,1)S(1)} copy-done((bf16[384,768]{1,0:T(8,128)(2,1)S(1)}, bf16[384,768]{1,0:T(8,128)(2,1)}, u32[]{:S(2)}) %copy-start.1) | copy-done | bytes 589848
  19.3 0.1 copy-done.2
  19.4 3.7 %shard_map.55 = (bf16[2,128,384]{2,1,0:T(8,128)(2,1)S(1)}, bf16[2,256,384]{2,1,0:T(8,128)(2,1)S(1)}) custom-call(s32[1]{0:T(128)} %bitcast.first_ref, bf16[2,128,1536]{2,1,0:T(8,128)(2,1)S(1)} %bitcast.26, bf16[384,384]{1,0:T(8,128)(2,1)S(1)} %copy-done.2, bf16[384,768]{1,0:T(8,128)(2,1)S(1)} %copy-done.1), custom_call_target="tpu_custom_call" | custom-call | tf_op jit(solution)/shard_map/pallas_call | solution.py:129
  23.0 0.0 copy-start.4
  23.0 0.3 copy.22
  23.3 0.2 pad
  23.5 0.1 copy.24
  23.6 0.0 copy-done.3
  23.6 0.1 copy-done.4
  23.7 1.2 %fusion.10 = bf16[2,2,8,9,192]{4,2,3,1,0:T(8,128)(2,1)S(1)} fusion(bf16[3,3,3,384,192]{3,4,2,1,0:T(8,128)(2,1)S(1)} %copy-done.3, bf16[2,4,1,7,2,384]{5,3,4,1,0,2:T(8,128)(2,1)S(1)} %slice.12, bf16[2,4,1,8,9,384]{5,3,4,1,0,2:T(8,128)(2,1)S(1)} %copy.24, pred[8,9]{0,1:T(8,128)(4,1)S(1)} %copy-done.4), kind=kOutput, calls=%fused_computation.7 | convolution fusion | flops 575041536 | bytes 3307520 | tf_op jit(solution)/shard_map/conv_general_dilated | solution.py:141
  24.9 0.1 copy.27
  25.1 0.1 slice.14
  25.2 3.4 %collective-permute-start = (bf16[2,2,64,192]{3,2,1,0:T(8,128)(2,1)S(1)}, bf16[2,2,64,192]{3,2,1,0:T(8,128)(2,1)S(1)}, u32[]{:S(2)}, u32[]{:S(2)}) collective-permute-start(bf16[2,2,64,192]{3,2,1,0:T(8,128)(2,1)S(1)} %bitcast.34), channel_id=1, source_target_pairs={{0,2},{1,3},{4,6},{5,7},{8,10},{9,11},{12,14},{13,15},{16,18},{17,... | collective-permute-start | bytes 294920 | tf_op jit(solution)/shard_map/ppermute | solution.py:181
  28.6 1.2 %fusion.4 = f32[2,2,8,9,192]{4,2,3,1,0:T(8,128)S(1)} fusion(bf16[3,3,3,384,192]{3,4,2,1,0:T(8,128)(2,1)S(1)} %copy-done.3, bf16[2,4,1,7,2,384]{5,3,4,1,0,2:T(8,128)(2,1)S(1)} %slice.12, bf16[2,4,1,8,9,384]{5,3,4,1,0,2:T(8,128)(2,1)S(1)} %copy.24, pred[8,9]{0,1:T(8,128)(4,1)S(1)} %copy-done.4), kind=kOutput, calls=%fused_computation.5 | convolution fusion | flops 574986240 | bytes 3418112 | tf_op jit(solution)/shard_map/conv_general_dilated | solution.py:141
  29.9 0.2 copy.25
  30.0 0.1 fusion.16
  30.2 1.7 %collective-permute-done = bf16[2,2,64,192]{3,2,1,0:T(8,128)(2,1)S(1)} collective-permute-done((bf16[2,2,64,192]{3,2,1,0:T(8,128)(2,1)S(1)}, bf16[2,2,64,192]{3,2,1,0:T(8,128)(2,1)S(1)}, u32[]{:S(2)}, u32[]{:S(2)}) %collective-permute-start) | collective-permute-done | bytes 98336 | tf_op jit(solution)/shard_map/ppermute | solution.py:181
  31.9 0.7 %add_convert_fusion = bf16[2,2,64,192]{3,2,1,0:T(8,128)(2,1)} fusion(f32[2,2,64,192]{3,2,1,0:T(8,128)S(1)} %fusion.16, bf16[2,2,64,192]{3,2,1,0:T(8,128)(2,1)S(1)} %collective-permute-done), kind=kLoop, calls=%fused_computation.14 | loop fusion | flops 147456 | bytes 393216 | tf_op jit(solution)/shard_map/convert_element_type | solution.py:187
  (7 shorter events, 0.1 us)
Async XLA Ops:
  0.0 0.9 %copy-start = (bf16[1,64,4,384]{3,2,1,0:T(4,128)(2,1)S(1)}, bf16[1,64,4,384]{3,2,1,0:T(4,128)(2,1)}, u32[]{:S(2)}) copy-start(bf16[1,64,4,384]{3,2,1,0:T(4,128)(2,1)} %param.5) | copy-start | bytes 589828
  18.2 1.1 %copy-start.1 = (bf16[384,768]{1,0:T(8,128)(2,1)S(1)}, bf16[384,768]{1,0:T(8,128)(2,1)}, u32[]{:S(2)}) copy-start(bf16[384,768]{1,0:T(8,128)(2,1)} %wkv_ref.1) | copy-start | bytes 1769476
  18.2 1.1 %copy-start.2 = (bf16[384,384]{1,0:T(8,128)(2,1)S(1)}, bf16[384,384]{1,0:T(8,128)(2,1)}, u32[]{:S(2)}) copy-start(bf16[384,384]{1,0:T(8,128)(2,1)} %wq_ref.1) | copy-start | bytes 884740
  19.3 4.3 %copy-start.3 = (bf16[3,3,3,384,192]{3,4,2,1,0:T(8,128)(2,1)S(1)}, bf16[3,3,3,384,192]{3,4,2,1,0:T(8,128)(2,1)}, u32[]{:S(2)}) copy-start(bf16[3,3,3,384,192]{3,4,2,1,0:T(8,128)(2,1)} %param.9) | copy-start | bytes 11943940
  23.0 0.7 %copy-start.4 = (pred[8,9]{0,1:T(8,128)(4,1)S(1)}, pred[8,9]{0,1:T(8,128)(4,1)}, u32[]{:S(2)}) copy-start(pred[8,9]{0,1:T(8,128)(4,1)} %constant.79) | copy-start | bytes 220
  25.2 6.7 %collective-permute-start = (bf16[2,2,64,192]{3,2,1,0:T(8,128)(2,1)S(1)}, bf16[2,2,64,192]{3,2,1,0:T(8,128)(2,1)S(1)}, u32[]{:S(2)}, u32[]{:S(2)}) collective-permute-start(bf16[2,2,64,192]{3,2,1,0:T(8,128)(2,1)S(1)} %bitcast.34), channel_id=1, source_target_pairs={{0,2},{1,3},{4,6},{5,7},{8,10},{9,11},{12,14},{13,15},{16,18},{17,... | collective-permute-start | bytes 294920 | tf_op jit(solution)/shard_map/ppermute | solution.py:181

commit v16 on v14

--- a/solution.py
+++ b/solution.py
@@ -161,7 +161,9 @@
         first, whole.reshape(FD, rows * W, C), (RD + 2) * W, w_query, w_keyval
     )
     activated = activated.reshape(FD, RD + 2, W, C)
-    to_next = timed_conv(activated, conv_weight[:2], (0, 1)).astype(jnp.bfloat16)
+    both_taps = timed_conv(activated, conv_weight[:2], (0, 0))
+    last_tap = timed_conv(activated[1:], conv_weight[:1], (0, 0))
+    to_next = jnp.concatenate([both_taps, last_tap]).astype(jnp.bfloat16)
     pairs = [(i, i + 1) for i in range(span_count - 1)]
     from_prev = lax.ppermute(to_next, "span", pairs)
     own_sum = timed_conv(activated, conv_weight[1:], (1, 0))

time: 31.9 us -> 34.1 us (1.069)
  matrix products: 2.85 us -> 4.67 us
    conv_general_dilated x2 -> x3, matrix products: 2.48 us -> 4.29 us  [timed_conv(): lax.conv_general_dilated(frames[None], kernel, (1, 1, 1), (time_pad, (0,...]
  transfers between devices with their start and end apart: 1 -> 1, of which waited for: 1 -> 1; matrix products, arithmetic and copies ran while one was open for 5% -> 4% of each run, Pallas kernels for 0% -> 0%
where the time goes in v16:
time: 34.1 us; the launch traced here: 33.9 us
  blocking collectives  17.2 us (50%)
  matrix products  4.67 us (14%)
  starting transfers between devices  3.41 us (10%)
  Pallas kernels  2.74 us (8%)
  local copies, waits for them, and re-layouts  2.34 us (7%)
  waiting for transfers between devices  1.69 us (5%)
  other arithmetic  1.56 us (5%)
    all_gather x1, blocking collectives, local(): lax.all_gather(own_share, ('patch', 'chan'), axis=1, tiled=True)[0]  17.2 us
    conv_general_dilated x3, matrix products, timed_conv(): lax.conv_general_dilated(frames[None], kernel, (1, 1, 1), (time_pad, (0,...  4.29 us
    ppermute x1, starting transfers between devices, local(): from_prev = lax.ppermute(to_next, 'span', pairs)  3.41 us
    pallas_call x1, Pallas kernels, attend_frames(): pl.pallas_call(attention_kernel, grid_spec=grid_spec, compiler_params=plt...  2.74 us
    ppermute x1, waiting for transfers between devices, local(): from_prev = lax.ppermute(to_next, 'span', pairs)  1.69 us
    add x1, other arithmetic, local(): spot // per_frame * (tile_total // FD) + owner * per_frame  0.74 us
    convert_element_type x1, other arithmetic, local(): return (base + from_prev.astype(jnp.float32)).astype(jnp.bfloat16)  0.68 us
  transfers between devices with their start and end apart: 1, of which 1 were waited for; matrix products, arithmetic and copies ran while one was open for 4% of the time, Pallas kernels for 0%

profile of v16, /device:TPU:0, one launch (start us, length us, event | category | flops | bytes accessed | tf_op | source)
XLA Modules:
  0.0 33.9 jit_solution(14345320569743760037)
XLA Ops:
  0.0 0.7 %fusion.36 = s32[1,256]{1,0:T(1,128)S(1)} fusion(s32[1,256]{1,0:T(1,128)} %param.6), kind=kLoop, calls=%fused_computation.42 | loop fusion | flops 10752 | bytes 2048 | tf_op jit(solution)/shard_map/add | solution.py:152
  0.7 0.2 copy-done
  1.0 17.2 %all_gather.3 = bf16[1,256,4,384]{3,2,0,1:T(4,128)(2,1)S(1)} all-gather(bf16[1,32,4,384]{3,2,0,1:T(4,128)(2,1)S(1)} %constant_dynamic-slice_fusion), channel_id=1, replica_groups=mesh['clips'=2,'patch'=4,'span'=2,'chan'=2] {'patch','chan'}, dimensions={1}, use_global_device_ids=true | all-gather | bytes 884736 | tf_op jit(solution)/shard_map/all_gather | solution.py:145
  18.2 0.1 copy.45
  18.3 0.4 %convolution_convert_fusion = bf16[256,1536]{1,0:T(8,128)(2,1)S(1)} fusion(bf16[256,1536]{1,0:T(8,128)(2,1)S(1)} %bitcast.35, s32[256]{0:T(256)S(1)} %bitcast.42), kind=kOutput, calls=%fused_computation.4 | convolution fusion | flops 201785344 | bytes 1573888 | tf_op jit(solution)/shard_map/dot_general | solution.py:155
  18.7 0.5 %reshape_reshape.3.cells_ref = bf16[2,512,384]{2,1,0:T(8,128)(2,1)S(1)} reshape(bf16[256,1536]{1,0:T(8,128)(2,1)S(1)} %convolution_convert_fusion) | data formatting | bytes 1572864 | tf_op jit(solution)/shard_map/reshape;reshape | solution.py:161
  19.2 0.2 copy-done.1
  19.4 0.1 copy-done.2
  19.5 2.7 %shard_map.55 = (bf16[2,128,384]{2,1,0:T(8,128)(2,1)S(1)}, bf16[2,256,384]{2,1,0:T(8,128)(2,1)S(1)}) custom-call(s32[1]{0:T(128)} %bitcast.first_ref, bf16[2,512,384]{2,1,0:T(8,128)(2,1)S(1)} %reshape_reshape.3.cells_ref, bf16[384,384]{1,0:T(8,128)(2,1)S(1)} %copy-done.2, bf16[384,768]{1,0:T(8,128)(2,1)S(1)} %copy-done.1), custom_call_target="tpu_custom_call" | custom-call | tf_op jit(solution)/shard_map/pallas_call | solution.py:113
  22.2 0.2 copy.37
  22.4 0.1 pad.4
  22.6 2.1 %fusion.18 = bf16[1,2,8,9,192]{4,2,3,1,0:T(8,128)(2,1)S(1)} fusion(bf16[3,3,3,384,192]{3,4,2,1,0:T(8,128)(2,1)} %param.9, bf16[1,4,1,7,2,384]{5,3,4,1,2,0:T(8,128)(2,1)S(1)} %slice.26, bf16[1,4,1,8,9,384]{5,3,4,1,2,0:T(8,128)(2,1)S(1)} %copy.39, pred[8,9]{0,1:T(8,128)(4,1)S(1)} %copy-done.4), kind=kOutput, calls=%fused_computation.11 | convolution fusion | flops 191969280 | bytes 1646664 | tf_op jit(solution)/shard_map/conv_general_dilated | solution.py:125
  24.6 0.1 copy.40
  24.8 0.3 copy.30
  25.1 0.2 pad
  25.3 0.1 copy.32
  25.4 1.0 %fusion.15 = bf16[1,2,8,9,192]{4,2,3,1,0:T(8,128)(2,1)S(1)} fusion(bf16[3,3,3,384,192]{3,4,2,1,0:T(8,128)(2,1)S(1)} %copy-done.3, bf16[2,4,1,7,2,384]{5,3,4,1,0,2:T(8,128)(2,1)S(1)} %slice.23, bf16[2,4,1,8,9,384]{5,3,4,1,0,2:T(8,128)(2,1)S(1)} %copy.32, pred[8,9]{0,1:T(8,128)(4,1)S(1)} %copy-done.4), kind=kOutput, calls=%fused_computation.10 | convolution fusion | flops 383883264 | bytes 3252224 | tf_op jit(solution)/shard_map/conv_general_dilated | solution.py:125
  26.4 0.1 copy.35
  26.6 3.4 %collective-permute-start = (bf16[2,2,64,192]{3,2,1,0:T(8,128)(2,1)S(1)}, bf16[2,2,64,192]{3,2,1,0:T(8,128)(2,1)S(1)}, u32[]{:S(2)}, u32[]{:S(2)}) collective-permute-start(bf16[2,2,64,192]{3,2,1,0:T(8,128)(2,1)S(1)} %pad_maximum_fusion), channel_id=1, source_target_pairs={{0,2},{1,3},{4,6},{5,7},{8,10},{9,11},{12,14},{13,15},{16,18},{17,... | collective-permute-start | bytes 294920 | tf_op jit(solution)/shard_map/ppermute | solution.py:168
  30.0 1.2 %fusion.6 = f32[2,2,8,9,192]{4,2,3,1,0:T(8,128)S(1)} fusion(bf16[3,3,3,384,192]{3,4,2,1,0:T(8,128)(2,1)S(1)} %copy-done.3, bf16[2,4,1,7,2,384]{5,3,4,1,0,2:T(8,128)(2,1)S(1)} %slice.23, bf16[2,4,1,8,9,384]{5,3,4,1,0,2:T(8,128)(2,1)S(1)} %copy.32, pred[8,9]{0,1:T(8,128)(4,1)S(1)} %copy-done.4), kind=kOutput, calls=%fused_computation.7 | convolution fusion | flops 574986240 | bytes 3418112 | tf_op jit(solution)/shard_map/conv_general_dilated | solution.py:125
  31.2 0.2 copy.33
  31.4 0.1 fusion.31
  31.5 1.7 %collective-permute-done = bf16[2,2,64,192]{3,2,1,0:T(8,128)(2,1)S(1)} collective-permute-done((bf16[2,2,64,192]{3,2,1,0:T(8,128)(2,1)S(1)}, bf16[2,2,64,192]{3,2,1,0:T(8,128)(2,1)S(1)}, u32[]{:S(2)}, u32[]{:S(2)}) %collective-permute-start) | collective-permute-done | bytes 98336 | tf_op jit(solution)/shard_map/ppermute | solution.py:168
  33.2 0.7 %add_convert_fusion = bf16[2,2,64,192]{3,2,1,0:T(8,128)(2,1)} fusion(f32[2,2,64,192]{3,2,1,0:T(8,128)S(1)} %fusion.31, bf16[2,2,64,192]{3,2,1,0:T(8,128)(2,1)S(1)} %collective-permute-done), kind=kLoop, calls=%fused_computation.25 | loop fusion | flops 147456 | bytes 393216 | tf_op jit(solution)/shard_map/convert_element_type | solution.py:174
  (17 shorter events, 0.3 us)
Async XLA Ops:
  0.0 0.9 %copy-start = (bf16[1,64,4,384]{3,2,1,0:T(4,128)(2,1)S(1)}, bf16[1,64,4,384]{3,2,1,0:T(4,128)(2,1)}, u32[]{:S(2)}) copy-start(bf16[1,64,4,384]{3,2,1,0:T(4,128)(2,1)} %param.5) | copy-start | bytes 589828
  18.3 1.1 %copy-start.1 = (bf16[384,768]{1,0:T(8,128)(2,1)S(1)}, bf16[384,768]{1,0:T(8,128)(2,1)}, u32[]{:S(2)}) copy-start(bf16[384,768]{1,0:T(8,128)(2,1)} %wkv_ref.1) | copy-start | bytes 1769476
  18.3 1.1 %copy-start.2 = (bf16[384,384]{1,0:T(8,128)(2,1)S(1)}, bf16[384,384]{1,0:T(8,128)(2,1)}, u32[]{:S(2)}) copy-start(bf16[384,384]{1,0:T(8,128)(2,1)} %wq_ref.1) | copy-start | bytes 884740
  19.5 3.1 %copy-start.4 = (pred[8,9]{0,1:T(8,128)(4,1)S(1)}, pred[8,9]{0,1:T(8,128)(4,1)}, u32[]{:S(2)}) copy-start(pred[8,9]{0,1:T(8,128)(4,1)} %constant.83) | copy-start | bytes 220
  22.6 2.8 %copy-start.3 = (bf16[3,3,3,384,192]{3,4,2,1,0:T(8,128)(2,1)S(1)}, bf16[3,3,3,384,192]{3,4,2,1,0:T(8,128)(2,1)}, u32[]{:S(2)}) copy-start(bf16[3,3,3,384,192]{3,4,2,1,0:T(8,128)(2,1)} %param.9) | copy-start | bytes 11943940
  26.6 6.7 %collective-permute-start = (bf16[2,2,64,192]{3,2,1,0:T(8,128)(2,1)S(1)}, bf16[2,2,64,192]{3,2,1,0:T(8,128)(2,1)S(1)}, u32[]{:S(2)}, u32[]{:S(2)}) collective-permute-start(bf16[2,2,64,192]{3,2,1,0:T(8,128)(2,1)S(1)} %pad_maximum_fusion), channel_id=1, source_target_pairs={{0,2},{1,3},{4,6},{5,7},{8,10},{9,11},{12,14},{13,15},{16,18},{17,... | collective-permute-start | bytes 294920 | tf_op jit(solution)/shard_map/ppermute | solution.py:168

commit v17 on v14

--- a/solution.py
+++ b/solution.py
@@ -88,7 +88,14 @@
     normed = scaled_rms(mixed)
     row_of = lax.broadcasted_iota(jnp.int32, (rows, width), 0) // line + first
     inside = (row_of >= 0) & (row_of < frame_rows)
-    act_ref[frame] = jnp.where(inside, normed / (1.0 + jnp.exp(-normed)), 0.0).astype(jnp.bfloat16)
+    activated = jnp.where(inside, normed / (1.0 + jnp.exp(-normed)), 0.0).astype(jnp.bfloat16)
+    band = rows // line
+    target = lax.broadcasted_iota(jnp.int32, (rows, rows), 0)
+    source = lax.broadcasted_iota(jnp.int32, (rows, rows), 1)
+    swap = (source == (target % band) * line + target // band).astype(jnp.bfloat16)
+    act_ref[frame] = jnp.dot(swap, activated, preferred_element_type=jnp.float32).astype(
+        jnp.bfloat16
+    )
 
 
 def attend_frames(first, cells, ext_rows, w_query, w_keyval):
@@ -160,7 +167,7 @@
     mixed_own, activated = attend_frames(
         first, whole.reshape(FD, rows * W, C), (RD + 2) * W, w_query, w_keyval
     )
-    activated = activated.reshape(FD, RD + 2, W, C)
+    activated = activated.reshape(FD, W, RD + 2, C).transpose(0, 2, 1, 3)
     to_next = timed_conv(activated, conv_weight[:2], (0, 1)).astype(jnp.bfloat16)
     pairs = [(i, i + 1) for i in range(span_count - 1)]
     from_prev = lax.ppermute(to_next, "span", pairs)

time: 31.9 us -> 34.3 us (1.075)
  matrix products: 2.85 us -> 4.73 us
  Pallas kernels: 2.74 us -> 3.19 us
    conv_general_dilated x2, matrix products: 2.48 us -> 4.35 us  [timed_conv(): lax.conv_general_dilated(frames[None], kernel, (1, 1, 1), (time_pad, (0,...]
    another operation x2 -> x0, local copies, waits for them, and re-layouts: 0.47 us -> none  [timed_conv(): frames[None]]
    pallas_call x1, Pallas kernels: 2.74 us -> 3.19 us  [attend_frames(): pl.pallas_call(attention_kernel, grid_spec=grid_spec, compiler_params=plt...]
  transfers between devices with their start and end apart: 1 -> 1, of which waited for: 1 -> 1; matrix products, arithmetic and copies ran while one was open for 5% -> 4% of each run, Pallas kernels for 0% -> 0%
where the time goes in v17:
time: 34.3 us; the launch traced here: 34.1 us
  blocking collectives  17.2 us (50%)
  matrix products  4.73 us (14%)
  starting transfers between devices  3.41 us (10%)
  Pallas kernels  3.19 us (9%)
  local copies, waits for them, and re-layouts  2.12 us (6%)
  waiting for transfers between devices  1.68 us (5%)
  other arithmetic  1.53 us (4%)
    all_gather x1, blocking collectives, local(): lax.all_gather(own_share, ('patch', 'chan'), axis=1, tiled=True)[0]  17.2 us
    conv_general_dilated x2, matrix products, timed_conv(): lax.conv_general_dilated(frames[None], kernel, (1, 1, 1), (time_pad, (0,...  4.35 us
    ppermute x1, starting transfers between devices, local(): from_prev = lax.ppermute(to_next, 'span', pairs)  3.41 us
    pallas_call x1, Pallas kernels, attend_frames(): pl.pallas_call(attention_kernel, grid_spec=grid_spec, compiler_params=plt...  3.19 us
    ppermute x1, waiting for transfers between devices, local(): from_prev = lax.ppermute(to_next, 'span', pairs)  1.68 us
    unnamed x12, local copies, waits for them, and re-layouts  0.9 us
    add x1, other arithmetic, local(): spot // per_frame * (tile_total // FD) + owner * per_frame  0.74 us
  transfers between devices with their start and end apart: 1, of which 1 were waited for; matrix products, arithmetic and copies ran while one was open for 4% of the time, Pallas kernels for 0%

profile of v17, /device:TPU:0, one launch (start us, length us, event | category | flops | bytes accessed | tf_op | source)
XLA Modules:
  0.0 34.1 jit_solution(4219033556744547944)
XLA Ops:
  0.0 0.7 %fusion.20 = s32[1,256]{1,0:T(1,128)S(1)} fusion(s32[1,256]{1,0:T(1,128)} %param.6), kind=kLoop, calls=%fused_computation.28 | loop fusion | flops 10752 | bytes 2048 | tf_op jit(solution)/shard_map/add | solution.py:159
  0.7 0.2 copy-done
  1.0 17.2 %all_gather.3 = bf16[1,256,4,384]{3,2,0,1:T(4,128)(2,1)S(1)} all-gather(bf16[1,32,4,384]{3,2,0,1:T(4,128)(2,1)S(1)} %constant_dynamic-slice_fusion), channel_id=1, replica_groups=mesh['clips'=2,'patch'=4,'span'=2,'chan'=2] {'patch','chan'}, dimensions={1}, use_global_device_ids=true | all-gather | bytes 884736 | tf_op jit(solution)/shard_map/all_gather | solution.py:152
  18.2 0.1 copy.28
  18.3 0.0 copy-start.1
  18.3 0.4 %convolution_convert_fusion = bf16[256,1536]{1,0:T(8,128)(2,1)S(1)} fusion(bf16[256,1536]{1,0:T(8,128)(2,1)S(1)} %bitcast.29, s32[256]{0:T(256)S(1)} %bitcast.35), kind=kOutput, calls=%fused_computation.4 | convolution fusion | flops 201785344 | bytes 1573888 | tf_op jit(solution)/shard_map/dot_general | solution.py:162
  18.7 0.5 %reshape_reshape.3.cells_ref = bf16[2,512,384]{2,1,0:T(8,128)(2,1)S(1)} reshape(bf16[256,1536]{1,0:T(8,128)(2,1)S(1)} %convolution_convert_fusion) | data formatting | bytes 1572864 | tf_op jit(solution)/shard_map/reshape;reshape | solution.py:168
  19.2 0.2 copy-done.1
  19.4 0.1 copy-done.2
  19.5 3.2 %shard_map.55 = (bf16[2,128,384]{2,1,0:T(8,128)(2,1)S(1)}, bf16[2,256,384]{2,1,0:T(8,128)(2,1)S(1)}) custom-call(s32[1]{0:T(128)} %bitcast.first_ref, bf16[2,512,384]{2,1,0:T(8,128)(2,1)S(1)} %reshape_reshape.3.cells_ref, bf16[384,384]{1,0:T(8,128)(2,1)S(1)} %copy-done.2, bf16[384,768]{1,0:T(8,128)(2,1)S(1)} %copy-done.1), custom_call_target="tpu_custom_call" | custom-call | tf_op jit(solution)/shard_map/pallas_call | solution.py:120
  22.7 0.0 copy-start.4
  22.7 0.1 reshape.12
  22.8 0.2 pad
  22.9 0.1 copy.21
  23.0 0.3 copy-done.4
  23.4 3.1 %fusion.10 = bf16[2,2,8,9,192]{4,2,3,1,0:T(8,128)(2,1)S(1)} fusion(bf16[3,3,3,384,192]{3,4,2,1,0:T(8,128)(2,1)} %param.9, bf16[2,4,1,7,2,384]{5,3,4,1,0,2:T(8,128)(2,1)S(1)} %slice.12, bf16[2,4,1,8,9,384]{5,3,4,1,0,2:T(8,128)(2,1)S(1)} %copy.21, pred[8,9]{0,1:T(8,128)(4,1)S(1)} %copy-done.4), kind=kOutput, calls=%fused_computation.7 | convolution fusion | flops 575041536 | bytes 3293256 | tf_op jit(solution)/shard_map/conv_general_dilated | solution.py:132
  26.5 0.1 copy.24
  26.6 0.1 slice.14
  26.7 3.4 %collective-permute-start = (bf16[2,2,64,192]{3,2,1,0:T(8,128)(2,1)S(1)}, bf16[2,2,64,192]{3,2,1,0:T(8,128)(2,1)S(1)}, u32[]{:S(2)}, u32[]{:S(2)}) collective-permute-start(bf16[2,2,64,192]{3,2,1,0:T(8,128)(2,1)S(1)} %bitcast.34), channel_id=1, source_target_pairs={{0,2},{1,3},{4,6},{5,7},{8,10},{9,11},{12,14},{13,15},{16,18},{17,... | collective-permute-start | bytes 294920 | tf_op jit(solution)/shard_map/ppermute | solution.py:173
  30.2 1.2 %fusion.4 = f32[2,2,8,9,192]{4,2,3,1,0:T(8,128)S(1)} fusion(bf16[3,3,3,384,192]{3,4,2,1,0:T(8,128)(2,1)S(1)} %copy-done.3, bf16[2,4,1,7,2,384]{5,3,4,1,0,2:T(8,128)(2,1)S(1)} %slice.12, bf16[2,4,1,8,9,384]{5,3,4,1,0,2:T(8,128)(2,1)S(1)} %copy.21, pred[8,9]{0,1:T(8,128)(4,1)S(1)} %copy-done.4), kind=kOutput, calls=%fused_computation.5 | convolution fusion | flops 574986240 | bytes 3418112 | tf_op jit(solution)/shard_map/conv_general_dilated | solution.py:132
  31.4 0.2 copy.22
  31.6 0.1 fusion.16
  31.7 1.7 %collective-permute-done = bf16[2,2,64,192]{3,2,1,0:T(8,128)(2,1)S(1)} collective-permute-done((bf16[2,2,64,192]{3,2,1,0:T(8,128)(2,1)S(1)}, bf16[2,2,64,192]{3,2,1,0:T(8,128)(2,1)S(1)}, u32[]{:S(2)}, u32[]{:S(2)}) %collective-permute-start) | collective-permute-done | bytes 98336 | tf_op jit(solution)/shard_map/ppermute | solution.py:173
  33.4 0.7 %add_convert_fusion = bf16[2,2,64,192]{3,2,1,0:T(8,128)(2,1)} fusion(f32[2,2,64,192]{3,2,1,0:T(8,128)S(1)} %fusion.16, bf16[2,2,64,192]{3,2,1,0:T(8,128)(2,1)S(1)} %collective-permute-done), kind=kLoop, calls=%fused_computation.14 | loop fusion | flops 147456 | bytes 393216 | tf_op jit(solution)/shard_map/convert_element_type | solution.py:179
  (8 shorter events, 0.1 us)
Async XLA Ops:
  0.0 0.9 %copy-start = (bf16[1,64,4,384]{3,2,1,0:T(4,128)(2,1)S(1)}, bf16[1,64,4,384]{3,2,1,0:T(4,128)(2,1)}, u32[]{:S(2)}) copy-start(bf16[1,64,4,384]{3,2,1,0:T(4,128)(2,1)} %param.5) | copy-start | bytes 589828
  18.3 1.1 %copy-start.1 = (bf16[384,768]{1,0:T(8,128)(2,1)S(1)}, bf16[384,768]{1,0:T(8,128)(2,1)}, u32[]{:S(2)}) copy-start(bf16[384,768]{1,0:T(8,128)(2,1)} %wkv_ref.1) | copy-start | bytes 1769476
  18.3 1.1 %copy-start.2 = (bf16[384,384]{1,0:T(8,128)(2,1)S(1)}, bf16[384,384]{1,0:T(8,128)(2,1)}, u32[]{:S(2)}) copy-start(bf16[384,384]{1,0:T(8,128)(2,1)} %wq_ref.1) | copy-start | bytes 884740
  22.7 0.7 %copy-start.4 = (pred[8,9]{0,1:T(8,128)(4,1)S(1)}, pred[8,9]{0,1:T(8,128)(4,1)}, u32[]{:S(2)}) copy-start(pred[8,9]{0,1:T(8,128)(4,1)} %constant.79) | copy-start | bytes 220
  23.3 6.8 %copy-start.3 = (bf16[3,3,3,384,192]{3,4,2,1,0:T(8,128)(2,1)S(1)}, bf16[3,3,3,384,192]{3,4,2,1,0:T(8,128)(2,1)}, u32[]{:S(2)}) copy-start(bf16[3,3,3,384,192]{3,4,2,1,0:T(8,128)(2,1)} %param.9) | copy-start | bytes 11943940
  26.7 6.7 %collective-permute-start = (bf16[2,2,64,192]{3,2,1,0:T(8,128)(2,1)S(1)}, bf16[2,2,64,192]{3,2,1,0:T(8,128)(2,1)S(1)}, u32[]{:S(2)}, u32[]{:S(2)}) collective-permute-start(bf16[2,2,64,192]{3,2,1,0:T(8,128)(2,1)S(1)} %bitcast.34), channel_id=1, source_target_pairs={{0,2},{1,3},{4,6},{5,7},{8,10},{9,11},{12,14},{13,15},{16,18},{17,... | collective-permute-start | bytes 294920 | tf_op jit(solution)/shard_map/ppermute | solution.py:173

commit v18 on v14

--- a/solution.py
+++ b/solution.py
@@ -23,11 +23,18 @@
 
 
 def attention_kernel(first_ref, cells_ref, wq_ref, wkv_ref, mixed_ref, act_ref):
-    for frame in range(cells_ref.shape[0]):
-        attend_frame(first_ref, cells_ref, wq_ref, wkv_ref, mixed_ref, act_ref, frame)
-
-
-def attend_frame(first_ref, cells_ref, wq_ref, wkv_ref, mixed_ref, act_ref, frame):
+    frames, count, width = cells_ref.shape
+    shared = None
+    if count <= KEY_BLOCK:
+        every = cells_ref[...].reshape(frames * count, width)
+        shared = jnp.dot(
+            scaled_rms(every).astype(jnp.bfloat16), wkv_ref[...], preferred_element_type=jnp.float32
+        ).astype(jnp.bfloat16)
+    for frame in range(frames):
+        attend_frame(first_ref, cells_ref, wq_ref, wkv_ref, mixed_ref, act_ref, frame, shared)
+
+
+def attend_frame(first_ref, cells_ref, wq_ref, wkv_ref, mixed_ref, act_ref, frame, shared):
     width = wq_ref.shape[0]
     scale = 1.0 / math.sqrt(width)
     count = cells_ref.shape[1]
@@ -52,10 +59,15 @@
 
     def fold(step, carry):
         run_max, run_total, run_acc = carry
-        cells = cells_ref[frame, pl.ds(step * block, block), :]
-        keyvals = jnp.dot(
-            scaled_rms(cells).astype(jnp.bfloat16), wkv_ref[...], preferred_element_type=jnp.float32
-        ).astype(jnp.bfloat16)
+        if shared is None:
+            cells = cells_ref[frame, pl.ds(step * block, block), :]
+            keyvals = jnp.dot(
+                scaled_rms(cells).astype(jnp.bfloat16),
+                wkv_ref[...],
+                preferred_element_type=jnp.float32,
+            ).astype(jnp.bfloat16)
+        else:
+            keyvals = shared[frame * count : (frame + 1) * count]
         scores = (
             lax.dot_general(
                 queries,

time: 31.9 us -> 31.9 us (level)
  no operation moved by 1% of the time
where the time goes in v18:
time: 31.9 us; the launch traced here: 31.7 us
  blocking collectives  17.2 us (54%)
  starting transfers between devices  3.4 us (11%)
  matrix products  2.85 us (9%)
  Pallas kernels  2.76 us (9%)
  local copies, waits for them, and re-layouts  2.11 us (7%)
  waiting for transfers between devices  1.68 us (5%)
  other arithmetic  1.53 us (5%)
    all_gather x1, blocking collectives, local(): lax.all_gather(own_share, ('patch', 'chan'), axis=1, tiled=True)[0]  17.2 us
    ppermute x1, starting transfers between devices, local(): from_prev = lax.ppermute(to_next, 'span', pairs)  3.4 us
    pallas_call x1, Pallas kernels, attend_frames(): pl.pallas_call(attention_kernel, grid_spec=grid_spec, compiler_params=plt...  2.76 us
    conv_general_dilated x2, matrix products, timed_conv(): lax.conv_general_dilated(frames[None], kernel, (1, 1, 1), (time_pad, (0,...  2.48 us
    ppermute x1, waiting for transfers between devices, local(): from_prev = lax.ppermute(to_next, 'span', pairs)  1.68 us
    add x1, other arithmetic, local(): spot // per_frame * (tile_total // FD) + owner * per_frame  0.74 us
    convert_element_type x1, other arithmetic, local(): return (base + from_prev.astype(jnp.float32)).astype(jnp.bfloat16)  0.68 us
    unnamed x12, local copies, waits for them, and re-layouts  0.68 us
  transfers between devices with their start and end apart: 1, of which 1 were waited for; matrix products, arithmetic and copies ran while one was open for 5% of the time, Pallas kernels for 0%

profile of v18, /device:TPU:0, one launch (start us, length us, event | category | flops | bytes accessed | tf_op | source)
XLA Modules:
  0.0 31.7 jit_solution(6043150358245390444)
XLA Ops:
  0.0 0.7 %fusion.20 = s32[1,256]{1,0:T(1,128)S(1)} fusion(s32[1,256]{1,0:T(1,128)} %param.6), kind=kLoop, calls=%fused_computation.28 | loop fusion | flops 10752 | bytes 2048 | tf_op jit(solution)/shard_map/add | solution.py:164
  0.7 0.2 copy-done
  1.0 17.2 %all_gather.3 = bf16[1,256,4,384]{3,2,0,1:T(4,128)(2,1)S(1)} all-gather(bf16[1,32,4,384]{3,2,0,1:T(4,128)(2,1)S(1)} %constant_dynamic-slice_fusion), channel_id=1, replica_groups=mesh['clips'=2,'patch'=4,'span'=2,'chan'=2] {'patch','chan'}, dimensions={1}, use_global_device_ids=true | all-gather | bytes 884736 | tf_op jit(solution)/shard_map/all_gather | solution.py:157
  18.2 0.1 copy.31
  18.3 0.0 copy-start.1
  18.3 0.4 %convolution_convert_fusion = bf16[256,1536]{1,0:T(8,128)(2,1)S(1)} fusion(bf16[256,1536]{1,0:T(8,128)(2,1)S(1)} %bitcast.28, s32[256]{0:T(256)S(1)} %bitcast.33), kind=kOutput, calls=%fused_computation.4 | convolution fusion | flops 201785344 | bytes 1573888 | tf_op jit(solution)/shard_map/dot_general | solution.py:167
  18.7 0.5 %reshape_reshape.3.cells_ref = bf16[2,512,384]{2,1,0:T(8,128)(2,1)S(1)} reshape(bf16[256,1536]{1,0:T(8,128)(2,1)S(1)} %convolution_convert_fusion) | data formatting | bytes 1572864 | tf_op jit(solution)/shard_map/reshape;reshape | solution.py:173
  19.2 0.2 copy-done.1
  19.4 0.1 copy-done.2
  19.5 2.8 %shard_map.55 = (bf16[2,128,384]{2,1,0:T(8,128)(2,1)S(1)}, bf16[2,256,384]{2,1,0:T(8,128)(2,1)S(1)}) custom-call(s32[1]{0:T(128)} %bitcast.first_ref, bf16[2,512,384]{2,1,0:T(8,128)(2,1)S(1)} %reshape_reshape.3.cells_ref, bf16[384,384]{1,0:T(8,128)(2,1)S(1)} %copy-done.2, bf16[384,768]{1,0:T(8,128)(2,1)S(1)} %copy-done.1), custom_call_target="tpu_custom_call" | custom-call | tf_op jit(solution)/shard_map/pallas_call | solution.py:125
  22.2 0.0 copy-start.4
  22.2 0.3 copy.22
  22.6 0.2 pad
  22.7 0.1 copy.24
  22.8 0.1 copy-done.4
  22.9 1.2 %fusion.10 = bf16[2,2,8,9,192]{4,2,3,1,0:T(8,128)(2,1)S(1)} fusion(bf16[3,3,3,384,192]{3,4,2,1,0:T(8,128)(2,1)S(1)} %copy-done.3, bf16[2,4,1,7,2,384]{5,3,4,1,0,2:T(8,128)(2,1)S(1)} %slice.12, bf16[2,4,1,8,9,384]{5,3,4,1,0,2:T(8,128)(2,1)S(1)} %copy.24, pred[8,9]{0,1:T(8,128)(4,1)S(1)} %copy-done.4), kind=kOutput, calls=%fused_computation.7 | convolution fusion | flops 575041536 | bytes 3307520 | tf_op jit(solution)/shard_map/conv_general_dilated | solution.py:137
  24.2 0.1 copy.27
  24.3 0.1 slice.14
  24.4 3.4 %collective-permute-start = (bf16[2,2,64,192]{3,2,1,0:T(8,128)(2,1)S(1)}, bf16[2,2,64,192]{3,2,1,0:T(8,128)(2,1)S(1)}, u32[]{:S(2)}, u32[]{:S(2)}) collective-permute-start(bf16[2,2,64,192]{3,2,1,0:T(8,128)(2,1)S(1)} %bitcast.32), channel_id=1, source_target_pairs={{0,2},{1,3},{4,6},{5,7},{8,10},{9,11},{12,14},{13,15},{16,18},{17,... | collective-permute-start | bytes 294920 | tf_op jit(solution)/shard_map/ppermute | solution.py:178
  27.8 1.2 %fusion.4 = f32[2,2,8,9,192]{4,2,3,1,0:T(8,128)S(1)} fusion(bf16[3,3,3,384,192]{3,4,2,1,0:T(8,128)(2,1)S(1)} %copy-done.3, bf16[2,4,1,7,2,384]{5,3,4,1,0,2:T(8,128)(2,1)S(1)} %slice.12, bf16[2,4,1,8,9,384]{5,3,4,1,0,2:T(8,128)(2,1)S(1)} %copy.24, pred[8,9]{0,1:T(8,128)(4,1)S(1)} %copy-done.4), kind=kOutput, calls=%fused_computation.5 | convolution fusion | flops 574986240 | bytes 3418112 | tf_op jit(solution)/shard_map/conv_general_dilated | solution.py:137
  29.1 0.2 copy.25
  29.3 0.1 fusion.16
  29.4 1.7 %collective-permute-done = bf16[2,2,64,192]{3,2,1,0:T(8,128)(2,1)S(1)} collective-permute-done((bf16[2,2,64,192]{3,2,1,0:T(8,128)(2,1)S(1)}, bf16[2,2,64,192]{3,2,1,0:T(8,128)(2,1)S(1)}, u32[]{:S(2)}, u32[]{:S(2)}) %collective-permute-start) | collective-permute-done | bytes 98336 | tf_op jit(solution)/shard_map/ppermute | solution.py:178
  31.1 0.7 %add_convert_fusion = bf16[2,2,64,192]{3,2,1,0:T(8,128)(2,1)} fusion(f32[2,2,64,192]{3,2,1,0:T(8,128)S(1)} %fusion.16, bf16[2,2,64,192]{3,2,1,0:T(8,128)(2,1)S(1)} %collective-permute-done), kind=kLoop, calls=%fused_computation.14 | loop fusion | flops 147456 | bytes 393216 | tf_op jit(solution)/shard_map/convert_element_type | solution.py:184
  (8 shorter events, 0.1 us)
Async XLA Ops:
  0.0 0.9 %copy-start = (bf16[1,64,4,384]{3,2,1,0:T(4,128)(2,1)S(1)}, bf16[1,64,4,384]{3,2,1,0:T(4,128)(2,1)}, u32[]{:S(2)}) copy-start(bf16[1,64,4,384]{3,2,1,0:T(4,128)(2,1)} %param.5) | copy-start | bytes 589828
  18.3 1.1 %copy-start.1 = (bf16[384,768]{1,0:T(8,128)(2,1)S(1)}, bf16[384,768]{1,0:T(8,128)(2,1)}, u32[]{:S(2)}) copy-start(bf16[384,768]{1,0:T(8,128)(2,1)} %wkv_ref.1) | copy-start | bytes 1769476
  18.3 1.1 %copy-start.2 = (bf16[384,384]{1,0:T(8,128)(2,1)S(1)}, bf16[384,384]{1,0:T(8,128)(2,1)}, u32[]{:S(2)}) copy-start(bf16[384,384]{1,0:T(8,128)(2,1)} %wq_ref.1) | copy-start | bytes 884740
  19.5 3.4 %copy-start.3 = (bf16[3,3,3,384,192]{3,4,2,1,0:T(8,128)(2,1)S(1)}, bf16[3,3,3,384,192]{3,4,2,1,0:T(8,128)(2,1)}, u32[]{:S(2)}) copy-start(bf16[3,3,3,384,192]{3,4,2,1,0:T(8,128)(2,1)} %param.9) | copy-start | bytes 11943940
  22.2 0.7 %copy-start.4 = (pred[8,9]{0,1:T(8,128)(4,1)S(1)}, pred[8,9]{0,1:T(8,128)(4,1)}, u32[]{:S(2)}) copy-start(pred[8,9]{0,1:T(8,128)(4,1)} %constant.79) | copy-start | bytes 220
  24.4 6.6 %collective-permute-start = (bf16[2,2,64,192]{3,2,1,0:T(8,128)(2,1)S(1)}, bf16[2,2,64,192]{3,2,1,0:T(8,128)(2,1)S(1)}, u32[]{:S(2)}, u32[]{:S(2)}) collective-permute-start(bf16[2,2,64,192]{3,2,1,0:T(8,128)(2,1)S(1)} %bitcast.32), channel_id=1, source_target_pairs={{0,2},{1,3},{4,6},{5,7},{8,10},{9,11},{12,14},{13,15},{16,18},{17,... | collective-permute-start | bytes 294920 | tf_op jit(solution)/shard_map/ppermute | solution.py:178

commit v19 on v18

--- a/solution.py
+++ b/solution.py
@@ -30,13 +30,21 @@
         shared = jnp.dot(
             scaled_rms(every).astype(jnp.bfloat16), wkv_ref[...], preferred_element_type=jnp.float32
         ).astype(jnp.bfloat16)
+    picked = [query_rows(first_ref, cells_ref, mixed_ref, act_ref, f) for f in range(frames)]
+    rows = picked[0].shape[0]
+    asked = jnp.dot(
+        scaled_rms(jnp.concatenate(picked, axis=0)).astype(jnp.bfloat16),
+        wq_ref[...],
+        preferred_element_type=jnp.float32,
+    ).astype(jnp.bfloat16)
     for frame in range(frames):
-        attend_frame(first_ref, cells_ref, wq_ref, wkv_ref, mixed_ref, act_ref, frame, shared)
-
-
-def attend_frame(first_ref, cells_ref, wq_ref, wkv_ref, mixed_ref, act_ref, frame, shared):
-    width = wq_ref.shape[0]
-    scale = 1.0 / math.sqrt(width)
+        queries = asked[frame * rows : (frame + 1) * rows]
+        attend_frame(
+            first_ref, cells_ref, wkv_ref, mixed_ref, act_ref, frame, shared, picked[frame], queries
+        )
+
+
+def query_rows(first_ref, cells_ref, mixed_ref, act_ref, frame):
     count = cells_ref.shape[1]
     own = mixed_ref.shape[1]
     line = (act_ref.shape[1] - own) // 2
@@ -44,7 +52,7 @@
     first = first_ref[0]
     top = jnp.maximum(first, 0) * line
     below = jnp.minimum(first + 1 + own // line, frame_rows - 1) * line
-    feats = jnp.concatenate(
+    return jnp.concatenate(
         [
             cells_ref[frame, pl.ds(top, line), :],
             cells_ref[frame, pl.ds((first + 1) * line, own), :],
@@ -52,9 +60,18 @@
         ],
         axis=0,
     ).astype(jnp.float32)
-    queries = jnp.dot(
-        scaled_rms(feats).astype(jnp.bfloat16), wq_ref[...], preferred_element_type=jnp.float32
-    ).astype(jnp.bfloat16)
+
+
+def attend_frame(
+    first_ref, cells_ref, wkv_ref, mixed_ref, act_ref, frame, shared, feats, queries
+):
+    width = cells_ref.shape[2]
+    scale = 1.0 / math.sqrt(width)
+    count = cells_ref.shape[1]
+    own = mixed_ref.shape[1]
+    line = (act_ref.shape[1] - own) // 2
+    frame_rows = count // line
+    first = first_ref[0]
     block = min(count, KEY_BLOCK)
 
     def fold(step, carry):

time: 31.9 us -> 31.8 us (level)
  no operation moved by 1% of the time
where the time goes in v19:
time: 31.8 us; the launch traced here: 31.6 us
  blocking collectives  17.2 us (54%)
  starting transfers between devices  3.4 us (11%)
  matrix products  2.85 us (9%)
  Pallas kernels  2.64 us (8%)
  local copies, waits for them, and re-layouts  2.11 us (7%)
  waiting for transfers between devices  1.7 us (5%)
  other arithmetic  1.53 us (5%)
    all_gather x1, blocking collectives, local(): lax.all_gather(own_share, ('patch', 'chan'), axis=1, tiled=True)[0]  17.2 us
    ppermute x1, starting transfers between devices, local(): from_prev = lax.ppermute(to_next, 'span', pairs)  3.4 us
    pallas_call x1, Pallas kernels, attend_frames(): pl.pallas_call(attention_kernel, grid_spec=grid_spec, compiler_params=plt...  2.64 us
    conv_general_dilated x2, matrix products, timed_conv(): lax.conv_general_dilated(frames[None], kernel, (1, 1, 1), (time_pad, (0,...  2.48 us
    ppermute x1, waiting for transfers between devices, local(): from_prev = lax.ppermute(to_next, 'span', pairs)  1.7 us
    add x1, other arithmetic, local(): spot // per_frame * (tile_total // FD) + owner * per_frame  0.74 us
    convert_element_type x1, other arithmetic, local(): return (base + from_prev.astype(jnp.float32)).astype(jnp.bfloat16)  0.68 us
    unnamed x12, local copies, waits for them, and re-layouts  0.68 us
  transfers between devices with their start and end apart: 1, of which 1 were waited for; matrix products, arithmetic and copies ran while one was open for 5% of the time, Pallas kernels for 0%

profile of v19, /device:TPU:0, one launch (start us, length us, event | category | flops | bytes accessed | tf_op | source)
XLA Modules:
  0.0 31.6 jit_solution(612148811598133706)
XLA Ops:
  0.0 0.7 %fusion.20 = s32[1,256]{1,0:T(1,128)S(1)} fusion(s32[1,256]{1,0:T(1,128)} %param.6), kind=kLoop, calls=%fused_computation.28 | loop fusion | flops 10752 | bytes 2048 | tf_op jit(solution)/shard_map/add | solution.py:181
  0.7 0.2 copy-done
  1.0 17.2 %all_gather.3 = bf16[1,256,4,384]{3,2,0,1:T(4,128)(2,1)S(1)} all-gather(bf16[1,32,4,384]{3,2,0,1:T(4,128)(2,1)S(1)} %constant_dynamic-slice_fusion), channel_id=1, replica_groups=mesh['clips'=2,'patch'=4,'span'=2,'chan'=2] {'patch','chan'}, dimensions={1}, use_global_device_ids=true | all-gather | bytes 884736 | tf_op jit(solution)/shard_map/all_gather | solution.py:174
  18.2 0.1 copy.31
  18.3 0.0 copy-start.1
  18.3 0.4 %convolution_convert_fusion = bf16[256,1536]{1,0:T(8,128)(2,1)S(1)} fusion(bf16[256,1536]{1,0:T(8,128)(2,1)S(1)} %bitcast.28, s32[256]{0:T(256)S(1)} %bitcast.33), kind=kOutput, calls=%fused_computation.4 | convolution fusion | flops 201785344 | bytes 1573888 | tf_op jit(solution)/shard_map/dot_general | solution.py:184
  18.7 0.5 %reshape_reshape.3.cells_ref = bf16[2,512,384]{2,1,0:T(8,128)(2,1)S(1)} reshape(bf16[256,1536]{1,0:T(8,128)(2,1)S(1)} %convolution_convert_fusion) | data formatting | bytes 1572864 | tf_op jit(solution)/shard_map/reshape;reshape | solution.py:190
  19.2 0.2 copy-done.1
  19.4 0.1 copy-done.2
  19.5 2.6 %shard_map.55 = (bf16[2,128,384]{2,1,0:T(8,128)(2,1)S(1)}, bf16[2,256,384]{2,1,0:T(8,128)(2,1)S(1)}) custom-call(s32[1]{0:T(128)} %bitcast.first_ref, bf16[2,512,384]{2,1,0:T(8,128)(2,1)S(1)} %reshape_reshape.3.cells_ref, bf16[384,384]{1,0:T(8,128)(2,1)S(1)} %copy-done.2, bf16[384,768]{1,0:T(8,128)(2,1)S(1)} %copy-done.1), custom_call_target="tpu_custom_call" | custom-call | tf_op jit(solution)/shard_map/pallas_call | solution.py:142
  22.1 0.0 copy-start.4
  22.1 0.3 copy.22
  22.4 0.2 pad
  22.6 0.1 copy.24
  22.7 0.1 copy-done.4
  22.8 1.2 %fusion.10 = bf16[2,2,8,9,192]{4,2,3,1,0:T(8,128)(2,1)S(1)} fusion(bf16[3,3,3,384,192]{3,4,2,1,0:T(8,128)(2,1)S(1)} %copy-done.3, bf16[2,4,1,7,2,384]{5,3,4,1,0,2:T(8,128)(2,1)S(1)} %slice.12, bf16[2,4,1,8,9,384]{5,3,4,1,0,2:T(8,128)(2,1)S(1)} %copy.24, pred[8,9]{0,1:T(8,128)(4,1)S(1)} %copy-done.4), kind=kOutput, calls=%fused_computation.7 | convolution fusion | flops 575041536 | bytes 3307520 | tf_op jit(solution)/shard_map/conv_general_dilated | solution.py:154
  24.1 0.1 copy.27
  24.2 0.1 slice.14
  24.3 3.4 %collective-permute-start = (bf16[2,2,64,192]{3,2,1,0:T(8,128)(2,1)S(1)}, bf16[2,2,64,192]{3,2,1,0:T(8,128)(2,1)S(1)}, u32[]{:S(2)}, u32[]{:S(2)}) collective-permute-start(bf16[2,2,64,192]{3,2,1,0:T(8,128)(2,1)S(1)} %bitcast.32), channel_id=1, source_target_pairs={{0,2},{1,3},{4,6},{5,7},{8,10},{9,11},{12,14},{13,15},{16,18},{17,... | collective-permute-start | bytes 294920 | tf_op jit(solution)/shard_map/ppermute | solution.py:195
  27.7 1.2 %fusion.4 = f32[2,2,8,9,192]{4,2,3,1,0:T(8,128)S(1)} fusion(bf16[3,3,3,384,192]{3,4,2,1,0:T(8,128)(2,1)S(1)} %copy-done.3, bf16[2,4,1,7,2,384]{5,3,4,1,0,2:T(8,128)(2,1)S(1)} %slice.12, bf16[2,4,1,8,9,384]{5,3,4,1,0,2:T(8,128)(2,1)S(1)} %copy.24, pred[8,9]{0,1:T(8,128)(4,1)S(1)} %copy-done.4), kind=kOutput, calls=%fused_computation.5 | convolution fusion | flops 574986240 | bytes 3418112 | tf_op jit(solution)/shard_map/conv_general_dilated | solution.py:154
  28.9 0.2 copy.25
  29.1 0.1 fusion.16
  29.3 1.7 %collective-permute-done = bf16[2,2,64,192]{3,2,1,0:T(8,128)(2,1)S(1)} collective-permute-done((bf16[2,2,64,192]{3,2,1,0:T(8,128)(2,1)S(1)}, bf16[2,2,64,192]{3,2,1,0:T(8,128)(2,1)S(1)}, u32[]{:S(2)}, u32[]{:S(2)}) %collective-permute-start) | collective-permute-done | bytes 98336 | tf_op jit(solution)/shard_map/ppermute | solution.py:195
  31.0 0.7 %add_convert_fusion = bf16[2,2,64,192]{3,2,1,0:T(8,128)(2,1)} fusion(f32[2,2,64,192]{3,2,1,0:T(8,128)S(1)} %fusion.16, bf16[2,2,64,192]{3,2,1,0:T(8,128)(2,1)S(1)} %collective-permute-done), kind=kLoop, calls=%fused_computation.14 | loop fusion | flops 147456 | bytes 393216 | tf_op jit(solution)/shard_map/convert_element_type | solution.py:201
  (8 shorter events, 0.1 us)
Async XLA Ops:
  0.0 0.9 %copy-start = (bf16[1,64,4,384]{3,2,1,0:T(4,128)(2,1)S(1)}, bf16[1,64,4,384]{3,2,1,0:T(4,128)(2,1)}, u32[]{:S(2)}) copy-start(bf16[1,64,4,384]{3,2,1,0:T(4,128)(2,1)} %param.5) | copy-start | bytes 589828
  18.3 1.1 %copy-start.1 = (bf16[384,768]{1,0:T(8,128)(2,1)S(1)}, bf16[384,768]{1,0:T(8,128)(2,1)}, u32[]{:S(2)}) copy-start(bf16[384,768]{1,0:T(8,128)(2,1)} %wkv_ref.1) | copy-start | bytes 1769476
  18.3 1.1 %copy-start.2 = (bf16[384,384]{1,0:T(8,128)(2,1)S(1)}, bf16[384,384]{1,0:T(8,128)(2,1)}, u32[]{:S(2)}) copy-start(bf16[384,384]{1,0:T(8,128)(2,1)} %wq_ref.1) | copy-start | bytes 884740
  19.5 3.2 %copy-start.3 = (bf16[3,3,3,384,192]{3,4,2,1,0:T(8,128)(2,1)S(1)}, bf16[3,3,3,384,192]{3,4,2,1,0:T(8,128)(2,1)}, u32[]{:S(2)}) copy-start(bf16[3,3,3,384,192]{3,4,2,1,0:T(8,128)(2,1)} %param.9) | copy-start | bytes 11943940
  22.1 0.7 %copy-start.4 = (pred[8,9]{0,1:T(8,128)(4,1)S(1)}, pred[8,9]{0,1:T(8,128)(4,1)}, u32[]{:S(2)}) copy-start(pred[8,9]{0,1:T(8,128)(4,1)} %constant.79) | copy-start | bytes 220
  24.3 6.6 %collective-permute-start = (bf16[2,2,64,192]{3,2,1,0:T(8,128)(2,1)S(1)}, bf16[2,2,64,192]{3,2,1,0:T(8,128)(2,1)S(1)}, u32[]{:S(2)}, u32[]{:S(2)}) collective-permute-start(bf16[2,2,64,192]{3,2,1,0:T(8,128)(2,1)S(1)} %bitcast.32), channel_id=1, source_target_pairs={{0,2},{1,3},{4,6},{5,7},{8,10},{9,11},{12,14},{13,15},{16,18},{17,... | collective-permute-start | bytes 294920 | tf_op jit(solution)/shard_map/ppermute | solution.py:195
